TPU v7x, 512 devices: a whole 4x8x8 slice. The times are simulated.
512 devices in a mesh: seq: 256 (over z, x, y), head: 2 (over core).
Axes of the slice: x: 4, y: 8, z: 8, core: 2. Of those that a mesh axis runs over, the one named last changes fastest.
Arguments:
- query_rows: bfloat16 [131072, 8, 128], P('seq', 'head'), may hold values from -8 to 8
- key_rows: bfloat16 [131072, 8, 128], P('seq', 'head'), may hold values from -8 to 8
- value_rows: bfloat16 [131072, 8, 128], P('seq', 'head'), may hold values from -8 to 8
- out_weight: bfloat16 [8, 128, 2048], P('head'), may hold values from -0.1875 to 0.1875
Outputs:
- layer_out: bfloat16 [131072, 2048], P('seq', 'head')
All inputs are finite; a program needn't handle non-finite values.
Results may differ from a plain program's by a relative error of at most 0.015.
Values may be sent and summed in bfloat16 or wider, within the bound.
No kernel may reach another device: no remote copies, remote signals or barrier semaphores. Data moves between devices by JAX's collectives and lax.ppermute only.
A program may use at most 64 MiB of HBM per device.

v0:
```python
import jax
import jax.numpy as jnp
from jax import lax
from jax.sharding import PartitionSpec as P

BLOCK = 128


def partner_2(value, axis, distance):
    mask = 2**distance
    pairs = [(source, source ^ mask) for source in range(lax.axis_size(axis))]
    return lax.ppermute(value, axis, pairs)


def with_halo(value, sides, width):
    for axis, dim in sides:
        size, length = (lax.axis_size(axis), value.shape[dim])
        up = [(i, (i + 1) % size) for i in range(size - 1)]
        down = [(j, i) for i, j in up]
        last = lax.slice_in_dim(value, length - width, length, axis=dim)
        initial = lax.slice_in_dim(value, 0, width, axis=dim)
        before = lax.ppermute(last, axis, up)
        after = lax.ppermute(initial, axis, down)
        value = jnp.concatenate([before, value, after], axis=dim)
    return value


def shifted(value, axis, steps):
    count = lax.axis_size(axis)
    initial, last = (max(0, -steps), min(count, count - steps))
    return lax.ppermute(value, axis, [(source, source + steps) for source in range(initial, last)])


def joined_along(parts, dim):
    parts = jnp.moveaxis(parts, 0, dim)
    shape = parts.shape
    return parts.reshape(*shape[:dim], shape[dim] * shape[dim + 1], *shape[dim + 2 :])


def gather_packed(arrays, axis, dims):
    ravelled = jnp.concatenate([a.reshape(-1) for a in arrays])
    lines, at, done = (lax.all_gather(ravelled, axis), 0, [])
    for a, dim in zip(arrays, dims):
        parts = lines[:, at : at + a.size].reshape(-1, *a.shape)
        done.append(joined_along(parts, dim))
        at += a.size
    return tuple(done)


def cut_along(value, dim, length):
    shape = value.shape
    parts = value.reshape(*shape[:dim], length, shape[dim] // length, *shape[dim + 1 :])
    return jnp.moveaxis(parts, dim, 0)


def summed_on_arrival(value, axis, dim):
    length = lax.axis_size(axis)
    parts = lax.all_to_all(cut_along(value, dim, length), axis, 0, 0, tiled=True)
    return jnp.sum(parts.astype(jnp.float32), axis=0)


def coarsen(source, level_index, average):
    count = source.shape[0] >> level_index
    grouped = source.astype(jnp.float32).reshape((count, 1 << level_index) + source.shape[1:])
    summed = jnp.sum(grouped, axis=1)
    if average:
        summed = summed / float(1 << level_index)
    return summed.astype(jnp.bfloat16)


def slot_targets(block_index, level_index):
    if level_index == 0:
        return [block_index - 1, block_index, block_index + 1]
    return [
        block_index - 2,
        block_index + 2,
        jnp.where(block_index % 2 == 0, block_index + 3, block_index - 3),
    ]


def slot_masks(block_index, block_total, level_index, width):
    targets = slot_targets(block_index, level_index)
    return jnp.concatenate(
        [
            jnp.repeat(((target >= 0) & (target < block_total))[:, None], width, axis=1)
            for target in targets
        ],
        axis=1,
    )


def level_attend(query_blocks, key_blocks, value_blocks, valid, level_index, scale):
    scores = (
        jnp.einsum("nqhd,nkhd->nhqk", query_blocks, key_blocks, preferred_element_type=jnp.float32)
        * scale
    )
    scores = jnp.where(valid[:, None, None, :], scores, -jnp.inf)
    row_peak = jnp.max(scores, axis=3, keepdims=True)
    weights = jnp.exp(scores - row_peak)
    denominator = float(1 << level_index) * jnp.sum(weights, axis=3)
    numerator = jnp.einsum(
        "nhqk,nkhd->nqhd",
        weights.astype(jnp.bfloat16),
        value_blocks,
        preferred_element_type=jnp.float32,
    )
    block_count = query_blocks.shape[0]
    row_count = query_blocks.shape[1]
    peak_rows = jnp.transpose(row_peak[..., 0], (0, 2, 1)).reshape(block_count * row_count, -1)
    denominator_rows = jnp.transpose(denominator, (0, 2, 1)).reshape(block_count * row_count, -1)
    numerator_rows = numerator.reshape(
        block_count * row_count, numerator.shape[2], numerator.shape[3]
    )
    return (peak_rows, numerator_rows, denominator_rows)


def upper_half(device_index, bit):
    return device_index // (1 << bit) % 2 == 1


def assemble_joint(pieces, level_list, device_index):
    current = {}
    for level_index in level_list:
        current[level_index] = pieces[level_index]
    deepest = max([level_index - 2 for level_index in level_list] + [0])
    for bit in range(deepest):
        members = [level_index for level_index in level_list if level_index - 2 > bit]
        widths = [current[level_index].shape[1] for level_index in members]
        joined = jnp.concatenate([current[level_index] for level_index in members], axis=1)
        partner = partner_2(joined, "seq", bit)
        upper = upper_half(device_index, bit)
        offset = 0
        for level_index, width in zip(members, widths):
            theirs = partner[:, offset : offset + width]
            offset = offset + width
            mine = current[level_index]
            current[level_index] = jnp.where(
                upper,
                jnp.concatenate([theirs, mine], axis=1),
                jnp.concatenate([mine, theirs], axis=1),
            )
    return current


def per_device(query_rows, key_rows, value_rows, out_weight):
    seq_count = lax.axis_size("seq")
    device_index = lax.axis_index("seq")
    token_count, head_local, head_size = query_rows.shape
    scale = float(head_size) ** (-0.5)
    top_level = seq_count.bit_length() - 1
    results = []
    local_blocks = token_count // BLOCK
    padded = with_halo(jnp.stack([key_rows, value_rows]), (("seq", 1),), BLOCK)
    padded = padded.reshape(2, local_blocks + 2, BLOCK, head_local, head_size)
    near_keys = jnp.concatenate(
        [
            padded[:, 0:local_blocks],
            padded[:, 1 : local_blocks + 1],
            padded[:, 2 : local_blocks + 2],
        ],
        axis=2,
    )
    fine_index = device_index * local_blocks + jnp.arange(local_blocks, dtype=jnp.int32)
    valid = slot_masks(fine_index, local_blocks * seq_count, 0, BLOCK)
    results.append(
        (
            0,
            level_attend(
                query_rows.reshape(local_blocks, BLOCK, head_local, head_size),
                near_keys[0],
                near_keys[1],
                valid,
                0,
                scale,
            ),
        )
    )
    half_blocks = local_blocks // 2
    first_queries = coarsen(query_rows, 1, True)
    first_pair = jnp.stack([coarsen(key_rows, 1, True), coarsen(value_rows, 1, False)])
    padded = with_halo(first_pair, (("seq", 1),), first_pair.shape[1])
    padded = padded.reshape(2, 3 * half_blocks, BLOCK, head_local, head_size)
    third_slot = jnp.stack([padded[:, 5], padded[:, 0]], axis=1)
    far_keys = jnp.concatenate([padded[:, 0:2], padded[:, 4:6], third_slot], axis=2)
    first_index = device_index * half_blocks + jnp.arange(half_blocks, dtype=jnp.int32)
    valid = slot_masks(first_index, half_blocks * seq_count, 1, BLOCK)
    results.append(
        (
            1,
            level_attend(
                first_queries.reshape(half_blocks, BLOCK, head_local, head_size),
                far_keys[0],
                far_keys[1],
                valid,
                1,
                scale,
            ),
        )
    )
    queries_at = {}
    pieces = {}
    for level_index in range(2, top_level + 1):
        queries_at[level_index] = coarsen(query_rows, level_index, True)
        pieces[level_index] = jnp.stack(
            [coarsen(key_rows, level_index, True), coarsen(value_rows, level_index, False)]
        )
    shift_levels = list(range(2, top_level - 1))
    assembled = assemble_joint(pieces, shift_levels, device_index)
    for level_index in shift_levels:
        group = 1 << level_index - 2
        whole_block = assembled[level_index]
        before_two = shifted(whole_block, "seq", 2 * group)
        after_two = shifted(whole_block, "seq", -2 * group)
        block_index = device_index // group
        outgoing = jnp.where(block_index % 2 == 0, before_two, after_two)
        third_block = partner_2(outgoing, "seq", level_index - 2)
        level_keys = jnp.concatenate([before_two, after_two, third_block], axis=1)[:, None]
        valid = slot_masks(jnp.reshape(block_index, (1,)), seq_count // group, level_index, BLOCK)
        results.append(
            (
                level_index,
                level_attend(
                    queries_at[level_index][None],
                    level_keys[0],
                    level_keys[1],
                    valid,
                    level_index,
                    scale,
                ),
            )
        )
    coarse_list = [top_level - 1, top_level]
    wholes = gather_packed((pieces[top_level - 1], pieces[top_level]), "seq", (1, 1))
    for position, level_index in enumerate(coarse_list):
        group = 1 << level_index - 2
        block_total = seq_count // group
        whole_level = wholes[position].reshape(2, block_total, BLOCK, head_local, head_size)
        block_index = device_index // group
        targets = slot_targets(block_index, level_index)
        chosen = [
            lax.dynamic_index_in_dim(
                whole_level, jnp.clip(target, 0, block_total - 1), axis=1, keepdims=False
            )
            for target in targets
        ]
        level_keys = jnp.concatenate(chosen, axis=1)[:, None]
        valid = slot_masks(jnp.reshape(block_index, (1,)), block_total, level_index, BLOCK)
        results.append(
            (
                level_index,
                level_attend(
                    queries_at[level_index][None],
                    level_keys[0],
                    level_keys[1],
                    valid,
                    level_index,
                    scale,
                ),
            )
        )
    expanded = []
    for level_index, terms in results:
        factor = 1 << level_index
        expanded.append(
            (
                jnp.repeat(terms[0], factor, axis=0),
                jnp.repeat(terms[1], factor, axis=0),
                jnp.repeat(terms[2], factor, axis=0),
            )
        )
    overall = expanded[0][0]
    for entry in expanded[1:]:
        overall = jnp.maximum(overall, entry[0])
    weighted = jnp.zeros((token_count, head_local, head_size), jnp.float32)
    total_weight = jnp.zeros((token_count, head_local), jnp.float32)
    for part_peak, numerator, denominator in expanded:
        level_factor = jnp.exp(part_peak - overall)
        weighted = weighted + level_factor[:, :, None] * numerator
        total_weight = total_weight + level_factor * denominator
    attended = (weighted / total_weight[:, :, None]).astype(jnp.bfloat16)
    flattened = attended.reshape(token_count, head_local * head_size)
    weight_flat = out_weight.reshape(head_local * head_size, out_weight.shape[2])
    partial_value = jnp.dot(flattened, weight_flat, preferred_element_type=jnp.float32)
    return summed_on_arrival(partial_value.astype(jnp.bfloat16), "head", 1).astype(jnp.bfloat16)


def solution(mesh):
    return jax.shard_map(
        per_device,
        mesh=mesh,
        in_specs=(
            P("seq", "head", None),
            P("seq", "head", None),
            P("seq", "head", None),
            P("head", None, None),
        ),
        out_specs=P("seq", "head"),
        check_vma=False,
    )
```

profile of v0, /device:TPU:193, one launch (start us, length us, event | category | flops | bytes accessed | tf_op | source)
XLA Modules:
  0.0 287.9 jit_solution(8112443279428638584)
XLA Ops:
  6.5 1.6 bitcast_reduce_fusion.19
  8.2 1.4 bitcast_reduce_fusion.20
  10.4 7.2 %collective-permute-start.5 = (bf16[2,128,4,128]{3,1,2,0:T(8,128)(2,1)}, bf16[2,128,4,128]{3,1,2,0:T(8,128)(2,1)}, u32[]{:S(2)}, u32[]{:S(2)}) collective-permute-start(bf16[2,128,4,128]{3,1,2,0:T(8,128)(2,1)} %pad_maximum_fusion.8), channel_id=1, source_target_pairs={{4,0},{6,2},{8,4},{10,6},{12,8},{14,10},{16,12},{18,14},{20,16},{2... | collective-permute-start | bytes 786440 | tf_op jit(solution)/shard_map/ppermute | solution.py:31
  17.5 1.9 collective-permute-start.4
  23.9 2.3 collective-permute-start.7
  27.1 1.2 pad_maximum_fusion.5
  28.3 8.4 %collective-permute-start.3 = (bf16[2,256,4,128]{3,2,1,0:T(4,128)(2,1)}, bf16[2,256,4,128]{3,2,1,0:T(4,128)(2,1)}, u32[]{:S(2)}, u32[]{:S(2)}) collective-permute-start(bf16[2,256,4,128]{3,2,1,0:T(4,128)(2,1)} %pad_maximum_fusion.5), channel_id=1, source_target_pairs={{2,0},{4,2},{6,4},{8,6},{10,8},{12,10},{14,12},{16,14},{18,16},{20... | collective-permute-start | bytes 1572872 | tf_op jit(solution)/shard_map/ppermute | solution.py:23
  38.4 1.9 collective-permute-start
  48.1 1.0 bitcast_reduce_fusion.21
  49.1 1.1 bitcast_reduce_fusion.24
  50.8 1.3 multiply_convert_fusion.4
  52.1 1.3 multiply_convert_fusion.3
  61.0 1.2 multiply_convert_fusion.1
  62.2 7.6 %collective-permute-start.1 = (bf16[2,128,4,128]{3,1,2,0:T(8,128)(2,1)}, bf16[2,128,4,128]{3,1,2,0:T(8,128)(2,1)S(1)}, u32[]{:S(2)}, u32[]{:S(2)}) collective-permute-start(bf16[2,128,4,128]{3,1,2,0:T(8,128)(2,1)} %get-tuple-element.31), channel_id=1, source_target_pairs={{2,0},{4,2},{6,4},{8,6},{10,8},{12,10},{14,12},{16,14},{18,16},{20... | collective-permute-start | bytes 786440 | tf_op jit(solution)/shard_map/ppermute | solution.py:23
  74.9 1.9 collective-permute-start.2
  76.8 2.1 collective-permute-start.9
  79.0 1.1 pad_maximum_fusion.1
  82.4 1.6 fusion.12
  83.9 1.1 copy.394
  85.0 7.3 %collective-permute-start.8 = (bf16[2,128,4,128]{3,1,2,0:T(8,128)(2,1)S(1)}, bf16[2,128,4,128]{3,1,2,0:T(8,128)(2,1)S(1)}, u32[]{:S(2)}, u32[]{:S(2)}) collective-permute-start(bf16[2,128,4,128]{3,1,2,0:T(8,128)(2,1)S(1)} %maximum_select_fusion), channel_id=1, source_target_pairs={{0,8},{2,10},{4,12},{6,14},{8,16},{10,18},{12,20},{14,22},{16,24},... | collective-permute-start | bytes 786440 | tf_op jit(solution)/shard_map/ppermute | solution.py:31
  93.3 1.4 fusion.1
  94.7 1.9 collective-permute-start.11
  96.6 1.1 broadcast_select_fusion.4
  97.8 18.9 %collective-permute-done.11 = bf16[2,112,4,128]{3,1,2,0:T(8,128)(2,1)S(1)} collective-permute-done((bf16[2,112,4,128]{3,1,2,0:T(8,128)(2,1)S(1)}, bf16[2,112,4,128]{3,1,2,0:T(8,128)(2,1)S(1)}, u32[]{:S(2)}, u32[]{:S(2)}) %collective-permute-start.11) | collective-permute-done | bytes 229408 | tf_op jit(solution)/shard_map/ppermute | solution.py:12
  116.6 5.4 %collective-permute-start.6 = (bf16[2,128,4,128]{3,1,2,0:T(8,128)(2,1)S(1)}, bf16[2,128,4,128]{3,1,2,0:T(8,128)(2,1)S(1)}, u32[]{:S(2)}, u32[]{:S(2)}) collective-permute-start(bf16[2,128,4,128]{3,1,2,0:T(8,128)(2,1)S(1)} %get-tuple-element.40), channel_id=1, source_target_pairs={{0,2},{2,0},{4,6},{6,4},{8,10},{10,8},{12,14},{14,12},{16,18},{18,... | collective-permute-start | bytes 786440 | tf_op jit(solution)/shard_map/ppermute | solution.py:12
  123.6 1.9 collective-permute-start.13
  125.6 3.4 %collective-permute-start.12 = (bf16[2,128,4,128]{3,1,2,0:T(8,128)(2,1)}, bf16[2,128,4,128]{3,1,2,0:T(8,128)(2,1)}, u32[]{:S(2)}, u32[]{:S(2)}) collective-permute-start(bf16[2,128,4,128]{3,1,2,0:T(8,128)(2,1)} %maximum_select_fusion.1), channel_id=1, source_target_pairs={{0,16},{2,18},{4,20},{6,22},{8,24},{10,26},{12,28},{14,30},{16,32}... | collective-permute-start | bytes 786440 | tf_op jit(solution)/shard_map/ppermute | solution.py:31
  129.8 1.9 collective-permute-start.15
  131.7 5.0 %collective-permute-start.10 = (bf16[2,128,4,128]{3,1,2,0:T(8,128)(2,1)}, bf16[2,128,4,128]{3,1,2,0:T(8,128)(2,1)}, u32[]{:S(2)}, u32[]{:S(2)}) collective-permute-start(bf16[2,128,4,128]{3,1,2,0:T(8,128)(2,1)} %get-tuple-element.32), channel_id=1, source_target_pairs={{0,4},{2,6},{4,0},{6,2},{8,12},{10,14},{12,8},{14,10},{16,20},{18,... | collective-permute-start | bytes 786440 | tf_op jit(solution)/shard_map/ppermute | solution.py:12
  136.8 7.7 %pad_maximum_fusion.2 = bf16[2,768,4,128]{3,2,1,0:T(4,128)(2,1)S(1)} fusion(bf16[2,256,4,128]{3,2,1,0:T(4,128)(2,1)} %collective-permute-done.3, bf16[1,256,4,128]{3,2,1,0:T(4,128)(2,1)S(1)} %bitcast.529, bf16[1,256,4,128]{3,2,1,0:T(4,128)(2,1)S(1)} %copy-done.10, bf16[2,256,4,128]{3,2,1,0:T(4,128)(2,1)S(1)} %collective-permute-done.2), kind=kLoop, calls=%fused_computation.11 | loop fusion | flops 2359296 | bytes 3145728 | tf_op jit(solution)/shard_map/concatenate | solution.py:24
  151.0 1.0 broadcast_in_dim.457
  155.3 2.1 collective-permute-start.17
  157.4 4.6 %collective-permute-start.16 = (bf16[2,128,4,128]{3,1,2,0:T(8,128)(2,1)}, bf16[2,128,4,128]{3,1,2,0:T(8,128)(2,1)}, u32[]{:S(2)}, u32[]{:S(2)}) collective-permute-start(bf16[2,128,4,128]{3,1,2,0:T(8,128)(2,1)} %maximum_select_fusion.2), channel_id=1, source_target_pairs={{0,32},{2,34},{4,36},{6,38},{8,40},{10,42},{12,44},{14,46},{16,48}... | collective-permute-start | bytes 786440 | tf_op jit(solution)/shard_map/ppermute | solution.py:31
  163.6 7.5 %collective-permute-start.19 = (bf16[2,64,4,128]{3,1,2,0:T(8,128)(2,1)}, bf16[2,64,4,128]{3,1,2,0:T(8,128)(2,1)}, u32[]{:S(2)}, u32[]{:S(2)}) collective-permute-start(bf16[2,64,4,128]{3,1,2,0:T(8,128)(2,1)} %maximum_select_fusion.6), channel_id=1, source_target_pairs={{0,16},{2,18},{4,20},{6,22},{8,24},{10,26},{12,28},{14,30},{16,0},... | collective-permute-start | bytes 393224 | tf_op jit(solution)/shard_map/ppermute | solution.py:12
  172.1 1.9 broadcast_select_fusion.2
  173.9 7.4 %collective-permute-start.14 = (bf16[2,128,4,128]{3,1,2,0:T(8,128)(2,1)}, bf16[2,128,4,128]{3,1,2,0:T(8,128)(2,1)}, u32[]{:S(2)}, u32[]{:S(2)}) collective-permute-start(bf16[2,128,4,128]{3,1,2,0:T(8,128)(2,1)} %get-tuple-element.34), channel_id=1, source_target_pairs={{0,8},{2,10},{4,12},{6,14},{8,0},{10,2},{12,4},{14,6},{16,24},{18,... | collective-permute-start | bytes 786440 | tf_op jit(solution)/shard_map/ppermute | solution.py:12
  181.4 1.7 constant_dynamic-update-slice_fusion.3
  183.1 1.4 fusion.142
  184.6 1.3 convolution_bitcast_fusion.2
  187.6 2.0 maximum_select_fusion.3
  189.6 1.9 collective-permute-start.21
  191.5 4.6 %collective-permute-start.20 = (bf16[2,128,4,128]{3,1,2,0:T(8,128)(2,1)}, bf16[2,128,4,128]{3,1,2,0:T(8,128)(2,1)S(1)}, u32[]{:S(2)}, u32[]{:S(2)}) collective-permute-start(bf16[2,128,4,128]{3,1,2,0:T(8,128)(2,1)} %maximum_select_fusion.3), channel_id=1, source_target_pairs={{0,64},{2,66},{4,68},{6,70},{8,72},{10,74},{12,76},{14,78},{16,80}... | collective-permute-start | bytes 786440 | tf_op jit(solution)/shard_map/ppermute | solution.py:31
  197.0 1.9 broadcast_select_fusion.1
  198.9 2.1 collective-permute-start.18
  205.0 1.9 convolution_bitcast_fusion.3
  207.0 1.8 broadcast_select_fusion
  208.8 7.4 %collective-permute-start.22 = (bf16[2,128,4,128]{3,1,2,0:T(8,128)(2,1)}, bf16[2,128,4,128]{3,1,2,0:T(8,128)(2,1)S(1)}, u32[]{:S(2)}, u32[]{:S(2)}) collective-permute-start(bf16[2,128,4,128]{3,1,2,0:T(8,128)(2,1)} %get-tuple-element.38), channel_id=1, source_target_pairs={{0,32},{2,34},{4,36},{6,38},{8,40},{10,42},{12,44},{14,46},{16,48}... | collective-permute-start | bytes 786440 | tf_op jit(solution)/shard_map/ppermute | solution.py:12
  216.2 1.0 constant_dynamic-update-slice_fusion.9
  220.8 1.8 convolution_bitcast_fusion.4
  223.4 1.3 fusion.139
  226.4 1.8 convolution_bitcast_fusion.5
  228.2 5.6 %reshape.1304 = bf16[256,6144]{1,0:T(8,128)(2,1)} reshape(bf16[1572864]{0:T(1024)(128)(2,1)} %all-gather.3.cloned.1.call-done) | data formatting | bytes 6291456 | tf_op jit(solution)/shard_map/all_gather | solution.py:42
  233.9 2.3 slice.191
  236.2 3.2 %slice.189 = bf16[256,4096]{1,0:T(8,128)(2,1)} slice(bf16[256,6144]{1,0:T(8,128)(2,1)} %reshape.1304), slice={[0:256], [0:4096]} | slice | bytes 4194304 | tf_op jit(solution)/shard_map/slice | solution.py:44
  239.4 2.3 copy.388
  241.6 3.7 %copy.389 = bf16[2,256,2,4,128]{4,2,1,3,0:T(2,128)(2,1)} copy(bf16[2,256,2,4,128]{1,4,3,2,0:T(8,128)(2,1)} %bitcast.525) | data formatting | bytes 2097152 | tf_op jit(solution)/shard_map/transpose | solution.py:35
  245.3 1.2 dynamic-slice_bitcast_fusion.2
  248.6 4.1 %copy.383 = bf16[256,4096]{0,1:T(8,128)(2,1)} copy(bf16[256,4096]{1,0:T(8,128)(2,1)} %slice.189) | data formatting | bytes 4194304 | tf_op jit(solution)/shard_map/slice | solution.py:44
  252.7 4.2 %copy.384 = bf16[2,256,4,4,128]{4,2,1,3,0:T(4,128)(2,1)} copy(bf16[2,256,4,4,128]{1,4,3,2,0:T(8,128)(2,1)} %bitcast.519) | data formatting | bytes 4194304 | tf_op jit(solution)/shard_map/transpose | solution.py:35
  256.9 1.2 dynamic-slice_bitcast_fusion.5
  262.3 3.6 %fusion.24 = bf16[512,4,128]{2,0,1:T(8,128)(2,1)S(1)} fusion(f32[4,128,4,128]{3,1,0,2:T(8,128)S(1)} %copy-done.8, f32[512,4,128]{2,0,1:T(8,128)S(1)} %bitcast.523, f32[512,4,128]{2,0,1:T(8,128)S(1)} %bitcast.524, f32[512,4]{0,1:T(4,128)S(1)} %get-tuple-element.5, f32[2,4,128]{2,0,1:T(2,128)S(1)} %copy-done.37, f32[512,4]{0,1:T(4,128)S(1)} %get-tuple-element.12, ...), kind=kLoop, calls=%fused_computation.50 | loop fusion | flops 4980736 | bytes 4009984 | tf_op jit(solution)/shard_map/convert_element_type | solution.py:280
  265.9 1.3 bitcast_convert_fusion
  267.4 10.4 %all_to_all.5 = bf16[2,512,1024]{2,1,0:T(8,128)(2,1)} all-to-all(bf16[2,512,1024]{2,1,0:T(8,128)(2,1)S(1)} %bitcast.520), channel_id=1, replica_groups=mesh['seq'=256,'head'=2] {'head'}, dimensions={0} | all-to-all | bytes 4194304 | tf_op jit(solution)/shard_map/all_to_all | solution.py:58
  277.7 3.3 %reduce_sum.342 = bf16[512,1024]{1,0:T(8,128)(2,1)} reduce(bf16[2,512,1024]{2,1,0:T(8,128)(2,1)} %all_to_all.5, bf16[]{:T(256)} %constant.337.clone.1), dimensions={0}, to_apply=%region_42.43 | reduce | flops 524288 | bytes 3145730 | tf_op jit(solution)/shard_map/reduce_sum | solution.py:59
  (321 shorter events, 64.9 us)
Async XLA Ops:
  6.5 259.3 %copy-start = (bf16[4,128,2048]{2,1,0:T(8,128)(2,1)S(1)}, bf16[4,128,2048]{2,1,0:T(8,128)(2,1)}, u32[]{:S(2)}) copy-start(bf16[4,128,2048]{2,1,0:T(8,128)(2,1)} %param.7) | copy-start | bytes 6291460
  6.5 12.9 %copy-start.1 = (bf16[512,4,128]{2,1,0:T(4,128)(2,1)S(1)}, bf16[512,4,128]{2,1,0:T(4,128)(2,1)}, u32[]{:S(2)}) copy-start(bf16[512,4,128]{2,1,0:T(4,128)(2,1)} %param.6) | copy-start | bytes 1572868
  6.5 13.2 %copy-start.2 = (bf16[512,4,128]{2,1,0:T(4,128)(2,1)S(1)}, bf16[512,4,128]{2,1,0:T(4,128)(2,1)}, u32[]{:S(2)}) copy-start(bf16[512,4,128]{2,1,0:T(4,128)(2,1)} %param.5) | copy-start | bytes 1572868
  6.5 221.7 %all-gather.3.cloned.1.call-start = ((), (), s32[]{:S(2)}) async-start(), calls=%async_computation.1 | async-start | bytes 3158016 | tf_op jit(solution)/shard_map/all_gather | solution.py:42
  10.4 84.3 %collective-permute-start.5 = (bf16[2,128,4,128]{3,1,2,0:T(8,128)(2,1)}, bf16[2,128,4,128]{3,1,2,0:T(8,128)(2,1)}, u32[]{:S(2)}, u32[]{:S(2)}) collective-permute-start(bf16[2,128,4,128]{3,1,2,0:T(8,128)(2,1)} %pad_maximum_fusion.8), channel_id=1, source_target_pairs={{4,0},{6,2},{8,4},{10,6},{12,8},{14,10},{16,12},{18,14},{20,16},{2... | collective-permute-start | bytes 786440 | tf_op jit(solution)/shard_map/ppermute | solution.py:31
  17.5 67.5 %collective-permute-start.4 = (bf16[2,128,4,128]{3,1,2,0:T(8,128)(2,1)}, bf16[2,128,4,128]{3,1,2,0:T(8,128)(2,1)}, u32[]{:S(2)}, u32[]{:S(2)}) collective-permute-start(bf16[2,128,4,128]{3,1,2,0:T(8,128)(2,1)} %pad_maximum_fusion.8), channel_id=1, source_target_pairs={{0,4},{2,6},{4,8},{6,10},{8,12},{10,14},{12,16},{14,18},{16,20},{1... | collective-permute-start | bytes 786440 | tf_op jit(solution)/shard_map/ppermute | solution.py:31
  23.0 0.9 copy-start.32
  23.9 38.3 %collective-permute-start.7 = (bf16[2,120,4,128]{3,1,2,0:T(8,128)(2,1)}, bf16[2,120,4,128]{3,1,2,0:T(8,128)(2,1)}, u32[]{:S(2)}, u32[]{:S(2)}) collective-permute-start(bf16[2,120,4,128]{3,1,2,0:T(8,128)(2,1)} %maximum_maximum_fusion.1), channel_id=1, source_target_pairs={{0,2},{2,0},{4,6},{6,4},{8,10},{10,8},{12,14},{14,12},{16,18},{18,... | collective-permute-start | bytes 737288 | tf_op jit(solution)/shard_map/ppermute | solution.py:12
  27.1 1.2 copy-start.9
  28.3 101.5 %collective-permute-start.3 = (bf16[2,256,4,128]{3,2,1,0:T(4,128)(2,1)}, bf16[2,256,4,128]{3,2,1,0:T(4,128)(2,1)}, u32[]{:S(2)}, u32[]{:S(2)}) collective-permute-start(bf16[2,256,4,128]{3,2,1,0:T(4,128)(2,1)} %pad_maximum_fusion.5), channel_id=1, source_target_pairs={{2,0},{4,2},{6,4},{8,6},{10,8},{12,10},{14,12},{16,14},{18,16},{20... | collective-permute-start | bytes 1572872 | tf_op jit(solution)/shard_map/ppermute | solution.py:23
  36.8 1.6 copy-start.6
  36.8 6.2 %copy-start.3 = (bf16[512,4,128]{2,1,0:T(4,128)(2,1)S(1)}, bf16[512,4,128]{2,1,0:T(4,128)(2,1)}, u32[]{:S(2)}) copy-start(bf16[512,4,128]{2,1,0:T(4,128)(2,1)} %param.4) | copy-start | bytes 1572868
  38.4 36.5 %collective-permute-start = (bf16[2,128,4,128]{3,1,2,0:T(8,128)(2,1)}, bf16[2,128,4,128]{3,1,2,0:T(8,128)(2,1)}, u32[]{:S(2)}, u32[]{:S(2)}) collective-permute-start(bf16[2,128,4,128]{3,1,2,0:T(8,128)(2,1)} %get-tuple-element.30), channel_id=1, source_target_pairs={{0,2},{2,4},{4,6},{6,8},{8,10},{10,12},{12,14},{14,16},{16,18},{18... | collective-permute-start | bytes 786440 | tf_op jit(solution)/shard_map/ppermute | solution.py:22
  50.2 28.7 %copy-start.5 = (bf16[1,512,4,128]{3,1,2,0:T(8,128)(2,1)S(1)}, bf16[1,512,4,128]{3,1,2,0:T(8,128)(2,1)}, u32[]{:S(2)}) copy-start(bf16[1,512,4,128]{3,1,2,0:T(8,128)(2,1)} %copy-done.4) | copy-start | bytes 1572868
  50.2 23.6 %copy-start.31 = (bf16[1,8,4,128]{3,1,2,0:T(8,128)(2,1)S(1)}, bf16[1,8,4,128]{3,1,2,0:T(8,128)(2,1)}, u32[]{:S(2)}) copy-start(bf16[1,8,4,128]{3,1,2,0:T(8,128)(2,1)} %copy-done.30) | copy-start | bytes 24580
  50.2 23.6 %copy-start.33 = (bf16[8,4,128]{2,0,1:T(8,128)(2,1)S(1)}, bf16[8,4,128]{2,0,1:T(8,128)(2,1)}, u32[]{:S(2)}) copy-start(bf16[8,4,128]{2,0,1:T(8,128)(2,1)} %copy-done.32) | copy-start | bytes 24580
  50.2 28.7 %copy-start.7 = (bf16[1,512,4,128]{3,1,2,0:T(8,128)(2,1)S(1)}, bf16[1,512,4,128]{3,1,2,0:T(8,128)(2,1)}, u32[]{:S(2)}) copy-start(bf16[1,512,4,128]{3,1,2,0:T(8,128)(2,1)} %copy-done.6) | copy-start | bytes 1572868
  62.2 14.6 %collective-permute-start.1 = (bf16[2,128,4,128]{3,1,2,0:T(8,128)(2,1)}, bf16[2,128,4,128]{3,1,2,0:T(8,128)(2,1)S(1)}, u32[]{:S(2)}, u32[]{:S(2)}) collective-permute-start(bf16[2,128,4,128]{3,1,2,0:T(8,128)(2,1)} %get-tuple-element.31), channel_id=1, source_target_pairs={{2,0},{4,2},{6,4},{8,6},{10,8},{12,10},{14,12},{16,14},{18,16},{20... | collective-permute-start | bytes 786440 | tf_op jit(solution)/shard_map/ppermute | solution.py:23
  74.9 56.8 %collective-permute-start.2 = (bf16[2,256,4,128]{3,2,1,0:T(4,128)(2,1)}, bf16[2,256,4,128]{3,2,1,0:T(4,128)(2,1)S(1)}, u32[]{:S(2)}, u32[]{:S(2)}) collective-permute-start(bf16[2,256,4,128]{3,2,1,0:T(4,128)(2,1)} %pad_maximum_fusion.5), channel_id=1, source_target_pairs={{0,2},{2,4},{4,6},{6,8},{8,10},{10,12},{12,14},{14,16},{16,18},{18... | collective-permute-start | bytes 1572872 | tf_op jit(solution)/shard_map/ppermute | solution.py:22
  76.8 48.7 %collective-permute-start.9 = (bf16[2,128,4,128]{3,1,2,0:T(8,128)(2,1)S(1)}, bf16[2,128,4,128]{3,1,2,0:T(8,128)(2,1)S(1)}, u32[]{:S(2)}, u32[]{:S(2)}) collective-permute-start(bf16[2,128,4,128]{3,1,2,0:T(8,128)(2,1)S(1)} %maximum_select_fusion), channel_id=1, source_target_pairs={{8,0},{10,2},{12,4},{14,6},{16,8},{18,10},{20,12},{22,14},{24,16},... | collective-permute-start | bytes 786440 | tf_op jit(solution)/shard_map/ppermute | solution.py:31
  85.0 38.6 %collective-permute-start.8 = (bf16[2,128,4,128]{3,1,2,0:T(8,128)(2,1)S(1)}, bf16[2,128,4,128]{3,1,2,0:T(8,128)(2,1)S(1)}, u32[]{:S(2)}, u32[]{:S(2)}) collective-permute-start(bf16[2,128,4,128]{3,1,2,0:T(8,128)(2,1)S(1)} %maximum_select_fusion), channel_id=1, source_target_pairs={{0,8},{2,10},{4,12},{6,14},{8,16},{10,18},{12,20},{14,22},{16,24},... | collective-permute-start | bytes 786440 | tf_op jit(solution)/shard_map/ppermute | solution.py:31
  94.7 22.0 %collective-permute-start.11 = (bf16[2,112,4,128]{3,1,2,0:T(8,128)(2,1)S(1)}, bf16[2,112,4,128]{3,1,2,0:T(8,128)(2,1)S(1)}, u32[]{:S(2)}, u32[]{:S(2)}) collective-permute-start(bf16[2,112,4,128]{3,1,2,0:T(8,128)(2,1)S(1)} %pad_maximum_fusion.9), channel_id=1, source_target_pairs={{0,4},{2,6},{4,0},{6,2},{8,12},{10,14},{12,8},{14,10},{16,20},{18,... | collective-permute-start | bytes 688136 | tf_op jit(solution)/shard_map/ppermute | solution.py:12
  116.6 29.4 %collective-permute-start.6 = (bf16[2,128,4,128]{3,1,2,0:T(8,128)(2,1)S(1)}, bf16[2,128,4,128]{3,1,2,0:T(8,128)(2,1)S(1)}, u32[]{:S(2)}, u32[]{:S(2)}) collective-permute-start(bf16[2,128,4,128]{3,1,2,0:T(8,128)(2,1)S(1)} %get-tuple-element.40), channel_id=1, source_target_pairs={{0,2},{2,0},{4,6},{6,4},{8,10},{10,8},{12,14},{14,12},{16,18},{18,... | collective-permute-start | bytes 786440 | tf_op jit(solution)/shard_map/ppermute | solution.py:12
  122.0 14.7 %copy-start.10 = (bf16[1,256,4,128]{3,2,1,0:T(4,128)(2,1)S(1)}, bf16[1,256,4,128]{3,2,1,0:T(4,128)(2,1)}, u32[]{:S(2)}) copy-start(bf16[1,256,4,128]{3,2,1,0:T(4,128)(2,1)} %copy-done.9) | copy-start | bytes 786436
  122.1 22.4 %copy-start.19 = (bf16[2,32,4,128]{3,1,2,0:T(8,128)(2,1)}, bf16[2,32,4,128]{3,1,2,0:T(8,128)(2,1)S(1)}, u32[]{:S(2)}) copy-start(bf16[2,32,4,128]{3,1,2,0:T(8,128)(2,1)S(1)} %maximum_select_fusion.8) | copy-start | bytes 196612
  123.6 48.4 %collective-permute-start.13 = (bf16[2,128,4,128]{3,1,2,0:T(8,128)(2,1)}, bf16[2,128,4,128]{3,1,2,0:T(8,128)(2,1)}, u32[]{:S(2)}, u32[]{:S(2)}) collective-permute-start(bf16[2,128,4,128]{3,1,2,0:T(8,128)(2,1)} %maximum_select_fusion.1), channel_id=1, source_target_pairs={{16,0},{18,2},{20,4},{22,6},{24,8},{26,10},{28,12},{30,14},{32,16}... | collective-permute-start | bytes 786440 | tf_op jit(solution)/shard_map/ppermute | solution.py:31
  125.6 38.0 %collective-permute-start.12 = (bf16[2,128,4,128]{3,1,2,0:T(8,128)(2,1)}, bf16[2,128,4,128]{3,1,2,0:T(8,128)(2,1)}, u32[]{:S(2)}, u32[]{:S(2)}) collective-permute-start(bf16[2,128,4,128]{3,1,2,0:T(8,128)(2,1)} %maximum_select_fusion.1), channel_id=1, source_target_pairs={{0,16},{2,18},{4,20},{6,22},{8,24},{10,26},{12,28},{14,30},{16,32}... | collective-permute-start | bytes 786440 | tf_op jit(solution)/shard_map/ppermute | solution.py:31
  129.8 1.9 copy-start.11
  129.8 23.7 %collective-permute-start.15 = (bf16[2,96,4,128]{3,1,2,0:T(8,128)(2,1)}, bf16[2,96,4,128]{3,1,2,0:T(8,128)(2,1)}, u32[]{:S(2)}, u32[]{:S(2)}) collective-permute-start(bf16[2,96,4,128]{3,1,2,0:T(8,128)(2,1)} %pad_maximum_fusion.10), channel_id=1, source_target_pairs={{0,8},{2,10},{4,12},{6,14},{8,0},{10,2},{12,4},{14,6},{16,24},{18,... | collective-permute-start | bytes 589832 | tf_op jit(solution)/shard_map/ppermute | solution.py:12
  131.7 49.6 %collective-permute-start.10 = (bf16[2,128,4,128]{3,1,2,0:T(8,128)(2,1)}, bf16[2,128,4,128]{3,1,2,0:T(8,128)(2,1)}, u32[]{:S(2)}, u32[]{:S(2)}) collective-permute-start(bf16[2,128,4,128]{3,1,2,0:T(8,128)(2,1)} %get-tuple-element.32), channel_id=1, source_target_pairs={{0,4},{2,6},{4,0},{6,2},{8,12},{10,14},{12,8},{14,10},{16,20},{18,... | collective-permute-start | bytes 786440 | tf_op jit(solution)/shard_map/ppermute | solution.py:12
  145.5 1.0 copy-start.18
  150.1 12.9 %copy-start.20 = (bf16[2,32,4,128]{3,1,2,0:T(8,128)(2,1)S(1)}, bf16[2,32,4,128]{3,1,2,0:T(8,128)(2,1)}, u32[]{:S(2)}) copy-start(bf16[2,32,4,128]{3,1,2,0:T(8,128)(2,1)} %copy-done.19) | copy-start | bytes 196612
  154.4 28.6 %copy-start.22 = (f32[64,4,128]{2,1,0:T(4,128)S(1)}, f32[64,4,128]{2,1,0:T(4,128)}, u32[]{:S(2)}) copy-start(f32[64,4,128]{2,1,0:T(4,128)} %bitcast_reduce_fusion.18) | copy-start | bytes 393220
  154.5 28.6 %copy-start.39 = (pred[384]{0:T(512)(128)(4,1)S(1)}, pred[384]{0:T(512)(128)(4,1)}, u32[]{:S(2)}) copy-start(pred[384]{0:T(512)(128)(4,1)} %fusion.116) | copy-start | bytes 1156
  155.3 41.8 %collective-permute-start.17 = (bf16[2,128,4,128]{3,1,2,0:T(8,128)(2,1)}, bf16[2,128,4,128]{3,1,2,0:T(8,128)(2,1)}, u32[]{:S(2)}, u32[]{:S(2)}) collective-permute-start(bf16[2,128,4,128]{3,1,2,0:T(8,128)(2,1)} %maximum_select_fusion.2), channel_id=1, source_target_pairs={{32,0},{34,2},{36,4},{38,6},{40,8},{42,10},{44,12},{46,14},{48,16}... | collective-permute-start | bytes 786440 | tf_op jit(solution)/shard_map/ppermute | solution.py:31
  157.4 38.6 %collective-permute-start.16 = (bf16[2,128,4,128]{3,1,2,0:T(8,128)(2,1)}, bf16[2,128,4,128]{3,1,2,0:T(8,128)(2,1)}, u32[]{:S(2)}, u32[]{:S(2)}) collective-permute-start(bf16[2,128,4,128]{3,1,2,0:T(8,128)(2,1)} %maximum_select_fusion.2), channel_id=1, source_target_pairs={{0,32},{2,34},{4,36},{6,38},{8,40},{10,42},{12,44},{14,46},{16,48}... | collective-permute-start | bytes 786440 | tf_op jit(solution)/shard_map/ppermute | solution.py:31
  163.6 24.0 %collective-permute-start.19 = (bf16[2,64,4,128]{3,1,2,0:T(8,128)(2,1)}, bf16[2,64,4,128]{3,1,2,0:T(8,128)(2,1)}, u32[]{:S(2)}, u32[]{:S(2)}) collective-permute-start(bf16[2,64,4,128]{3,1,2,0:T(8,128)(2,1)} %maximum_select_fusion.6), channel_id=1, source_target_pairs={{0,16},{2,18},{4,20},{6,22},{8,24},{10,26},{12,28},{14,30},{16,0},... | collective-permute-start | bytes 393224 | tf_op jit(solution)/shard_map/ppermute | solution.py:12
  173.9 12.0 %copy-start.12 = (bf16[2,384,4,128]{3,1,2,0:T(8,128)(2,1)}, bf16[2,384,4,128]{3,1,2,0:T(8,128)(2,1)S(1)}, u32[]{:S(2)}) copy-start(bf16[2,384,4,128]{3,1,2,0:T(8,128)(2,1)S(1)} %get-tuple-element.35) | copy-start | bytes 2359300
  173.9 27.1 %collective-permute-start.14 = (bf16[2,128,4,128]{3,1,2,0:T(8,128)(2,1)}, bf16[2,128,4,128]{3,1,2,0:T(8,128)(2,1)}, u32[]{:S(2)}, u32[]{:S(2)}) collective-permute-start(bf16[2,128,4,128]{3,1,2,0:T(8,128)(2,1)} %get-tuple-element.34), channel_id=1, source_target_pairs={{0,8},{2,10},{4,12},{6,14},{8,0},{10,2},{12,4},{14,6},{16,24},{18,... | collective-permute-start | bytes 786440 | tf_op jit(solution)/shard_map/ppermute | solution.py:12
  185.9 16.9 %copy-start.26 = (f32[32,4,128]{2,1,0:T(4,128)S(1)}, f32[32,4,128]{2,1,0:T(4,128)}, u32[]{:S(2)}) copy-start(f32[32,4,128]{2,1,0:T(4,128)} %bitcast_reduce_fusion.9) | copy-start | bytes 196612
  186.0 16.9 %copy-start.42 = (pred[384]{0:T(512)(128)(4,1)S(1)}, pred[384]{0:T(512)(128)(4,1)}, u32[]{:S(2)}) copy-start(pred[384]{0:T(512)(128)(4,1)} %fusion.115) | copy-start | bytes 1156
  187.6 13.4 %copy-start.13 = (bf16[2,384,4,128]{3,1,2,0:T(8,128)(2,1)S(1)}, bf16[2,384,4,128]{3,1,2,0:T(8,128)(2,1)}, u32[]{:S(2)}) copy-start(bf16[2,384,4,128]{3,1,2,0:T(8,128)(2,1)} %copy-done.12) | copy-start | bytes 2359300
  189.6 17.4 %collective-permute-start.21 = (bf16[2,128,4,128]{3,1,2,0:T(8,128)(2,1)}, bf16[2,128,4,128]{3,1,2,0:T(8,128)(2,1)}, u32[]{:S(2)}, u32[]{:S(2)}) collective-permute-start(bf16[2,128,4,128]{3,1,2,0:T(8,128)(2,1)} %maximum_select_fusion.3), channel_id=1, source_target_pairs={{64,0},{66,2},{68,4},{70,6},{72,8},{74,10},{76,12},{78,14},{80,16}... | collective-permute-start | bytes 786440 | tf_op jit(solution)/shard_map/ppermute | solution.py:31
  191.5 15.4 %collective-permute-start.20 = (bf16[2,128,4,128]{3,1,2,0:T(8,128)(2,1)}, bf16[2,128,4,128]{3,1,2,0:T(8,128)(2,1)S(1)}, u32[]{:S(2)}, u32[]{:S(2)}) collective-permute-start(bf16[2,128,4,128]{3,1,2,0:T(8,128)(2,1)} %maximum_select_fusion.3), channel_id=1, source_target_pairs={{0,64},{2,66},{4,68},{6,70},{8,72},{10,74},{12,76},{14,78},{16,80}... | collective-permute-start | bytes 786440 | tf_op jit(solution)/shard_map/ppermute | solution.py:31
  198.9 4.3 %copy-start.15 = (bf16[2,384,4,128]{3,1,2,0:T(8,128)(2,1)}, bf16[2,384,4,128]{3,1,2,0:T(8,128)(2,1)S(1)}, u32[]{:S(2)}) copy-start(bf16[2,384,4,128]{3,1,2,0:T(8,128)(2,1)S(1)} %get-tuple-element.37) | copy-start | bytes 2359300
  198.9 17.3 %collective-permute-start.18 = (bf16[2,128,4,128]{3,1,2,0:T(8,128)(2,1)}, bf16[2,128,4,128]{3,1,2,0:T(8,128)(2,1)}, u32[]{:S(2)}, u32[]{:S(2)}) collective-permute-start(bf16[2,128,4,128]{3,1,2,0:T(8,128)(2,1)} %get-tuple-element.36), channel_id=1, source_target_pairs={{0,16},{2,18},{4,20},{6,22},{8,24},{10,26},{12,28},{14,30},{16,0},... | collective-permute-start | bytes 786440 | tf_op jit(solution)/shard_map/ppermute | solution.py:12
  202.0 0.9 copy-start.14
  205.0 11.2 %copy-start.16 = (bf16[2,384,4,128]{3,1,2,0:T(8,128)(2,1)S(1)}, bf16[2,384,4,128]{3,1,2,0:T(8,128)(2,1)}, u32[]{:S(2)}) copy-start(bf16[2,384,4,128]{3,1,2,0:T(8,128)(2,1)} %copy-done.15) | copy-start | bytes 2359300
  205.0 13.1 %copy-start.29 = (f32[16,4,128]{2,1,0:T(4,128)S(1)}, f32[16,4,128]{2,1,0:T(4,128)}, u32[]{:S(2)}) copy-start(f32[16,4,128]{2,1,0:T(4,128)} %bitcast_reduce_fusion.8) | copy-start | bytes 98308
  206.9 16.4 %copy-start.34 = (f32[8,4,128]{2,1,0:T(4,128)S(1)}, f32[8,4,128]{2,1,0:T(4,128)}, u32[]{:S(2)}) copy-start(f32[8,4,128]{2,1,0:T(4,128)} %bitcast_reduce_fusion.7) | copy-start | bytes 49156
  206.9 16.4 %copy-start.41 = (pred[384]{0:T(512)(128)(4,1)S(1)}, pred[384]{0:T(512)(128)(4,1)}, u32[]{:S(2)}) copy-start(pred[384]{0:T(512)(128)(4,1)} %fusion.113) | copy-start | bytes 1156
  208.7 10.3 %copy-start.21 = (bf16[2,384,4,128]{3,1,2,0:T(8,128)(2,1)}, bf16[2,384,4,128]{3,1,2,0:T(8,128)(2,1)S(1)}, u32[]{:S(2)}) copy-start(bf16[2,384,4,128]{3,1,2,0:T(8,128)(2,1)S(1)} %get-tuple-element.39) | copy-start | bytes 2359300
  208.8 13.9 %collective-permute-start.22 = (bf16[2,128,4,128]{3,1,2,0:T(8,128)(2,1)}, bf16[2,128,4,128]{3,1,2,0:T(8,128)(2,1)S(1)}, u32[]{:S(2)}, u32[]{:S(2)}) collective-permute-start(bf16[2,128,4,128]{3,1,2,0:T(8,128)(2,1)} %get-tuple-element.38), channel_id=1, source_target_pairs={{0,32},{2,34},{4,36},{6,38},{8,40},{10,42},{12,44},{14,46},{16,48}... | collective-permute-start | bytes 786440 | tf_op jit(solution)/shard_map/ppermute | solution.py:12
  217.2 0.9 copy-start.17
  245.3 1.2 copy-start.40
  245.3 1.3 copy-start.44
  256.9 1.2 copy-start.38
  256.9 1.3 copy-start.43
  260.7 1.5 copy-start.8
  260.7 1.5 copy-start.25
  260.7 1.5 copy-start.28
  260.7 1.5 copy-start.35
  260.8 1.5 copy-start.36
  260.8 1.5 copy-start.37
  (5 other events, 4.1 us)
Sparse Core Ops, SparseCore 0:
  21.3 158.6 all-gather.2
where the time goes:
time: 290 us; the launch traced here: 288 us
  starting transfers between devices  97.6 us (34%)
  local copies, waits for them, and re-layouts  64.6 us (22%)
  other arithmetic  62.2 us (21%)
  waiting for transfers between devices  19 us (7%)
  matrix products  18.7 us (6%)
  between operations  15.5 us (5%)
  blocking collectives  10.4 us (4%)
    ppermute x9, starting transfers between devices, partner_2(): return lax.ppermute(value, axis, pairs)  40.9 us
    ppermute x10, starting transfers between devices, shifted(): lax.ppermute(value, axis, [(source, source + steps) for source in range(i...  37 us
    ppermute x9, waiting for transfers between devices, partner_2(): return lax.ppermute(value, axis, pairs)  18.9 us
    ppermute x2, starting transfers between devices, with_halo(): after = lax.ppermute(initial, axis, down)  15.9 us
    reduce_sum x24, other arithmetic, coarsen(): summed = jnp.sum(grouped, axis=1)  13.7 us
    slice x4, local copies, waits for them, and re-layouts, gather_packed(): parts = lines[:, at:at + a.size].reshape(-1, *a.shape)  11.8 us
    dot_general x9, matrix products, level_attend(): jnp.einsum('nhqk,nkhd->nqhd', weights.astype(jnp.bfloat16), value_blocks,...  11.1 us
    all_to_all x1, blocking collectives, summed_on_arrival(): lax.all_to_all(cut_along(value, dim, length), axis, 0, 0, tiled=True)  10.4 us
  transfers between devices with their start and end apart: 24, of which 1 were waited for; matrix products, arithmetic and copies ran while one was open for 33% of the time, Pallas kernels for 0%

commit v1 on v0

v1 whole, which is shorter than its diff:
```python
import numpy as np
import jax
import jax.numpy as jnp
from jax import lax
from jax.sharding import PartitionSpec as P

BLOCK = 128
LEVEL_COUNT = 8


def shifted(value, count, steps):
    pairs = [(s, s + steps) for s in range(count) if 0 <= s + steps < count]
    return lax.ppermute(value, "seq", pairs)


def third_pairs(count, group):
    pairs = []
    for s in range(count):
        block = s // group
        target = s - 3 * group if block % 2 == 1 else s + 3 * group
        if 0 <= target < count:
            pairs.append((s, target))
    return pairs


def pooling_layout(token_count):
    row_level, row_index, offsets = [], [], {}
    offsets[1] = 0
    for r in range(token_count // 2):
        row_level.append(1)
        row_index.append(r)
    for level in range(2, LEVEL_COUNT + 1):
        offsets[level] = len(row_level)
        rows = token_count >> level
        for r in range(BLOCK):
            row_level.append(level)
            row_index.append(r if r < rows else -1)
    return np.array(row_level, np.int32), np.array(row_index, np.int32), offsets


def per_device(query_rows, key_rows, value_rows, out_weight):
    count = lax.axis_size("seq")
    device = lax.axis_index("seq")
    token_count, heads, head_size = query_rows.shape
    scale = float(head_size) ** (-0.5)
    local_blocks = token_count // BLOCK

    row_level, row_index, offsets = pooling_layout(token_count)
    tokens = lax.broadcasted_iota(jnp.int32, (row_level.shape[0], token_count), 1)
    pool = ((tokens >> row_level[:, None]) == row_index[:, None]).astype(jnp.bfloat16)
    width = heads * head_size
    stacked = jnp.concatenate(
        [
            query_rows.reshape(token_count, width),
            key_rows.reshape(token_count, width),
            value_rows.reshape(token_count, width),
        ],
        axis=1,
    )
    sums = jnp.dot(pool, stacked, preferred_element_type=jnp.float32)
    inverse = jnp.asarray((1.0 / (1 << row_level.astype(np.int64))).astype(np.float32))[:, None]
    coarse = jnp.concatenate(
        [sums[:, : 2 * width] * inverse, sums[:, 2 * width :]], axis=1
    ).astype(jnp.bfloat16)
    coarse_q = coarse[:, :width].reshape(-1, heads, head_size)
    coarse_kv = jnp.stack(
        [coarse[:, width : 2 * width], coarse[:, 2 * width :]]
    ).reshape(2, -1, heads, head_size)

    def level_kv(level):
        rows = token_count >> level
        at = offsets[level]
        return coarse_kv[:, at : at + rows]

    fine_kv = jnp.stack([key_rows, value_rows])
    first_kv = level_kv(1)
    up = jnp.concatenate([fine_kv[:, token_count - BLOCK :], first_kv], axis=1)
    down = jnp.concatenate([fine_kv[:, :BLOCK], first_kv], axis=1)
    from_left = shifted(up, count, 1)
    from_right = shifted(down, count, -1)

    pieces = {}
    for level in range(2, LEVEL_COUNT + 1):
        group = 1 << (level - 2)
        mine = level_kv(level)
        before = shifted(mine, count, 2 * group)
        after = shifted(mine, count, -2 * group)
        third = lax.ppermute(mine, "seq", third_pairs(count, group))
        pieces[level] = jnp.stack([before, after, third])

    for bit in range(LEVEL_COUNT - 2):
        members = [level for level in range(2, LEVEL_COUNT + 1) if level - 2 > bit]
        flat = jnp.concatenate([pieces[level].reshape(-1) for level in members])
        pairs = [(s, s ^ (1 << bit)) for s in range(count)]
        theirs = lax.ppermute(flat, "seq", pairs)
        at = 0
        for level in members:
            shape = pieces[level].shape
            size = pieces[level].size
            other = theirs[at : at + size].reshape(shape)
            at += size
            pieces[level] = jnp.concatenate([pieces[level], other], axis=2)

    fine_padded = jnp.concatenate(
        [from_left[:, :BLOCK], fine_kv, from_right[:, :BLOCK]], axis=1
    )
    fine_keys = jnp.stack(
        [fine_padded[:, b * BLOCK : (b + 3) * BLOCK] for b in range(local_blocks)], axis=1
    )
    left_first = from_left[:, BLOCK:]
    right_first = from_right[:, BLOCK:]
    first_even = jnp.concatenate(
        [left_first[:, :BLOCK], right_first[:, :BLOCK], right_first[:, BLOCK:]], axis=1
    )
    first_odd = jnp.concatenate(
        [left_first[:, BLOCK:], right_first[:, BLOCK:], left_first[:, :BLOCK]], axis=1
    )
    coarse_keys = jnp.stack(
        [pieces[level].transpose(1, 0, 2, 3, 4).reshape(2, 3 * BLOCK, heads, head_size)
         for level in range(2, LEVEL_COUNT + 1)],
        axis=1,
    )
    all_keys = jnp.concatenate(
        [fine_keys, first_even[:, None], first_odd[:, None], coarse_keys], axis=1
    )

    has_left = device >= 1
    has_right = device <= count - 2
    fine_index = device * local_blocks + jnp.arange(local_blocks, dtype=jnp.int32)
    fine_valid = jnp.stack(
        [fine_index >= 1, jnp.ones_like(has_left, shape=(local_blocks,)), fine_index + 1 < count * local_blocks],
        axis=1,
    )
    first_valid = jnp.stack(
        [jnp.stack([has_left, has_right, has_right]), jnp.stack([has_left, has_right, has_left])]
    )
    coarse_valid = []
    for level in range(2, LEVEL_COUNT + 1):
        group = 1 << (level - 2)
        block = device // group
        total = count // group
        even = block % 2 == 0
        coarse_valid.append(
            jnp.stack(
                [block >= 2, block + 2 < total, jnp.where(even, block + 3 < total, block >= 3)]
            )
        )
    valid = jnp.concatenate([fine_valid, first_valid, jnp.stack(coarse_valid)], axis=0)
    valid = jnp.repeat(valid, BLOCK, axis=1)

    all_queries = jnp.concatenate(
        [
            query_rows.reshape(local_blocks, BLOCK, heads, head_size),
            coarse_q.reshape(-1, BLOCK, heads, head_size),
        ],
        axis=0,
    )
    factors = jnp.asarray(
        np.array([1.0] * local_blocks + [2.0, 2.0] + [float(1 << l) for l in range(2, LEVEL_COUNT + 1)], np.float32)
    )

    scores = (
        jnp.einsum("nqhd,nkhd->nhqk", all_queries, all_keys[0], preferred_element_type=jnp.float32)
        * scale
    )
    scores = jnp.where(valid[:, None, None, :], scores, -jnp.inf)
    peak = jnp.max(scores, axis=3)
    weights = jnp.exp(scores - peak[..., None])
    denominator = factors[:, None, None] * jnp.sum(weights, axis=3)
    numerator = jnp.einsum(
        "nhqk,nkhd->nqhd", weights.astype(jnp.bfloat16), all_keys[1], preferred_element_type=jnp.float32
    )

    def expand(block_from, block_count, level):
        rows = (token_count >> level)
        m = peak[block_from : block_from + block_count].transpose(0, 2, 1).reshape(-1, heads)[:rows]
        r = denominator[block_from : block_from + block_count].transpose(0, 2, 1).reshape(-1, heads)[:rows]
        nn = numerator[block_from : block_from + block_count].reshape(-1, heads, head_size)[:rows]
        factor = 1 << level
        m = jnp.broadcast_to(m[:, None], (rows, factor, heads)).reshape(token_count, heads)
        r = jnp.broadcast_to(r[:, None], (rows, factor, heads)).reshape(token_count, heads)
        nn = jnp.broadcast_to(nn[:, None], (rows, factor, heads, head_size)).reshape(token_count, heads, head_size)
        return m, r, nn

    terms = [expand(0, local_blocks, 0), expand(local_blocks, 2, 1)]
    for level in range(2, LEVEL_COUNT + 1):
        terms.append(expand(local_blocks + level, 1, level))
    overall = terms[0][0]
    for term in terms[1:]:
        overall = jnp.maximum(overall, term[0])
    weighted = jnp.zeros((token_count, heads, head_size), jnp.float32)
    total_weight = jnp.zeros((token_count, heads), jnp.float32)
    for m, r, nn in terms:
        factor = jnp.exp(m - overall)
        weighted = weighted + factor[:, :, None] * nn
        total_weight = total_weight + factor * r
    attended = (weighted / total_weight[:, :, None]).astype(jnp.bfloat16)

    flattened = attended.reshape(token_count, heads * head_size)
    weight_flat = out_weight.reshape(heads * head_size, out_weight.shape[2])
    half = out_weight.shape[2] // 2
    core = lax.axis_index("head")
    other_weight = lax.dynamic_slice_in_dim(weight_flat, (1 - core) * half, half, axis=1)
    mine_weight = lax.dynamic_slice_in_dim(weight_flat, core * half, half, axis=1)
    other_part = jnp.dot(flattened, other_weight, preferred_element_type=jnp.float32).astype(jnp.bfloat16)
    received = lax.ppermute(other_part, "head", [(0, 1), (1, 0)])
    mine_part = jnp.dot(flattened, mine_weight, preferred_element_type=jnp.float32).astype(jnp.bfloat16)
    return (mine_part.astype(jnp.float32) + received.astype(jnp.float32)).astype(jnp.bfloat16)


def solution(mesh):
    return jax.shard_map(
        per_device,
        mesh=mesh,
        in_specs=(
            P("seq", "head", None),
            P("seq", "head", None),
            P("seq", "head", None),
            P("head", None, None),
        ),
        out_specs=P("seq", "head"),
        check_vma=False,
    )
```

time: 290 us -> 369 us (1.27)
  the two profiles are of different devices: /device:TPU:193 before, /device:TPU:1 now
where the time goes in v1:
time: 369 us; the launch traced here: 367 us
  starting transfers between devices  123 us (33%)
  waiting for transfers between devices  116 us (31%)
  local copies, waits for them, and re-layouts  91.5 us (25%)
  other arithmetic  17.5 us (5%)
  matrix products  16.1 us (4%)
    ppermute x6, waiting for transfers between devices, per_device(): theirs = lax.ppermute(flat, 'seq', pairs)  110 us
    ppermute x16, starting transfers between devices, shifted(): return lax.ppermute(value, 'seq', pairs)  50.8 us
    ppermute x7, starting transfers between devices, per_device(): third = lax.ppermute(mine, 'seq', third_pairs(count, group))  39.4 us
    ppermute x6, starting transfers between devices, per_device(): theirs = lax.ppermute(flat, 'seq', pairs)  27.6 us
    unnamed x162, local copies, waits for them, and re-layouts  16.9 us
    broadcast_in_dim x22, local copies, waits for them, and re-layouts, expand(): jnp.broadcast_to(nn[:, None], (rows, factor, heads, head_size))  10.9 us
    slice x8, local copies, waits for them, and re-layouts, level_kv(): return coarse_kv[:, at:at + rows]  9.49 us
    exp x9, local copies, waits for them, and re-layouts, per_device(): factor = jnp.exp(m - overall)  8.45 us
  transfers between devices with their start and end apart: 30, of which 10 were waited for; matrix products, arithmetic and copies ran while one was open for 12% of the time, Pallas kernels for 0%

profile of v1, /device:TPU:1, one launch (start us, length us, event | category | flops | bytes accessed | tf_op | source)
XLA Modules:
  0.0 366.6 jit_solution(5771966711373978872)
XLA Ops:
  1.3 1.4 copy_bitcast_fusion
  2.7 2.1 fusion.11
  5.8 1.6 fusion.71
  7.4 3.3 stack.291
  10.7 2.4 copy_dynamic-update-slice_fusion.1
  14.3 2.5 copy_dynamic-update-slice_fusion
  17.6 5.2 %collective-permute-start.13 = (bf16[2,16,4,128]{3,1,2,0:T(8,128)(2,1)S(1)}, bf16[2,16,4,128]{3,1,2,0:T(8,128)(2,1)S(1)}, u32[]{:S(2)}, u32[]{:S(2)}) collective-permute-start(bf16[2,16,4,128]{3,1,2,0:T(8,128)(2,1)S(1)} %slice.460), channel_id=1, source_target_pairs={{0,48},{2,50},{4,52},{6,54},{8,56},{10,58},{12,60},{14,62},{32,80}... | collective-permute-start | bytes 98312 | tf_op jit(solution)/shard_map/ppermute | solution.py:88
  22.8 1.3 collective-permute-start.12
  24.8 12.7 %collective-permute-start.22 = (bf16[2,2,4,128]{3,1,2,0:T(2,128)(2,1)S(1)}, bf16[2,2,4,128]{3,1,2,0:T(2,128)(2,1)S(1)}, u32[]{:S(2)}, u32[]{:S(2)}) collective-permute-start(bf16[2,2,4,128]{3,1,2,0:T(2,128)(2,1)S(1)} %slice.463), channel_id=1, source_target_pairs={{0,384},{2,386},{4,388},{6,390},{8,392},{10,394},{12,396},{14,398}... | collective-permute-start | bytes 12296 | tf_op jit(solution)/shard_map/ppermute | solution.py:88
  37.5 1.3 collective-permute-start.21
  38.8 7.9 %collective-permute-start.20 = (bf16[2,2,4,128]{3,1,2,0:T(2,128)(2,1)S(1)}, bf16[2,2,4,128]{3,1,2,0:T(2,128)(2,1)S(1)}, u32[]{:S(2)}, u32[]{:S(2)}) collective-permute-start(bf16[2,2,4,128]{3,1,2,0:T(2,128)(2,1)S(1)} %slice.463), channel_id=1, source_target_pairs={{0,256},{2,258},{4,260},{6,262},{8,264},{10,266},{12,268},{14,270}... | collective-permute-start | bytes 12296 | tf_op jit(solution)/shard_map/ppermute | solution.py:13
  46.8 1.9 slice.446
  48.7 1.3 copy_bitcast_fusion.3
  51.3 2.5 pad_maximum_fusion
  55.8 1.7 slice.457
  57.5 1.6 slice.458
  59.0 1.5 slice.459
  61.9 1.9 collective-permute-start.19
  63.9 1.3 collective-permute-start.18
  65.2 4.9 %collective-permute-start.17 = (bf16[2,4,4,128]{3,1,2,0:T(4,128)(2,1)S(1)}, bf16[2,4,4,128]{3,1,2,0:T(4,128)(2,1)S(1)}, u32[]{:S(2)}, u32[]{:S(2)}) collective-permute-start(bf16[2,4,4,128]{3,1,2,0:T(4,128)(2,1)S(1)} %slice.462), channel_id=1, source_target_pairs={{0,128},{2,130},{4,132},{6,134},{8,136},{10,138},{12,140},{14,142}... | collective-permute-start | bytes 24584 | tf_op jit(solution)/shard_map/ppermute | solution.py:13
  70.7 4.3 %collective-permute-start.16 = (bf16[2,8,4,128]{3,1,2,0:T(8,128)(2,1)S(1)}, bf16[2,8,4,128]{3,1,2,0:T(8,128)(2,1)S(1)}, u32[]{:S(2)}, u32[]{:S(2)}) collective-permute-start(bf16[2,8,4,128]{3,1,2,0:T(8,128)(2,1)S(1)} %slice.461), channel_id=1, source_target_pairs={{0,96},{2,98},{4,100},{6,102},{8,104},{10,106},{12,108},{14,110},{... | collective-permute-start | bytes 49160 | tf_op jit(solution)/shard_map/ppermute | solution.py:88
  75.1 1.3 collective-permute-start.15
  76.4 4.0 %collective-permute-start.14 = (bf16[2,8,4,128]{3,1,2,0:T(8,128)(2,1)S(1)}, bf16[2,8,4,128]{3,1,2,0:T(8,128)(2,1)S(1)}, u32[]{:S(2)}, u32[]{:S(2)}) collective-permute-start(bf16[2,8,4,128]{3,1,2,0:T(8,128)(2,1)S(1)} %slice.461), channel_id=1, source_target_pairs={{0,64},{2,66},{4,68},{6,70},{8,72},{10,74},{12,76},{14,78},{16,80}... | collective-permute-start | bytes 49160 | tf_op jit(solution)/shard_map/ppermute | solution.py:13
  81.1 2.2 collective-permute-start.11
  83.3 5.9 %collective-permute-start.7 = (bf16[2,64,4,128]{3,1,2,0:T(8,128)(2,1)}, bf16[2,64,4,128]{3,1,2,0:T(8,128)(2,1)S(1)}, u32[]{:S(2)}, u32[]{:S(2)}) collective-permute-start(bf16[2,64,4,128]{3,1,2,0:T(8,128)(2,1)} %slice.458), channel_id=1, source_target_pairs={{0,12},{2,14},{8,20},{10,22},{12,0},{14,2},{16,28},{18,30},{20,8},... | collective-permute-start | bytes 393224 | tf_op jit(solution)/shard_map/ppermute | solution.py:88
  89.2 7.5 %collective-permute-start.10 = (bf16[2,32,4,128]{3,1,2,0:T(8,128)(2,1)}, bf16[2,32,4,128]{3,1,2,0:T(8,128)(2,1)S(1)}, u32[]{:S(2)}, u32[]{:S(2)}) collective-permute-start(bf16[2,32,4,128]{3,1,2,0:T(8,128)(2,1)} %slice.459), channel_id=1, source_target_pairs={{0,24},{2,26},{4,28},{6,30},{16,40},{18,42},{20,44},{22,46},{24,0}... | collective-permute-start | bytes 196616 | tf_op jit(solution)/shard_map/ppermute | solution.py:88
  97.4 1.3 collective-permute-start.6
  98.7 7.9 %collective-permute-start.5 = (bf16[2,64,4,128]{3,1,2,0:T(8,128)(2,1)}, bf16[2,64,4,128]{3,1,2,0:T(8,128)(2,1)S(1)}, u32[]{:S(2)}, u32[]{:S(2)}) collective-permute-start(bf16[2,64,4,128]{3,1,2,0:T(8,128)(2,1)} %slice.458), channel_id=1, source_target_pairs={{0,8},{2,10},{4,12},{6,14},{8,16},{10,18},{12,20},{14,22},{16,24},... | collective-permute-start | bytes 393224 | tf_op jit(solution)/shard_map/ppermute | solution.py:13
  106.6 1.3 collective-permute-start.9
  108.0 4.0 %collective-permute-start.8 = (bf16[2,32,4,128]{3,1,2,0:T(8,128)(2,1)}, bf16[2,32,4,128]{3,1,2,0:T(8,128)(2,1)S(1)}, u32[]{:S(2)}, u32[]{:S(2)}) collective-permute-start(bf16[2,32,4,128]{3,1,2,0:T(8,128)(2,1)} %slice.459), channel_id=1, source_target_pairs={{0,16},{2,18},{4,20},{6,22},{8,24},{10,26},{12,28},{14,30},{16,32}... | collective-permute-start | bytes 196616 | tf_op jit(solution)/shard_map/ppermute | solution.py:13
  112.2 1.9 collective-permute-start.4
  114.9 1.3 collective-permute-start.3
  116.4 5.6 %collective-permute-start.2 = (bf16[2,128,4,128]{3,1,2,0:T(8,128)(2,1)}, bf16[2,128,4,128]{3,1,2,0:T(8,128)(2,1)}, u32[]{:S(2)}, u32[]{:S(2)}) collective-permute-start(bf16[2,128,4,128]{3,1,2,0:T(8,128)(2,1)} %slice.457), channel_id=1, source_target_pairs={{0,4},{2,6},{4,8},{6,10},{8,12},{10,14},{12,16},{14,18},{16,20},{1... | collective-permute-start | bytes 786440 | tf_op jit(solution)/shard_map/ppermute | solution.py:13
  122.0 4.1 %collective-permute-start = (bf16[2,384,4,128]{3,1,2,0:T(8,128)(2,1)}, bf16[2,384,4,128]{3,1,2,0:T(8,128)(2,1)}, u32[]{:S(2)}, u32[]{:S(2)}) collective-permute-start(bf16[2,384,4,128]{3,1,2,0:T(8,128)(2,1)} %get-tuple-element.23), channel_id=1, source_target_pairs={{0,2},{2,4},{4,6},{6,8},{8,10},{10,12},{12,14},{14,16},{16,18},{18... | collective-permute-start | bytes 2359304 | tf_op jit(solution)/shard_map/ppermute | solution.py:13
  126.1 1.3 collective-permute-start.1
  131.7 4.0 %collective-permute-start.23 = (bf16[387072]{0:T(1024)(128)(2,1)}, bf16[387072]{0:T(1024)(128)(2,1)}, u32[]{:S(2)}, u32[]{:S(2)}) collective-permute-start(bf16[387072]{0:T(1024)(128)(2,1)} %constant_dynamic-update-slice_fusion.51), channel_id=1, source_target_pairs={{0,2},{2,0},{4,6},{6,4},{8,10},{10,8},{12,14},{14,12},{16,18},{18,... | collective-permute-start | bytes 2322440 | tf_op jit(solution)/shard_map/ppermute | solution.py:95
  137.7 2.5 concatenate.128
  141.5 3.3 reshape_reshape.3
  144.8 2.7 copy.415
  150.8 2.8 collective-permute-done
  154.9 15.3 %collective-permute-done.23 = bf16[387072]{0:T(1024)(128)(2,1)} collective-permute-done((bf16[387072]{0:T(1024)(128)(2,1)}, bf16[387072]{0:T(1024)(128)(2,1)}, u32[]{:S(2)}, u32[]{:S(2)}) %collective-permute-start.23) | collective-permute-done | bytes 774176 | tf_op jit(solution)/shard_map/ppermute | solution.py:95
  175.3 3.9 %collective-permute-start.24 = (bf16[380928]{0:T(1024)(128)(2,1)S(1)}, bf16[380928]{0:T(1024)(128)(2,1)S(1)}, u32[]{:S(2)}, u32[]{:S(2)}) collective-permute-start(bf16[380928]{0:T(1024)(128)(2,1)S(1)} %constant_dynamic-update-slice_fusion.44), channel_id=1, source_target_pairs={{0,4},{2,6},{4,0},{6,2},{8,12},{10,14},{12,8},{14,10},{16,20},{18,... | collective-permute-start | bytes 2285576 | tf_op jit(solution)/shard_map/ppermute | solution.py:95
  180.8 30.7 %collective-permute-done.24 = bf16[380928]{0:T(1024)(128)(2,1)S(1)} collective-permute-done((bf16[380928]{0:T(1024)(128)(2,1)S(1)}, bf16[380928]{0:T(1024)(128)(2,1)S(1)}, u32[]{:S(2)}, u32[]{:S(2)}) %collective-permute-start.24) | collective-permute-done | bytes 761888 | tf_op jit(solution)/shard_map/ppermute | solution.py:95
  212.1 5.1 %collective-permute-start.25 = (bf16[368640]{0:T(1024)(128)(2,1)S(1)}, bf16[368640]{0:T(1024)(128)(2,1)S(1)}, u32[]{:S(2)}, u32[]{:S(2)}) collective-permute-start(bf16[368640]{0:T(1024)(128)(2,1)S(1)} %pad_maximum_fusion.6), channel_id=1, source_target_pairs={{0,8},{2,10},{4,12},{6,14},{8,0},{10,2},{12,4},{14,6},{16,24},{18,... | collective-permute-start | bytes 2211848 | tf_op jit(solution)/shard_map/ppermute | solution.py:95
  219.3 32.8 %collective-permute-done.25 = bf16[368640]{0:T(1024)(128)(2,1)S(1)} collective-permute-done((bf16[368640]{0:T(1024)(128)(2,1)S(1)}, bf16[368640]{0:T(1024)(128)(2,1)S(1)}, u32[]{:S(2)}, u32[]{:S(2)}) %collective-permute-start.25) | collective-permute-done | bytes 737312 | tf_op jit(solution)/shard_map/ppermute | solution.py:95
  252.7 3.1 collective-permute-start.26
  256.8 14.3 %collective-permute-done.26 = bf16[344064]{0:T(1024)(128)(2,1)S(1)} collective-permute-done((bf16[344064]{0:T(1024)(128)(2,1)S(1)}, bf16[344064]{0:T(1024)(128)(2,1)S(1)}, u32[]{:S(2)}, u32[]{:S(2)}) %collective-permute-start.26) | collective-permute-done | bytes 688160 | tf_op jit(solution)/shard_map/ppermute | solution.py:95
  271.5 4.3 %collective-permute-start.27 = (bf16[294912]{0:T(1024)(128)(2,1)S(1)}, bf16[294912]{0:T(1024)(128)(2,1)S(1)}, u32[]{:S(2)}, u32[]{:S(2)}) collective-permute-start(bf16[294912]{0:T(1024)(128)(2,1)S(1)} %pad_maximum_fusion.8), channel_id=1, source_target_pairs={{0,32},{2,34},{4,36},{6,38},{8,40},{10,42},{12,44},{14,46},{16,48}... | collective-permute-start | bytes 1769480 | tf_op jit(solution)/shard_map/ppermute | solution.py:95
  276.9 11.1 %collective-permute-done.27 = bf16[294912]{0:T(1024)(128)(2,1)S(1)} collective-permute-done((bf16[294912]{0:T(1024)(128)(2,1)S(1)}, bf16[294912]{0:T(1024)(128)(2,1)S(1)}, u32[]{:S(2)}, u32[]{:S(2)}) %collective-permute-start.27) | collective-permute-done | bytes 589856 | tf_op jit(solution)/shard_map/ppermute | solution.py:95
  288.3 7.3 %collective-permute-start.28 = (bf16[196608]{0:T(1024)(128)(2,1)S(1)}, bf16[196608]{0:T(1024)(128)(2,1)S(1)}, u32[]{:S(2)}, u32[]{:S(2)}) collective-permute-start(bf16[196608]{0:T(1024)(128)(2,1)S(1)} %bitcast.595), channel_id=1, source_target_pairs={{0,64},{2,66},{4,68},{6,70},{8,72},{10,74},{12,76},{14,78},{16,80}... | collective-permute-start | bytes 1179656 | tf_op jit(solution)/shard_map/ppermute | solution.py:95
  296.5 6.1 %collective-permute-done.28 = bf16[196608]{0:T(1024)(128)(2,1)S(1)} collective-permute-done((bf16[196608]{0:T(1024)(128)(2,1)S(1)}, bf16[196608]{0:T(1024)(128)(2,1)S(1)}, u32[]{:S(2)}, u32[]{:S(2)}) %collective-permute-start.28) | collective-permute-done | bytes 393248 | tf_op jit(solution)/shard_map/ppermute | solution.py:95
  303.1 3.9 %copy-done.46 = bf16[2,13,384,4,128]{4,2,3,1,0:T(8,128)(2,1)} copy-done((bf16[2,13,384,4,128]{4,2,3,1,0:T(8,128)(2,1)}, bf16[2,13,384,4,128]{4,2,3,1,0:T(8,128)(2,1)S(1)}, u32[]{:S(2)}) %copy-start.46) | copy-done | bytes 10223640
  307.0 4.3 %fusion = (f32[13,4,128]{2,1,0:T(4,128)S(1)}, f32[13,4,128,384]{3,2,1,0:T(8,128)S(1)}) fusion(pred[13,384]{1,0:T(8,128)(4,1)S(1)} %bitcast.586, bf16[2,13,384,4,128]{4,2,3,1,0:T(8,128)(2,1)} %copy-done.46, bf16[9,128,4,128]{3,1,2,0:T(8,128)(2,1)S(1)} %copy-done.4, bf16[4,128,4,128]{3,1,2,0:T(8,128)(2,1)S(1)} %copy-done.19), kind=kOutput, calls=%fused_computation.2 | convolution fusion | flops 662824448 | bytes 17070976 | tf_op jit(solution)/shard_map/nqhd,nkhd->nhqk/dot_general | solution.py:163
  311.3 3.1 fusion.1
  314.5 5.3 %fusion.12 = f32[13,128,4,128]{3,1,2,0:T(8,128)S(1)} fusion(bf16[2,13,384,4,128]{4,2,3,1,0:T(8,128)(2,1)} %copy-done.46, f32[13,4,128,384]{3,2,1,0:T(8,128)S(1)} %get-tuple-element.70, f32[13,4,128]{2,1,0:T(4,128)S(1)} %get-tuple-element.69, pred[13,384]{1,0:T(8,128)(4,1)S(1)} %bitcast.588), kind=kOutput, calls=%fused_computation.19 | convolution fusion | flops 664535040 | bytes 18774912 | tf_op jit(solution)/shard_map/nhqk,nkhd->nqhd/dot_general | solution.py:170
  331.7 1.4 copy.483
  333.9 1.5 copy.481
  340.9 1.9 copy.471
  342.8 1.6 copy.470
  352.4 1.5 fusion.27
  354.8 1.7 convolution_convert_fusion
  356.5 4.9 %collective-permute-start.29 = (bf16[512,1024]{1,0:T(8,128)(2,1)}, bf16[512,1024]{1,0:T(8,128)(2,1)S(1)}, u32[]{:S(2)}, u32[]{:S(2)}) collective-permute-start(bf16[512,1024]{1,0:T(8,128)(2,1)} %convolution_convert_fusion), channel_id=1, source_target_pairs={{0,1},{1,0},{2,3},{3,2},{4,5},{5,4},{6,7},{7,6},{8,9},{9,8},{10,11... | collective-permute-start | bytes 3145736 | tf_op jit(solution)/shard_map/ppermute | solution.py:206
  361.4 2.5 collective-permute-done.29
  363.8 2.7 add_convert_fusion
  (370 shorter events, 65.2 us)
Async XLA Ops:
  0.0 353.9 %copy-start = (bf16[4,128,2048]{2,1,0:T(8,128)(2,1)S(1)}, bf16[4,128,2048]{2,1,0:T(8,128)(2,1)}, u32[]{:S(2)}) copy-start(bf16[4,128,2048]{2,1,0:T(8,128)(2,1)} %param.11) | copy-start | bytes 6291460
  17.6 79.9 %collective-permute-start.13 = (bf16[2,16,4,128]{3,1,2,0:T(8,128)(2,1)S(1)}, bf16[2,16,4,128]{3,1,2,0:T(8,128)(2,1)S(1)}, u32[]{:S(2)}, u32[]{:S(2)}) collective-permute-start(bf16[2,16,4,128]{3,1,2,0:T(8,128)(2,1)S(1)} %slice.460), channel_id=1, source_target_pairs={{0,48},{2,50},{4,52},{6,54},{8,56},{10,58},{12,60},{14,62},{32,80}... | collective-permute-start | bytes 98312 | tf_op jit(solution)/shard_map/ppermute | solution.py:88
  22.8 75.9 %collective-permute-start.12 = (bf16[2,16,4,128]{3,1,2,0:T(8,128)(2,1)S(1)}, bf16[2,16,4,128]{3,1,2,0:T(8,128)(2,1)S(1)}, u32[]{:S(2)}, u32[]{:S(2)}) collective-permute-start(bf16[2,16,4,128]{3,1,2,0:T(8,128)(2,1)S(1)} %slice.460), channel_id=1, source_target_pairs={{32,0},{34,2},{36,4},{38,6},{40,8},{42,10},{44,12},{46,14},{48,16}... | collective-permute-start | bytes 98312 | tf_op jit(solution)/shard_map/ppermute | solution.py:13
  24.8 37.1 %collective-permute-start.22 = (bf16[2,2,4,128]{3,1,2,0:T(2,128)(2,1)S(1)}, bf16[2,2,4,128]{3,1,2,0:T(2,128)(2,1)S(1)}, u32[]{:S(2)}, u32[]{:S(2)}) collective-permute-start(bf16[2,2,4,128]{3,1,2,0:T(2,128)(2,1)S(1)} %slice.463), channel_id=1, source_target_pairs={{0,384},{2,386},{4,388},{6,390},{8,392},{10,394},{12,396},{14,398}... | collective-permute-start | bytes 12296 | tf_op jit(solution)/shard_map/ppermute | solution.py:88
  37.5 26.4 %collective-permute-start.21 = (bf16[2,2,4,128]{3,1,2,0:T(2,128)(2,1)S(1)}, bf16[2,2,4,128]{3,1,2,0:T(2,128)(2,1)S(1)}, u32[]{:S(2)}, u32[]{:S(2)}) collective-permute-start(bf16[2,2,4,128]{3,1,2,0:T(2,128)(2,1)S(1)} %slice.463), channel_id=1, source_target_pairs={{256,0},{258,2},{260,4},{262,6},{264,8},{266,10},{268,12},{270,14}... | collective-permute-start | bytes 12296 | tf_op jit(solution)/shard_map/ppermute | solution.py:13
  38.8 26.4 %collective-permute-start.20 = (bf16[2,2,4,128]{3,1,2,0:T(2,128)(2,1)S(1)}, bf16[2,2,4,128]{3,1,2,0:T(2,128)(2,1)S(1)}, u32[]{:S(2)}, u32[]{:S(2)}) collective-permute-start(bf16[2,2,4,128]{3,1,2,0:T(2,128)(2,1)S(1)} %slice.463), channel_id=1, source_target_pairs={{0,256},{2,258},{4,260},{6,262},{8,264},{10,266},{12,268},{14,270}... | collective-permute-start | bytes 12296 | tf_op jit(solution)/shard_map/ppermute | solution.py:13
  61.9 8.8 %collective-permute-start.19 = (bf16[2,4,4,128]{3,1,2,0:T(4,128)(2,1)S(1)}, bf16[2,4,4,128]{3,1,2,0:T(4,128)(2,1)S(1)}, u32[]{:S(2)}, u32[]{:S(2)}) collective-permute-start(bf16[2,4,4,128]{3,1,2,0:T(4,128)(2,1)S(1)} %slice.462), channel_id=1, source_target_pairs={{0,192},{2,194},{4,196},{6,198},{8,200},{10,202},{12,204},{14,206}... | collective-permute-start | bytes 24584 | tf_op jit(solution)/shard_map/ppermute | solution.py:88
  63.8 16.6 %copy-start.53 = (bf16[2,2,4,128]{3,1,2,0:T(2,128)(2,1)}, bf16[2,2,4,128]{3,1,2,0:T(2,128)(2,1)S(1)}, u32[]{:S(2)}) copy-start(bf16[2,2,4,128]{3,1,2,0:T(2,128)(2,1)S(1)} %collective-permute-done.21) | copy-start | bytes 12292
  63.9 11.2 %collective-permute-start.18 = (bf16[2,4,4,128]{3,1,2,0:T(4,128)(2,1)S(1)}, bf16[2,4,4,128]{3,1,2,0:T(4,128)(2,1)S(1)}, u32[]{:S(2)}, u32[]{:S(2)}) collective-permute-start(bf16[2,4,4,128]{3,1,2,0:T(4,128)(2,1)S(1)} %slice.462), channel_id=1, source_target_pairs={{128,0},{130,2},{132,4},{134,6},{136,8},{138,10},{140,12},{142,14}... | collective-permute-start | bytes 24584 | tf_op jit(solution)/shard_map/ppermute | solution.py:13
  65.2 15.3 %copy-start.55 = (bf16[2,2,4,128]{3,1,2,0:T(2,128)(2,1)}, bf16[2,2,4,128]{3,1,2,0:T(2,128)(2,1)S(1)}, u32[]{:S(2)}) copy-start(bf16[2,2,4,128]{3,1,2,0:T(2,128)(2,1)S(1)} %collective-permute-done.20) | copy-start | bytes 12292
  65.2 11.2 %collective-permute-start.17 = (bf16[2,4,4,128]{3,1,2,0:T(4,128)(2,1)S(1)}, bf16[2,4,4,128]{3,1,2,0:T(4,128)(2,1)S(1)}, u32[]{:S(2)}, u32[]{:S(2)}) collective-permute-start(bf16[2,4,4,128]{3,1,2,0:T(4,128)(2,1)S(1)} %slice.462), channel_id=1, source_target_pairs={{0,128},{2,130},{4,132},{6,134},{8,136},{10,138},{12,140},{14,142}... | collective-permute-start | bytes 24584 | tf_op jit(solution)/shard_map/ppermute | solution.py:13
  70.7 10.4 %collective-permute-start.16 = (bf16[2,8,4,128]{3,1,2,0:T(8,128)(2,1)S(1)}, bf16[2,8,4,128]{3,1,2,0:T(8,128)(2,1)S(1)}, u32[]{:S(2)}, u32[]{:S(2)}) collective-permute-start(bf16[2,8,4,128]{3,1,2,0:T(8,128)(2,1)S(1)} %slice.461), channel_id=1, source_target_pairs={{0,96},{2,98},{4,100},{6,102},{8,104},{10,106},{12,108},{14,110},{... | collective-permute-start | bytes 49160 | tf_op jit(solution)/shard_map/ppermute | solution.py:88
  75.1 6.0 %copy-start.48 = (bf16[2,4,4,128]{3,1,2,0:T(4,128)(2,1)}, bf16[2,4,4,128]{3,1,2,0:T(4,128)(2,1)S(1)}, u32[]{:S(2)}) copy-start(bf16[2,4,4,128]{3,1,2,0:T(4,128)(2,1)S(1)} %collective-permute-done.18) | copy-start | bytes 24580
  75.1 8.2 %collective-permute-start.15 = (bf16[2,8,4,128]{3,1,2,0:T(8,128)(2,1)S(1)}, bf16[2,8,4,128]{3,1,2,0:T(8,128)(2,1)S(1)}, u32[]{:S(2)}, u32[]{:S(2)}) collective-permute-start(bf16[2,8,4,128]{3,1,2,0:T(8,128)(2,1)S(1)} %slice.461), channel_id=1, source_target_pairs={{64,0},{66,2},{68,4},{70,6},{72,8},{74,10},{76,12},{78,14},{80,16}... | collective-permute-start | bytes 49160 | tf_op jit(solution)/shard_map/ppermute | solution.py:13
  76.4 20.3 %copy-start.50 = (bf16[2,4,4,128]{3,1,2,0:T(4,128)(2,1)}, bf16[2,4,4,128]{3,1,2,0:T(4,128)(2,1)S(1)}, u32[]{:S(2)}) copy-start(bf16[2,4,4,128]{3,1,2,0:T(4,128)(2,1)S(1)} %collective-permute-done.17) | copy-start | bytes 24580
  76.4 12.8 %collective-permute-start.14 = (bf16[2,8,4,128]{3,1,2,0:T(8,128)(2,1)S(1)}, bf16[2,8,4,128]{3,1,2,0:T(8,128)(2,1)S(1)}, u32[]{:S(2)}, u32[]{:S(2)}) collective-permute-start(bf16[2,8,4,128]{3,1,2,0:T(8,128)(2,1)S(1)} %slice.461), channel_id=1, source_target_pairs={{0,64},{2,66},{4,68},{6,70},{8,72},{10,74},{12,76},{14,78},{16,80}... | collective-permute-start | bytes 49160 | tf_op jit(solution)/shard_map/ppermute | solution.py:13
  81.1 25.5 %collective-permute-start.11 = (bf16[2,16,4,128]{3,1,2,0:T(8,128)(2,1)S(1)}, bf16[2,16,4,128]{3,1,2,0:T(8,128)(2,1)S(1)}, u32[]{:S(2)}, u32[]{:S(2)}) collective-permute-start(bf16[2,16,4,128]{3,1,2,0:T(8,128)(2,1)S(1)} %slice.460), channel_id=1, source_target_pairs={{0,32},{2,34},{4,36},{6,38},{8,40},{10,42},{12,44},{14,46},{16,48}... | collective-permute-start | bytes 98312 | tf_op jit(solution)/shard_map/ppermute | solution.py:13
  83.3 28.7 %copy-start.42 = (bf16[2,8,4,128]{3,1,2,0:T(8,128)(2,1)}, bf16[2,8,4,128]{3,1,2,0:T(8,128)(2,1)S(1)}, u32[]{:S(2)}) copy-start(bf16[2,8,4,128]{3,1,2,0:T(8,128)(2,1)S(1)} %collective-permute-done.15) | copy-start | bytes 49156
  83.3 33.1 %collective-permute-start.7 = (bf16[2,64,4,128]{3,1,2,0:T(8,128)(2,1)}, bf16[2,64,4,128]{3,1,2,0:T(8,128)(2,1)S(1)}, u32[]{:S(2)}, u32[]{:S(2)}) collective-permute-start(bf16[2,64,4,128]{3,1,2,0:T(8,128)(2,1)} %slice.458), channel_id=1, source_target_pairs={{0,12},{2,14},{8,20},{10,22},{12,0},{14,2},{16,28},{18,30},{20,8},... | collective-permute-start | bytes 393224 | tf_op jit(solution)/shard_map/ppermute | solution.py:88
  89.2 22.8 %copy-start.44 = (bf16[2,8,4,128]{3,1,2,0:T(8,128)(2,1)}, bf16[2,8,4,128]{3,1,2,0:T(8,128)(2,1)S(1)}, u32[]{:S(2)}) copy-start(bf16[2,8,4,128]{3,1,2,0:T(8,128)(2,1)S(1)} %collective-permute-done.14) | copy-start | bytes 49156
  89.2 18.7 %collective-permute-start.10 = (bf16[2,32,4,128]{3,1,2,0:T(8,128)(2,1)}, bf16[2,32,4,128]{3,1,2,0:T(8,128)(2,1)S(1)}, u32[]{:S(2)}, u32[]{:S(2)}) collective-permute-start(bf16[2,32,4,128]{3,1,2,0:T(8,128)(2,1)} %slice.459), channel_id=1, source_target_pairs={{0,24},{2,26},{4,28},{6,30},{16,40},{18,42},{20,44},{22,46},{24,0}... | collective-permute-start | bytes 196616 | tf_op jit(solution)/shard_map/ppermute | solution.py:88
  97.4 18.8 %copy-start.36 = (bf16[2,16,4,128]{3,1,2,0:T(8,128)(2,1)}, bf16[2,16,4,128]{3,1,2,0:T(8,128)(2,1)S(1)}, u32[]{:S(2)}) copy-start(bf16[2,16,4,128]{3,1,2,0:T(8,128)(2,1)S(1)} %collective-permute-done.13) | copy-start | bytes 98308
  97.4 24.6 %collective-permute-start.6 = (bf16[2,64,4,128]{3,1,2,0:T(8,128)(2,1)}, bf16[2,64,4,128]{3,1,2,0:T(8,128)(2,1)S(1)}, u32[]{:S(2)}, u32[]{:S(2)}) collective-permute-start(bf16[2,64,4,128]{3,1,2,0:T(8,128)(2,1)} %slice.458), channel_id=1, source_target_pairs={{8,0},{10,2},{12,4},{14,6},{16,8},{18,10},{20,12},{22,14},{24,16},... | collective-permute-start | bytes 393224 | tf_op jit(solution)/shard_map/ppermute | solution.py:13
  98.7 13.3 %copy-start.38 = (bf16[2,16,4,128]{3,1,2,0:T(8,128)(2,1)}, bf16[2,16,4,128]{3,1,2,0:T(8,128)(2,1)S(1)}, u32[]{:S(2)}) copy-start(bf16[2,16,4,128]{3,1,2,0:T(8,128)(2,1)S(1)} %collective-permute-done.12) | copy-start | bytes 98308
  98.7 27.4 %collective-permute-start.5 = (bf16[2,64,4,128]{3,1,2,0:T(8,128)(2,1)}, bf16[2,64,4,128]{3,1,2,0:T(8,128)(2,1)S(1)}, u32[]{:S(2)}, u32[]{:S(2)}) collective-permute-start(bf16[2,64,4,128]{3,1,2,0:T(8,128)(2,1)} %slice.458), channel_id=1, source_target_pairs={{0,8},{2,10},{4,12},{6,14},{8,16},{10,18},{12,20},{14,22},{16,24},... | collective-permute-start | bytes 393224 | tf_op jit(solution)/shard_map/ppermute | solution.py:13
  106.6 5.4 %copy-start.40 = (bf16[2,16,4,128]{3,1,2,0:T(8,128)(2,1)}, bf16[2,16,4,128]{3,1,2,0:T(8,128)(2,1)S(1)}, u32[]{:S(2)}) copy-start(bf16[2,16,4,128]{3,1,2,0:T(8,128)(2,1)S(1)} %collective-permute-done.11) | copy-start | bytes 98308
  106.6 5.5 %collective-permute-start.9 = (bf16[2,32,4,128]{3,1,2,0:T(8,128)(2,1)}, bf16[2,32,4,128]{3,1,2,0:T(8,128)(2,1)S(1)}, u32[]{:S(2)}, u32[]{:S(2)}) collective-permute-start(bf16[2,32,4,128]{3,1,2,0:T(8,128)(2,1)} %slice.459), channel_id=1, source_target_pairs={{16,0},{18,2},{20,4},{22,6},{24,8},{26,10},{28,12},{30,14},{32,16}... | collective-permute-start | bytes 196616 | tf_op jit(solution)/shard_map/ppermute | solution.py:13
  108.0 8.3 %copy-start.28 = (bf16[2,32,4,128]{3,1,2,0:T(8,128)(2,1)}, bf16[2,32,4,128]{3,1,2,0:T(8,128)(2,1)S(1)}, u32[]{:S(2)}) copy-start(bf16[2,32,4,128]{3,1,2,0:T(8,128)(2,1)S(1)} %collective-permute-done.10) | copy-start | bytes 196612
  108.0 6.9 %collective-permute-start.8 = (bf16[2,32,4,128]{3,1,2,0:T(8,128)(2,1)}, bf16[2,32,4,128]{3,1,2,0:T(8,128)(2,1)S(1)}, u32[]{:S(2)}, u32[]{:S(2)}) collective-permute-start(bf16[2,32,4,128]{3,1,2,0:T(8,128)(2,1)} %slice.459), channel_id=1, source_target_pairs={{0,16},{2,18},{4,20},{6,22},{8,24},{10,26},{12,28},{14,30},{16,32}... | collective-permute-start | bytes 196616 | tf_op jit(solution)/shard_map/ppermute | solution.py:13
  112.2 15.2 %copy-start.30 = (bf16[2,32,4,128]{3,1,2,0:T(8,128)(2,1)}, bf16[2,32,4,128]{3,1,2,0:T(8,128)(2,1)S(1)}, u32[]{:S(2)}) copy-start(bf16[2,32,4,128]{3,1,2,0:T(8,128)(2,1)S(1)} %collective-permute-done.9) | copy-start | bytes 196612
  112.2 19.6 %collective-permute-start.4 = (bf16[2,128,4,128]{3,1,2,0:T(8,128)(2,1)}, bf16[2,128,4,128]{3,1,2,0:T(8,128)(2,1)}, u32[]{:S(2)}, u32[]{:S(2)}) collective-permute-start(bf16[2,128,4,128]{3,1,2,0:T(8,128)(2,1)} %slice.457), channel_id=1, source_target_pairs={{0,6},{4,10},{6,0},{8,14},{10,4},{12,18},{14,8},{16,22},{18,12},{2... | collective-permute-start | bytes 786440 | tf_op jit(solution)/shard_map/ppermute | solution.py:88
  114.9 12.5 %copy-start.32 = (bf16[2,32,4,128]{3,1,2,0:T(8,128)(2,1)}, bf16[2,32,4,128]{3,1,2,0:T(8,128)(2,1)S(1)}, u32[]{:S(2)}) copy-start(bf16[2,32,4,128]{3,1,2,0:T(8,128)(2,1)S(1)} %collective-permute-done.8) | copy-start | bytes 196612
  114.9 33.5 %collective-permute-start.3 = (bf16[2,128,4,128]{3,1,2,0:T(8,128)(2,1)}, bf16[2,128,4,128]{3,1,2,0:T(8,128)(2,1)}, u32[]{:S(2)}, u32[]{:S(2)}) collective-permute-start(bf16[2,128,4,128]{3,1,2,0:T(8,128)(2,1)} %slice.457), channel_id=1, source_target_pairs={{4,0},{6,2},{8,4},{10,6},{12,8},{14,10},{16,12},{18,14},{20,16},{2... | collective-permute-start | bytes 786440 | tf_op jit(solution)/shard_map/ppermute | solution.py:13
  116.4 11.0 %copy-start.20 = (bf16[2,64,4,128]{3,1,2,0:T(8,128)(2,1)}, bf16[2,64,4,128]{3,1,2,0:T(8,128)(2,1)S(1)}, u32[]{:S(2)}) copy-start(bf16[2,64,4,128]{3,1,2,0:T(8,128)(2,1)S(1)} %collective-permute-done.7) | copy-start | bytes 393220
  116.4 32.0 %collective-permute-start.2 = (bf16[2,128,4,128]{3,1,2,0:T(8,128)(2,1)}, bf16[2,128,4,128]{3,1,2,0:T(8,128)(2,1)}, u32[]{:S(2)}, u32[]{:S(2)}) collective-permute-start(bf16[2,128,4,128]{3,1,2,0:T(8,128)(2,1)} %slice.457), channel_id=1, source_target_pairs={{0,4},{2,6},{4,8},{6,10},{8,12},{10,14},{12,16},{14,18},{16,20},{1... | collective-permute-start | bytes 786440 | tf_op jit(solution)/shard_map/ppermute | solution.py:13
  122.0 5.4 %copy-start.22 = (bf16[2,64,4,128]{3,1,2,0:T(8,128)(2,1)}, bf16[2,64,4,128]{3,1,2,0:T(8,128)(2,1)S(1)}, u32[]{:S(2)}) copy-start(bf16[2,64,4,128]{3,1,2,0:T(8,128)(2,1)S(1)} %collective-permute-done.6) | copy-start | bytes 393220
  122.0 31.6 %collective-permute-start = (bf16[2,384,4,128]{3,1,2,0:T(8,128)(2,1)}, bf16[2,384,4,128]{3,1,2,0:T(8,128)(2,1)}, u32[]{:S(2)}, u32[]{:S(2)}) collective-permute-start(bf16[2,384,4,128]{3,1,2,0:T(8,128)(2,1)} %get-tuple-element.23), channel_id=1, source_target_pairs={{0,2},{2,4},{4,6},{6,8},{8,10},{10,12},{12,14},{14,16},{16,18},{18... | collective-permute-start | bytes 2359304 | tf_op jit(solution)/shard_map/ppermute | solution.py:13
  126.1 23.6 %collective-permute-start.1 = (bf16[2,384,4,128]{3,1,2,0:T(8,128)(2,1)}, bf16[2,384,4,128]{3,1,2,0:T(8,128)(2,1)}, u32[]{:S(2)}, u32[]{:S(2)}) collective-permute-start(bf16[2,384,4,128]{3,1,2,0:T(8,128)(2,1)} %get-tuple-element.22), channel_id=1, source_target_pairs={{2,0},{4,2},{6,4},{8,6},{10,8},{12,10},{14,12},{16,14},{18,16},{20... | collective-permute-start | bytes 2359304 | tf_op jit(solution)/shard_map/ppermute | solution.py:13
  131.7 38.4 %collective-permute-start.23 = (bf16[387072]{0:T(1024)(128)(2,1)}, bf16[387072]{0:T(1024)(128)(2,1)}, u32[]{:S(2)}, u32[]{:S(2)}) collective-permute-start(bf16[387072]{0:T(1024)(128)(2,1)} %constant_dynamic-update-slice_fusion.51), channel_id=1, source_target_pairs={{0,2},{2,0},{4,6},{6,4},{8,10},{10,8},{12,14},{14,12},{16,18},{18,... | collective-permute-start | bytes 2322440 | tf_op jit(solution)/shard_map/ppermute | solution.py:95
  150.8 20.4 %copy-start.29 = (bf16[2,32,4,128]{3,1,2,0:T(8,128)(2,1)S(1)}, bf16[2,32,4,128]{3,1,2,0:T(8,128)(2,1)}, u32[]{:S(2)}) copy-start(bf16[2,32,4,128]{3,1,2,0:T(8,128)(2,1)} %copy-done.28) | copy-start | bytes 196612
  150.8 20.4 %copy-start.31 = (bf16[2,32,4,128]{3,1,2,0:T(8,128)(2,1)S(1)}, bf16[2,32,4,128]{3,1,2,0:T(8,128)(2,1)}, u32[]{:S(2)}) copy-start(bf16[2,32,4,128]{3,1,2,0:T(8,128)(2,1)} %copy-done.30) | copy-start | bytes 196612
  150.8 20.4 %copy-start.33 = (bf16[2,32,4,128]{3,1,2,0:T(8,128)(2,1)S(1)}, bf16[2,32,4,128]{3,1,2,0:T(8,128)(2,1)}, u32[]{:S(2)}) copy-start(bf16[2,32,4,128]{3,1,2,0:T(8,128)(2,1)} %copy-done.32) | copy-start | bytes 196612
  154.8 17.8 %copy-start.37 = (bf16[2,16,4,128]{3,1,2,0:T(8,128)(2,1)S(1)}, bf16[2,16,4,128]{3,1,2,0:T(8,128)(2,1)}, u32[]{:S(2)}) copy-start(bf16[2,16,4,128]{3,1,2,0:T(8,128)(2,1)} %copy-done.36) | copy-start | bytes 98308
  154.8 17.8 %copy-start.39 = (bf16[2,16,4,128]{3,1,2,0:T(8,128)(2,1)S(1)}, bf16[2,16,4,128]{3,1,2,0:T(8,128)(2,1)}, u32[]{:S(2)}) copy-start(bf16[2,16,4,128]{3,1,2,0:T(8,128)(2,1)} %copy-done.38) | copy-start | bytes 98308
  154.8 17.8 %copy-start.41 = (bf16[2,16,4,128]{3,1,2,0:T(8,128)(2,1)S(1)}, bf16[2,16,4,128]{3,1,2,0:T(8,128)(2,1)}, u32[]{:S(2)}) copy-start(bf16[2,16,4,128]{3,1,2,0:T(8,128)(2,1)} %copy-done.40) | copy-start | bytes 98308
  154.8 18.7 %copy-start.43 = (bf16[2,8,4,128]{3,1,2,0:T(8,128)(2,1)S(1)}, bf16[2,8,4,128]{3,1,2,0:T(8,128)(2,1)}, u32[]{:S(2)}) copy-start(bf16[2,8,4,128]{3,1,2,0:T(8,128)(2,1)} %copy-done.42) | copy-start | bytes 49156
  154.9 18.7 %copy-start.45 = (bf16[2,8,4,128]{3,1,2,0:T(8,128)(2,1)S(1)}, bf16[2,8,4,128]{3,1,2,0:T(8,128)(2,1)}, u32[]{:S(2)}) copy-start(bf16[2,8,4,128]{3,1,2,0:T(8,128)(2,1)} %copy-done.44) | copy-start | bytes 49156
  171.1 4.0 %copy-start.54 = (bf16[2,2,4,128]{3,1,2,0:T(2,128)(2,1)S(1)}, bf16[2,2,4,128]{3,1,2,0:T(2,128)(2,1)}, u32[]{:S(2)}) copy-start(bf16[2,2,4,128]{3,1,2,0:T(2,128)(2,1)} %copy-done.53) | copy-start | bytes 12292
  171.1 4.0 %copy-start.56 = (bf16[2,2,4,128]{3,1,2,0:T(2,128)(2,1)S(1)}, bf16[2,2,4,128]{3,1,2,0:T(2,128)(2,1)}, u32[]{:S(2)}) copy-start(bf16[2,2,4,128]{3,1,2,0:T(2,128)(2,1)} %copy-done.55) | copy-start | bytes 12292
  175.3 36.1 %collective-permute-start.24 = (bf16[380928]{0:T(1024)(128)(2,1)S(1)}, bf16[380928]{0:T(1024)(128)(2,1)S(1)}, u32[]{:S(2)}, u32[]{:S(2)}) collective-permute-start(bf16[380928]{0:T(1024)(128)(2,1)S(1)} %constant_dynamic-update-slice_fusion.44), channel_id=1, source_target_pairs={{0,4},{2,6},{4,0},{6,2},{8,12},{10,14},{12,8},{14,10},{16,20},{18,... | collective-permute-start | bytes 2285576 | tf_op jit(solution)/shard_map/ppermute | solution.py:95
  212.1 39.9 %collective-permute-start.25 = (bf16[368640]{0:T(1024)(128)(2,1)S(1)}, bf16[368640]{0:T(1024)(128)(2,1)S(1)}, u32[]{:S(2)}, u32[]{:S(2)}) collective-permute-start(bf16[368640]{0:T(1024)(128)(2,1)S(1)} %pad_maximum_fusion.6), channel_id=1, source_target_pairs={{0,8},{2,10},{4,12},{6,14},{8,0},{10,2},{12,4},{14,6},{16,24},{18,... | collective-permute-start | bytes 2211848 | tf_op jit(solution)/shard_map/ppermute | solution.py:95
  219.1 36.6 %copy-start.17 = (bf16[3,2,128,4,128]{4,3,2,1,0:T(4,128)(2,1)S(1)}, bf16[3,2,128,4,128]{4,3,2,1,0:T(4,128)(2,1)}, u32[]{:S(2)}) copy-start(bf16[3,2,128,4,128]{4,3,2,1,0:T(4,128)(2,1)} %get-tuple-element.67) | copy-start | bytes 2359300
  219.2 36.6 %copy-start.34 = (bf16[3,2,32,4,128]{4,3,2,1,0:T(4,128)(2,1)S(1)}, bf16[3,2,32,4,128]{4,3,2,1,0:T(4,128)(2,1)}, u32[]{:S(2)}) copy-start(bf16[3,2,32,4,128]{4,3,2,1,0:T(4,128)(2,1)} %get-tuple-element.66) | copy-start | bytes 589828
  219.2 36.6 %copy-start.59 = (bf16[3,2,64,4,128]{4,3,2,1,0:T(4,128)(2,1)S(1)}, bf16[3,2,64,4,128]{4,3,2,1,0:T(4,128)(2,1)}, u32[]{:S(2)}) copy-start(bf16[3,2,64,4,128]{4,3,2,1,0:T(4,128)(2,1)} %get-tuple-element.65) | copy-start | bytes 1179652
  252.7 18.4 %collective-permute-start.26 = (bf16[344064]{0:T(1024)(128)(2,1)S(1)}, bf16[344064]{0:T(1024)(128)(2,1)S(1)}, u32[]{:S(2)}, u32[]{:S(2)}) collective-permute-start(bf16[344064]{0:T(1024)(128)(2,1)S(1)} %pad_maximum_fusion.7), channel_id=1, source_target_pairs={{0,16},{2,18},{4,20},{6,22},{8,24},{10,26},{12,28},{14,30},{16,0},... | collective-permute-start | bytes 2064392 | tf_op jit(solution)/shard_map/ppermute | solution.py:95
  271.5 16.6 %collective-permute-start.27 = (bf16[294912]{0:T(1024)(128)(2,1)S(1)}, bf16[294912]{0:T(1024)(128)(2,1)S(1)}, u32[]{:S(2)}, u32[]{:S(2)}) collective-permute-start(bf16[294912]{0:T(1024)(128)(2,1)S(1)} %pad_maximum_fusion.8), channel_id=1, source_target_pairs={{0,32},{2,34},{4,36},{6,38},{8,40},{10,42},{12,44},{14,46},{16,48}... | collective-permute-start | bytes 1769480 | tf_op jit(solution)/shard_map/ppermute | solution.py:95
  288.3 14.3 %collective-permute-start.28 = (bf16[196608]{0:T(1024)(128)(2,1)S(1)}, bf16[196608]{0:T(1024)(128)(2,1)S(1)}, u32[]{:S(2)}, u32[]{:S(2)}) collective-permute-start(bf16[196608]{0:T(1024)(128)(2,1)S(1)} %bitcast.595), channel_id=1, source_target_pairs={{0,64},{2,66},{4,68},{6,70},{8,72},{10,74},{12,76},{14,78},{16,80}... | collective-permute-start | bytes 1179656 | tf_op jit(solution)/shard_map/ppermute | solution.py:95
  296.5 10.5 %copy-start.4 = (bf16[9,128,4,128]{3,1,2,0:T(8,128)(2,1)S(1)}, bf16[9,128,4,128]{3,1,2,0:T(8,128)(2,1)}, u32[]{:S(2)}) copy-start(bf16[9,128,4,128]{3,1,2,0:T(8,128)(2,1)} %copy.415) | copy-start | bytes 3538948
  296.5 10.5 %copy-start.19 = (bf16[4,128,4,128]{3,1,2,0:T(8,128)(2,1)S(1)}, bf16[4,128,4,128]{3,1,2,0:T(8,128)(2,1)}, u32[]{:S(2)}) copy-start(bf16[4,128,4,128]{3,1,2,0:T(8,128)(2,1)} %copy.414) | copy-start | bytes 1572868
  296.5 10.5 %copy-start.52 = (pred[2,8,3,128]{3,1,2,0:T(8,128)(4,1)S(1)}, pred[2,8,3,128]{3,1,2,0:T(8,128)(4,1)}, u32[]{:S(2)}) copy-start(pred[2,8,3,128]{3,1,2,0:T(8,128)(4,1)} %copy.503) | copy-start | bytes 18436
  303.1 3.9 %copy-start.46 = (bf16[2,13,384,4,128]{4,2,3,1,0:T(8,128)(2,1)}, bf16[2,13,384,4,128]{4,2,3,1,0:T(8,128)(2,1)S(1)}, u32[]{:S(2)}) copy-start(bf16[2,13,384,4,128]{4,2,3,1,0:T(8,128)(2,1)S(1)} %constant_dynamic-update-slice_fusion.36) | copy-start | bytes 30670852
  319.8 3.4 copy-start.3
  325.0 13.8 %slice-start = ((f32[13,128,4,128]{3,1,2,0:T(8,128)}), f32[2,128,4,128]{3,1,2,0:T(8,128)S(1)}, s32[]{:S(2)}) async-start(f32[13,128,4,128]{3,1,2,0:T(8,128)} %copy-done.3), calls=%async_computation | async-start | bytes 1048576 | tf_op jit(solution)/shard_map/slice | solution.py:178
  356.5 7.4 %collective-permute-start.29 = (bf16[512,1024]{1,0:T(8,128)(2,1)}, bf16[512,1024]{1,0:T(8,128)(2,1)S(1)}, u32[]{:S(2)}, u32[]{:S(2)}) collective-permute-start(bf16[512,1024]{1,0:T(8,128)(2,1)} %convolution_convert_fusion), channel_id=1, source_target_pairs={{0,1},{1,0},{2,3},{3,2},{4,5},{5,4},{6,7},{7,6},{8,9},{9,8},{10,11... | collective-permute-start | bytes 3145736 | tf_op jit(solution)/shard_map/ppermute | solution.py:206
  (29 other events, 52.8 us)

commit v2 on v0

--- a/solution.py
+++ b/solution.py
@@ -112,6 +112,15 @@
         block_count * row_count, numerator.shape[2], numerator.shape[3]
     )
     return (peak_rows, numerator_rows, denominator_rows)
+
+
+def third_pairs(count, group):
+    pairs = []
+    for source in range(count):
+        target = source - 3 * group if (source // group) % 2 == 1 else source + 3 * group
+        if 0 <= target < count:
+            pairs.append((source, target))
+    return pairs
 
 
 def upper_half(device_index, bit):
@@ -134,11 +143,7 @@
             theirs = partner[:, offset : offset + width]
             offset = offset + width
             mine = current[level_index]
-            current[level_index] = jnp.where(
-                upper,
-                jnp.concatenate([theirs, mine], axis=1),
-                jnp.concatenate([mine, theirs], axis=1),
-            )
+            current[level_index] = jnp.concatenate([mine, theirs], axis=1)
     return current
 
 
@@ -212,8 +217,7 @@
         before_two = shifted(whole_block, "seq", 2 * group)
         after_two = shifted(whole_block, "seq", -2 * group)
         block_index = device_index // group
-        outgoing = jnp.where(block_index % 2 == 0, before_two, after_two)
-        third_block = partner_2(outgoing, "seq", level_index - 2)
+        third_block = lax.ppermute(whole_block, "seq", third_pairs(seq_count, group))
         level_keys = jnp.concatenate([before_two, after_two, third_block], axis=1)[:, None]
         valid = slot_masks(jnp.reshape(block_index, (1,)), seq_count // group, level_index, BLOCK)
         results.append(
@@ -280,8 +284,15 @@
     attended = (weighted / total_weight[:, :, None]).astype(jnp.bfloat16)
     flattened = attended.reshape(token_count, head_local * head_size)
     weight_flat = out_weight.reshape(head_local * head_size, out_weight.shape[2])
-    partial_value = jnp.dot(flattened, weight_flat, preferred_element_type=jnp.float32)
-    return summed_on_arrival(partial_value.astype(jnp.bfloat16), "head", 1).astype(jnp.bfloat16)
+    half = weight_flat.shape[1] // 2
+    core = lax.axis_index("head")
+    other_weight = lax.dynamic_slice_in_dim(weight_flat, (1 - core) * half, half, axis=1)
+    mine_weight = lax.dynamic_slice_in_dim(weight_flat, core * half, half, axis=1)
+    other_part = jnp.dot(flattened, other_weight, preferred_element_type=jnp.float32)
+    received = lax.ppermute(other_part.astype(jnp.bfloat16), "head", [(0, 1), (1, 0)])
+    mine_part = jnp.dot(flattened, mine_weight, preferred_element_type=jnp.float32)
+    total = mine_part.astype(jnp.bfloat16).astype(jnp.float32) + received.astype(jnp.float32)
+    return total.astype(jnp.bfloat16)
 
 
 def solution(mesh):

time: 290 us -> 306 us (1.055)
  the two profiles are of different devices: /device:TPU:193 before, /device:TPU:223 now
where the time goes in v2:
time: 306 us; the launch traced here: 303 us
  starting transfers between devices  101 us (33%)
  local copies, waits for them, and re-layouts  92.1 us (30%)
  other arithmetic  54.6 us (18%)
  waiting for transfers between devices  25.8 us (8%)
  between operations  16 us (5%)
  matrix products  13 us (4%)
    ppermute x10, starting transfers between devices, shifted(): lax.ppermute(value, axis, [(source, source + steps) for source in range(i...  50.3 us
    ppermute x4, starting transfers between devices, partner_2(): return lax.ppermute(value, axis, pairs)  25.3 us
    reduce_sum x24, other arithmetic, coarsen(): summed = jnp.sum(grouped, axis=1)  16.9 us
    unnamed x175, local copies, waits for them, and re-layouts  15.2 us
    ppermute x10, waiting for transfers between devices, shifted(): lax.ppermute(value, axis, [(source, source + steps) for source in range(i...  14.7 us
    ppermute x5, starting transfers between devices, per_device(): lax.ppermute(whole_block, 'seq', third_pairs(seq_count, group))  10.7 us
    slice x9, local copies, waits for them, and re-layouts, assemble_joint(): theirs = partner[:, offset:offset + width]  10.6 us
    exp x9, local copies, waits for them, and re-layouts, per_device(): level_factor = jnp.exp(part_peak - overall)  10.5 us
  transfers between devices with their start and end apart: 25, of which 5 were waited for; matrix products, arithmetic and copies ran while one was open for 33% of the time, Pallas kernels for 0%

profile of v2, /device:TPU:223, one launch (start us, length us, event | category | flops | bytes accessed | tf_op | source)
XLA Modules:
  0.0 302.9 jit_solution(2348394129216550789)
XLA Ops:
  6.5 1.6 bitcast_reduce_fusion.19
  8.2 1.4 bitcast_reduce_fusion.20
  10.4 1.9 collective-permute-start.6
  12.3 6.1 %collective-permute-start.5 = (bf16[2,128,4,128]{3,1,2,0:T(8,128)(2,1)}, bf16[2,128,4,128]{3,1,2,0:T(8,128)(2,1)}, u32[]{:S(2)}, u32[]{:S(2)}) collective-permute-start(bf16[2,128,4,128]{3,1,2,0:T(8,128)(2,1)} %pad_maximum_fusion.8), channel_id=1, source_target_pairs={{4,0},{6,2},{8,4},{10,6},{12,8},{14,10},{16,12},{18,14},{20,16},{2... | collective-permute-start | bytes 786440 | tf_op jit(solution)/shard_map/ppermute | solution.py:31
  18.4 1.9 collective-permute-start.4
  24.7 5.1 %collective-permute-start.7 = (bf16[2,120,4,128]{3,1,2,0:T(8,128)(2,1)}, bf16[2,120,4,128]{3,1,2,0:T(8,128)(2,1)}, u32[]{:S(2)}, u32[]{:S(2)}) collective-permute-start(bf16[2,120,4,128]{3,1,2,0:T(8,128)(2,1)} %maximum_maximum_fusion.1), channel_id=1, source_target_pairs={{0,2},{2,0},{4,6},{6,4},{8,10},{10,8},{12,14},{14,12},{16,18},{18,... | collective-permute-start | bytes 737288 | tf_op jit(solution)/shard_map/ppermute | solution.py:12
  32.7 1.9 collective-permute-start.3
  37.2 1.9 bitcast_reduce_fusion.1
  39.1 1.8 bitcast_reduce_fusion.6
  40.9 1.9 bitcast_reduce_fusion.7
  52.6 2.0 pad_maximum_fusion.7
  60.6 4.7 %collective-permute-start.2 = (bf16[2,256,4,128]{3,2,1,0:T(4,128)(2,1)}, bf16[2,256,4,128]{3,2,1,0:T(4,128)(2,1)}, u32[]{:S(2)}, u32[]{:S(2)}) collective-permute-start(bf16[2,256,4,128]{3,2,1,0:T(4,128)(2,1)} %pad_maximum_fusion.5), channel_id=1, source_target_pairs={{0,2},{2,4},{4,6},{6,8},{8,10},{10,12},{12,14},{14,16},{16,18},{18... | collective-permute-start | bytes 1572872 | tf_op jit(solution)/shard_map/ppermute | solution.py:22
  65.3 1.5 fusion.138
  67.5 1.4 fusion.139
  69.6 1.4 fusion.140
  72.6 1.9 collective-permute-start
  75.5 3.4 %collective-permute-start.1 = (bf16[2,128,4,128]{3,1,2,0:T(8,128)(2,1)}, bf16[2,128,4,128]{3,1,2,0:T(8,128)(2,1)}, u32[]{:S(2)}, u32[]{:S(2)}) collective-permute-start(bf16[2,128,4,128]{3,1,2,0:T(8,128)(2,1)} %get-tuple-element.31), channel_id=1, source_target_pairs={{2,0},{4,2},{6,4},{8,6},{10,8},{12,10},{14,12},{16,14},{18,16},{20... | collective-permute-start | bytes 786440 | tf_op jit(solution)/shard_map/ppermute | solution.py:23
  79.9 2.8 collective-permute-start.10
  85.6 1.8 copy.289
  88.2 1.7 reshape.1235
  90.8 1.7 reshape.1308
  92.5 4.9 %collective-permute-start.9 = (bf16[2,128,4,128]{3,1,2,0:T(8,128)(2,1)}, bf16[2,128,4,128]{3,1,2,0:T(8,128)(2,1)}, u32[]{:S(2)}, u32[]{:S(2)}) collective-permute-start(bf16[2,128,4,128]{3,1,2,0:T(8,128)(2,1)} %pad_maximum_fusion.9), channel_id=1, source_target_pairs={{8,0},{10,2},{12,4},{14,6},{16,8},{18,10},{20,12},{22,14},{24,16},... | collective-permute-start | bytes 786440 | tf_op jit(solution)/shard_map/ppermute | solution.py:31
  97.5 10.5 %collective-permute-start.11 = (bf16[2,112,4,128]{3,1,2,0:T(8,128)(2,1)}, bf16[2,112,4,128]{3,1,2,0:T(8,128)(2,1)}, u32[]{:S(2)}, u32[]{:S(2)}) collective-permute-start(bf16[2,112,4,128]{3,1,2,0:T(8,128)(2,1)} %get-tuple-element.38), channel_id=1, source_target_pairs={{0,4},{2,6},{4,0},{6,2},{8,12},{10,14},{12,8},{14,10},{16,20},{18,... | collective-permute-start | bytes 688136 | tf_op jit(solution)/shard_map/ppermute | solution.py:12
  112.2 1.7 copy-done.9
  113.9 1.5 fusion.12
  116.8 2.9 fusion.1
  119.7 8.4 %collective-permute-done.11 = bf16[2,112,4,128]{3,1,2,0:T(8,128)(2,1)} collective-permute-done((bf16[2,112,4,128]{3,1,2,0:T(8,128)(2,1)}, bf16[2,112,4,128]{3,1,2,0:T(8,128)(2,1)}, u32[]{:S(2)}, u32[]{:S(2)}) %collective-permute-start.11) | collective-permute-done | bytes 229408 | tf_op jit(solution)/shard_map/ppermute | solution.py:12
  128.2 1.9 collective-permute-start.8
  130.1 1.5 fusion.141
  133.6 1.4 fusion.142
  136.6 9.8 %collective-permute-done.8 = bf16[2,128,4,128]{3,1,2,0:T(8,128)(2,1)S(1)} collective-permute-done((bf16[2,128,4,128]{3,1,2,0:T(8,128)(2,1)}, bf16[2,128,4,128]{3,1,2,0:T(8,128)(2,1)S(1)}, u32[]{:S(2)}, u32[]{:S(2)}) %collective-permute-start.8) | collective-permute-done | bytes 262176 | tf_op jit(solution)/shard_map/ppermute | solution.py:31
  146.5 2.1 collective-permute-start.14
  148.6 6.5 %collective-permute-start.13 = (bf16[2,128,4,128]{3,1,2,0:T(8,128)(2,1)}, bf16[2,128,4,128]{3,1,2,0:T(8,128)(2,1)}, u32[]{:S(2)}, u32[]{:S(2)}) collective-permute-start(bf16[2,128,4,128]{3,1,2,0:T(8,128)(2,1)} %pad_maximum_fusion.10), channel_id=1, source_target_pairs={{16,0},{18,2},{20,4},{22,6},{24,8},{26,10},{28,12},{30,14},{32,16}... | collective-permute-start | bytes 786440 | tf_op jit(solution)/shard_map/ppermute | solution.py:31
  156.1 5.9 %collective-permute-start.12 = (bf16[2,128,4,128]{3,1,2,0:T(8,128)(2,1)}, bf16[2,128,4,128]{3,1,2,0:T(8,128)(2,1)}, u32[]{:S(2)}, u32[]{:S(2)}) collective-permute-start(bf16[2,128,4,128]{3,1,2,0:T(8,128)(2,1)} %pad_maximum_fusion.10), channel_id=1, source_target_pairs={{0,16},{2,18},{4,20},{6,22},{8,24},{10,26},{12,28},{14,30},{16,32}... | collective-permute-start | bytes 786440 | tf_op jit(solution)/shard_map/ppermute | solution.py:31
  165.7 3.0 collective-permute-start.15
  168.7 7.8 %pad_maximum_fusion.2 = bf16[2,768,4,128]{3,2,1,0:T(4,128)(2,1)S(1)} fusion(bf16[2,256,4,128]{3,2,1,0:T(4,128)(2,1)} %collective-permute-done.3, bf16[1,256,4,128]{3,2,1,0:T(4,128)(2,1)S(1)} %bitcast.590, bf16[1,256,4,128]{3,2,1,0:T(4,128)(2,1)S(1)} %copy-done.11, bf16[2,256,4,128]{3,2,1,0:T(4,128)(2,1)} %collective-permute-done.2), kind=kLoop, calls=%fused_computation.10 | loop fusion | flops 2359296 | bytes 3145728 | tf_op jit(solution)/shard_map/concatenate | solution.py:24
  180.8 1.9 fusion.10
  185.2 1.9 collective-permute-start.18
  187.1 1.9 collective-permute-start.17
  189.1 1.5 fusion.143
  190.6 8.5 %collective-permute-start.16 = (bf16[2,128,4,128]{3,1,2,0:T(8,128)(2,1)S(1)}, bf16[2,128,4,128]{3,1,2,0:T(8,128)(2,1)S(1)}, u32[]{:S(2)}, u32[]{:S(2)}) collective-permute-start(bf16[2,128,4,128]{3,1,2,0:T(8,128)(2,1)S(1)} %pad_maximum_fusion.11), channel_id=1, source_target_pairs={{0,32},{2,34},{4,36},{6,38},{8,40},{10,42},{12,44},{14,46},{16,48}... | collective-permute-start | bytes 786440 | tf_op jit(solution)/shard_map/ppermute | solution.py:31
  200.1 6.6 %collective-permute-start.19 = (bf16[2,64,4,128]{3,1,2,0:T(8,128)(2,1)S(1)}, bf16[2,64,4,128]{3,1,2,0:T(8,128)(2,1)}, u32[]{:S(2)}, u32[]{:S(2)}) collective-permute-start(bf16[2,64,4,128]{3,1,2,0:T(8,128)(2,1)S(1)} %pad_maximum_fusion.12), channel_id=1, source_target_pairs={{0,16},{2,18},{4,20},{6,22},{8,24},{10,26},{12,28},{14,30},{16,0},... | collective-permute-start | bytes 393224 | tf_op jit(solution)/shard_map/ppermute | solution.py:12
  210.6 1.6 constant_dynamic-update-slice_fusion.24
  212.2 1.9 collective-permute-start.22
  214.1 1.9 collective-permute-start.21
  216.0 10.8 %collective-permute-start.20 = (bf16[2,128,4,128]{3,1,2,0:T(8,128)(2,1)}, bf16[2,128,4,128]{3,1,2,0:T(8,128)(2,1)}, u32[]{:S(2)}, u32[]{:S(2)}) collective-permute-start(bf16[2,128,4,128]{3,1,2,0:T(8,128)(2,1)} %constant_dynamic-update-slice_fusion.24), channel_id=1, source_target_pairs={{0,64},{2,66},{4,68},{6,70},{8,72},{10,74},{12,76},{14,78},{16,80}... | collective-permute-start | bytes 786440 | tf_op jit(solution)/shard_map/ppermute | solution.py:31
  228.7 3.1 %collective-permute-done.20 = bf16[2,128,4,128]{3,1,2,0:T(8,128)(2,1)} collective-permute-done((bf16[2,128,4,128]{3,1,2,0:T(8,128)(2,1)}, bf16[2,128,4,128]{3,1,2,0:T(8,128)(2,1)}, u32[]{:S(2)}, u32[]{:S(2)}) %collective-permute-start.20) | collective-permute-done | bytes 262176 | tf_op jit(solution)/shard_map/ppermute | solution.py:31
  232.7 1.8 collective-permute-done.21
  237.6 5.7 %reshape.1322 = bf16[256,6144]{1,0:T(8,128)(2,1)} reshape(bf16[1572864]{0:T(1024)(128)(2,1)} %all-gather.3.cloned.1.call-done) | data formatting | bytes 6291456 | tf_op jit(solution)/shard_map/all_gather | solution.py:42
  243.3 3.2 %slice.189 = bf16[256,4096]{1,0:T(8,128)(2,1)} slice(bf16[256,6144]{1,0:T(8,128)(2,1)} %reshape.1322), slice={[0:256], [0:4096]} | slice | bytes 4194304 | tf_op jit(solution)/shard_map/slice | solution.py:44
  247.8 2.5 copy.275
  251.8 4.1 %copy.269 = bf16[256,4096]{0,1:T(8,128)(2,1)} copy(bf16[256,4096]{1,0:T(8,128)(2,1)} %slice.189) | data formatting | bytes 4194304 | tf_op jit(solution)/shard_map/slice | solution.py:44
  255.9 4.2 %copy.270 = bf16[2,256,4,4,128]{4,2,1,3,0:T(4,128)(2,1)} copy(bf16[2,256,4,4,128]{1,4,3,2,0:T(8,128)(2,1)} %bitcast.565) | data formatting | bytes 4194304 | tf_op jit(solution)/shard_map/transpose | solution.py:35
  266.0 1.5 copy.292
  267.5 1.6 copy.294
  269.1 1.6 copy.296
  270.6 1.5 copy.300
  272.2 1.5 copy.279
  273.7 1.6 copy.298
  284.0 1.5 fusion.22
  285.5 1.7 convolution_convert_fusion
  287.2 3.2 %collective-permute-start.23 = (bf16[512,1024]{1,0:T(8,128)(2,1)}, bf16[512,1024]{1,0:T(8,128)(2,1)}, u32[]{:S(2)}, u32[]{:S(2)}) collective-permute-start(bf16[512,1024]{1,0:T(8,128)(2,1)} %convolution_convert_fusion), channel_id=1, source_target_pairs={{0,1},{1,0},{2,3},{3,2},{4,5},{5,4},{6,7},{7,6},{8,9},{9,8},{10,11... | collective-permute-start | bytes 3145736 | tf_op jit(solution)/shard_map/ppermute | solution.py:292
  290.5 2.6 collective-permute-done.23
  293.1 2.9 add_convert_fusion
  (420 shorter events, 82.7 us)
Async XLA Ops:
  6.5 279.0 %copy-start = (bf16[4,128,2048]{2,1,0:T(8,128)(2,1)S(1)}, bf16[4,128,2048]{2,1,0:T(8,128)(2,1)}, u32[]{:S(2)}) copy-start(bf16[4,128,2048]{2,1,0:T(8,128)(2,1)} %param.7) | copy-start | bytes 6291460
  6.5 13.8 %copy-start.1 = (bf16[512,4,128]{2,1,0:T(4,128)(2,1)S(1)}, bf16[512,4,128]{2,1,0:T(4,128)(2,1)}, u32[]{:S(2)}) copy-start(bf16[512,4,128]{2,1,0:T(4,128)(2,1)} %param.6) | copy-start | bytes 1572868
  6.5 14.1 %copy-start.2 = (bf16[512,4,128]{2,1,0:T(4,128)(2,1)S(1)}, bf16[512,4,128]{2,1,0:T(4,128)(2,1)}, u32[]{:S(2)}) copy-start(bf16[512,4,128]{2,1,0:T(4,128)(2,1)} %param.5) | copy-start | bytes 1572868
  6.5 231.1 %all-gather.3.cloned.1.call-start = ((), (), s32[]{:S(2)}) async-start(), calls=%async_computation | async-start | bytes 3158016 | tf_op jit(solution)/shard_map/all_gather | solution.py:42
  10.4 69.5 %collective-permute-start.6 = (bf16[2,128,4,128]{3,1,2,0:T(8,128)(2,1)}, bf16[2,128,4,128]{3,1,2,0:T(8,128)(2,1)}, u32[]{:S(2)}, u32[]{:S(2)}) collective-permute-start(bf16[2,128,4,128]{3,1,2,0:T(8,128)(2,1)} %pad_maximum_fusion.8), channel_id=1, source_target_pairs={{0,6},{4,10},{6,0},{8,14},{10,4},{12,18},{14,8},{16,22},{18,12},{2... | collective-permute-start | bytes 786440 | tf_op jit(solution)/shard_map/ppermute | solution.py:220
  12.3 63.2 %collective-permute-start.5 = (bf16[2,128,4,128]{3,1,2,0:T(8,128)(2,1)}, bf16[2,128,4,128]{3,1,2,0:T(8,128)(2,1)}, u32[]{:S(2)}, u32[]{:S(2)}) collective-permute-start(bf16[2,128,4,128]{3,1,2,0:T(8,128)(2,1)} %pad_maximum_fusion.8), channel_id=1, source_target_pairs={{4,0},{6,2},{8,4},{10,6},{12,8},{14,10},{16,12},{18,14},{20,16},{2... | collective-permute-start | bytes 786440 | tf_op jit(solution)/shard_map/ppermute | solution.py:31
  18.4 54.2 %collective-permute-start.4 = (bf16[2,128,4,128]{3,1,2,0:T(8,128)(2,1)}, bf16[2,128,4,128]{3,1,2,0:T(8,128)(2,1)}, u32[]{:S(2)}, u32[]{:S(2)}) collective-permute-start(bf16[2,128,4,128]{3,1,2,0:T(8,128)(2,1)} %pad_maximum_fusion.8), channel_id=1, source_target_pairs={{0,4},{2,6},{4,8},{6,10},{8,12},{10,14},{12,16},{14,18},{16,20},{1... | collective-permute-start | bytes 786440 | tf_op jit(solution)/shard_map/ppermute | solution.py:31
  24.7 35.9 %collective-permute-start.7 = (bf16[2,120,4,128]{3,1,2,0:T(8,128)(2,1)}, bf16[2,120,4,128]{3,1,2,0:T(8,128)(2,1)}, u32[]{:S(2)}, u32[]{:S(2)}) collective-permute-start(bf16[2,120,4,128]{3,1,2,0:T(8,128)(2,1)} %maximum_maximum_fusion.1), channel_id=1, source_target_pairs={{0,2},{2,0},{4,6},{6,4},{8,10},{10,8},{12,14},{14,12},{16,18},{18,... | collective-permute-start | bytes 737288 | tf_op jit(solution)/shard_map/ppermute | solution.py:12
  32.7 133.0 %collective-permute-start.3 = (bf16[2,256,4,128]{3,2,1,0:T(4,128)(2,1)}, bf16[2,256,4,128]{3,2,1,0:T(4,128)(2,1)}, u32[]{:S(2)}, u32[]{:S(2)}) collective-permute-start(bf16[2,256,4,128]{3,2,1,0:T(4,128)(2,1)} %pad_maximum_fusion.5), channel_id=1, source_target_pairs={{2,0},{4,2},{6,4},{8,6},{10,8},{12,10},{14,12},{16,14},{18,16},{20... | collective-permute-start | bytes 1572872 | tf_op jit(solution)/shard_map/ppermute | solution.py:23
  34.9 7.9 %copy-start.3 = (bf16[512,4,128]{2,1,0:T(4,128)(2,1)S(1)}, bf16[512,4,128]{2,1,0:T(4,128)(2,1)}, u32[]{:S(2)}) copy-start(bf16[512,4,128]{2,1,0:T(4,128)(2,1)} %param.4) | copy-start | bytes 1572868
  37.2 8.2 %copy-start.24 = (bf16[1,32,4,128]{3,1,2,0:T(8,128)(2,1)S(1)}, bf16[1,32,4,128]{3,1,2,0:T(8,128)(2,1)}, u32[]{:S(2)}) copy-start(bf16[1,32,4,128]{3,1,2,0:T(8,128)(2,1)} %copy-done.23) | copy-start | bytes 98308
  37.2 8.2 %copy-start.27 = (bf16[32,4,128]{2,0,1:T(8,128)(2,1)S(1)}, bf16[32,4,128]{2,0,1:T(8,128)(2,1)}, u32[]{:S(2)}) copy-start(bf16[32,4,128]{2,0,1:T(8,128)(2,1)} %copy-done.26) | copy-start | bytes 98308
  49.3 5.3 %copy-start.78 = (pred[2]{0:T(512)(128)(4,1)S(1)}, pred[2]{0:T(512)(128)(4,1)}, u32[]{:S(2)}) copy-start(pred[2]{0:T(512)(128)(4,1)} %compare_and_fusion.2) | copy-start | bytes 10
  49.3 5.4 %copy-start.76 = (pred[2]{0:T(512)(128)(4,1)S(1)}, pred[2]{0:T(512)(128)(4,1)}, u32[]{:S(2)}) copy-start(pred[2]{0:T(512)(128)(4,1)} %get-tuple-element.71) | copy-start | bytes 10
  49.3 5.5 %copy-start.75 = (pred[2]{0:T(512)(128)(4,1)S(1)}, pred[2]{0:T(512)(128)(4,1)}, u32[]{:S(2)}) copy-start(pred[2]{0:T(512)(128)(4,1)} %get-tuple-element.72) | copy-start | bytes 10
  49.3 6.2 %copy-start.77 = (pred[4]{0:T(512)(128)(4,1)S(1)}, pred[4]{0:T(512)(128)(4,1)}, u32[]{:S(2)}) copy-start(pred[4]{0:T(512)(128)(4,1)} %compare_and_fusion.5) | copy-start | bytes 16
  49.3 6.2 %copy-start.74 = (pred[4]{0:T(512)(128)(4,1)S(1)}, pred[4]{0:T(512)(128)(4,1)}, u32[]{:S(2)}) copy-start(pred[4]{0:T(512)(128)(4,1)} %get-tuple-element.73) | copy-start | bytes 16
  49.3 6.3 %copy-start.73 = (pred[4]{0:T(512)(128)(4,1)S(1)}, pred[4]{0:T(512)(128)(4,1)}, u32[]{:S(2)}) copy-start(pred[4]{0:T(512)(128)(4,1)} %get-tuple-element.74) | copy-start | bytes 16
  49.3 10.5 %copy-start.13 = (f32[256,4,128]{2,1,0:T(4,128)S(1)}, f32[256,4,128]{2,1,0:T(4,128)}, u32[]{:S(2)}) copy-start(f32[256,4,128]{2,1,0:T(4,128)} %bitcast_reduce_fusion.24) | copy-start | bytes 1572868
  49.3 17.5 %copy-start.32 = (bf16[16,4,128]{2,0,1:T(8,128)(2,1)S(1)}, bf16[16,4,128]{2,0,1:T(8,128)(2,1)}, u32[]{:S(2)}) copy-start(bf16[16,4,128]{2,0,1:T(8,128)(2,1)} %copy-done.31) | copy-start | bytes 49156
  49.3 19.6 %copy-start.37 = (bf16[8,4,128]{2,0,1:T(8,128)(2,1)S(1)}, bf16[8,4,128]{2,0,1:T(8,128)(2,1)}, u32[]{:S(2)}) copy-start(bf16[8,4,128]{2,0,1:T(8,128)(2,1)} %copy-done.36) | copy-start | bytes 24580
  49.3 19.6 %copy-start.41 = (bf16[1,8,4,128]{3,1,2,0:T(8,128)(2,1)S(1)}, bf16[1,8,4,128]{3,1,2,0:T(8,128)(2,1)}, u32[]{:S(2)}) copy-start(bf16[1,8,4,128]{3,1,2,0:T(8,128)(2,1)} %copy-done.40) | copy-start | bytes 24580
  60.6 23.1 %copy-start.21 = (f32[128,4,128]{2,1,0:T(4,128)S(1)}, f32[128,4,128]{2,1,0:T(4,128)}, u32[]{:S(2)}) copy-start(f32[128,4,128]{2,1,0:T(4,128)} %bitcast_reduce_fusion.21) | copy-start | bytes 786436
  60.6 108.1 %collective-permute-start.2 = (bf16[2,256,4,128]{3,2,1,0:T(4,128)(2,1)}, bf16[2,256,4,128]{3,2,1,0:T(4,128)(2,1)}, u32[]{:S(2)}, u32[]{:S(2)}) collective-permute-start(bf16[2,256,4,128]{3,2,1,0:T(4,128)(2,1)} %pad_maximum_fusion.5), channel_id=1, source_target_pairs={{0,2},{2,4},{4,6},{6,8},{8,10},{10,12},{12,14},{14,16},{16,18},{18... | collective-permute-start | bytes 1572872 | tf_op jit(solution)/shard_map/ppermute | solution.py:22
  68.9 15.2 %copy-start.63 = (bf16[2,96,4,128]{3,1,2,0:T(8,128)(2,1)}, bf16[2,96,4,128]{3,1,2,0:T(8,128)(2,1)S(1)}, u32[]{:S(2)}) copy-start(bf16[2,96,4,128]{3,1,2,0:T(8,128)(2,1)S(1)} %get-tuple-element.36) | copy-start | bytes 589828
  72.6 19.9 %collective-permute-start = (bf16[2,128,4,128]{3,1,2,0:T(8,128)(2,1)}, bf16[2,128,4,128]{3,1,2,0:T(8,128)(2,1)}, u32[]{:S(2)}, u32[]{:S(2)}) collective-permute-start(bf16[2,128,4,128]{3,1,2,0:T(8,128)(2,1)} %get-tuple-element.30), channel_id=1, source_target_pairs={{0,2},{2,4},{4,6},{6,8},{8,10},{10,12},{12,14},{14,16},{16,18},{18... | collective-permute-start | bytes 786440 | tf_op jit(solution)/shard_map/ppermute | solution.py:22
  75.5 22.0 %collective-permute-start.1 = (bf16[2,128,4,128]{3,1,2,0:T(8,128)(2,1)}, bf16[2,128,4,128]{3,1,2,0:T(8,128)(2,1)}, u32[]{:S(2)}, u32[]{:S(2)}) collective-permute-start(bf16[2,128,4,128]{3,1,2,0:T(8,128)(2,1)} %get-tuple-element.31), channel_id=1, source_target_pairs={{2,0},{4,2},{6,4},{8,6},{10,8},{12,10},{14,12},{16,14},{18,16},{20... | collective-permute-start | bytes 786440 | tf_op jit(solution)/shard_map/ppermute | solution.py:23
  79.9 76.3 %collective-permute-start.10 = (bf16[2,128,4,128]{3,1,2,0:T(8,128)(2,1)}, bf16[2,128,4,128]{3,1,2,0:T(8,128)(2,1)}, u32[]{:S(2)}, u32[]{:S(2)}) collective-permute-start(bf16[2,128,4,128]{3,1,2,0:T(8,128)(2,1)} %pad_maximum_fusion.9), channel_id=1, source_target_pairs={{0,12},{2,14},{8,20},{10,22},{12,0},{14,2},{16,28},{18,30},{20,8},... | collective-permute-start | bytes 786440 | tf_op jit(solution)/shard_map/ppermute | solution.py:220
  84.1 23.9 %copy-start.6 = (bf16[1,512,4,128]{3,1,2,0:T(8,128)(2,1)S(1)}, bf16[1,512,4,128]{3,1,2,0:T(8,128)(2,1)}, u32[]{:S(2)}) copy-start(bf16[1,512,4,128]{3,1,2,0:T(8,128)(2,1)} %get-tuple-element.69) | copy-start | bytes 1572868
  84.1 23.9 %copy-start.7 = (bf16[1,512,4,128]{3,1,2,0:T(8,128)(2,1)S(1)}, bf16[1,512,4,128]{3,1,2,0:T(8,128)(2,1)}, u32[]{:S(2)}) copy-start(bf16[1,512,4,128]{3,1,2,0:T(8,128)(2,1)} %get-tuple-element.70) | copy-start | bytes 1572868
  92.5 56.1 %collective-permute-start.9 = (bf16[2,128,4,128]{3,1,2,0:T(8,128)(2,1)}, bf16[2,128,4,128]{3,1,2,0:T(8,128)(2,1)}, u32[]{:S(2)}, u32[]{:S(2)}) collective-permute-start(bf16[2,128,4,128]{3,1,2,0:T(8,128)(2,1)} %pad_maximum_fusion.9), channel_id=1, source_target_pairs={{8,0},{10,2},{12,4},{14,6},{16,8},{18,10},{20,12},{22,14},{24,16},... | collective-permute-start | bytes 786440 | tf_op jit(solution)/shard_map/ppermute | solution.py:31
  97.5 30.7 %collective-permute-start.11 = (bf16[2,112,4,128]{3,1,2,0:T(8,128)(2,1)}, bf16[2,112,4,128]{3,1,2,0:T(8,128)(2,1)}, u32[]{:S(2)}, u32[]{:S(2)}) collective-permute-start(bf16[2,112,4,128]{3,1,2,0:T(8,128)(2,1)} %get-tuple-element.38), channel_id=1, source_target_pairs={{0,4},{2,6},{4,0},{6,2},{8,12},{10,14},{12,8},{14,10},{16,20},{18,... | collective-permute-start | bytes 688136 | tf_op jit(solution)/shard_map/ppermute | solution.py:12
  116.8 14.9 %copy-start.38 = (bf16[8,4,128]{2,0,1:T(8,128)(2,1)S(1)}, bf16[8,4,128]{2,0,1:T(8,128)(2,1)}, u32[]{:S(2)}) copy-start(bf16[8,4,128]{2,0,1:T(8,128)(2,1)} %copy-done.36) | copy-start | bytes 24580
  116.8 14.9 %copy-start.42 = (bf16[1,8,4,128]{3,1,2,0:T(8,128)(2,1)S(1)}, bf16[1,8,4,128]{3,1,2,0:T(8,128)(2,1)}, u32[]{:S(2)}) copy-start(bf16[1,8,4,128]{3,1,2,0:T(8,128)(2,1)} %copy-done.40) | copy-start | bytes 24580
  116.8 19.1 %copy-start.25 = (bf16[1,32,4,128]{3,1,2,0:T(8,128)(2,1)S(1)}, bf16[1,32,4,128]{3,1,2,0:T(8,128)(2,1)}, u32[]{:S(2)}) copy-start(bf16[1,32,4,128]{3,1,2,0:T(8,128)(2,1)} %copy-done.23) | copy-start | bytes 98308
  116.8 19.1 %copy-start.28 = (bf16[32,4,128]{2,0,1:T(8,128)(2,1)S(1)}, bf16[32,4,128]{2,0,1:T(8,128)(2,1)}, u32[]{:S(2)}) copy-start(bf16[32,4,128]{2,0,1:T(8,128)(2,1)} %copy-done.26) | copy-start | bytes 98308
  116.8 19.1 %copy-start.34 = (bf16[2,32,4,128]{3,1,2,0:T(8,128)(2,1)S(1)}, bf16[2,32,4,128]{3,1,2,0:T(8,128)(2,1)}, u32[]{:S(2)}) copy-start(bf16[2,32,4,128]{3,1,2,0:T(8,128)(2,1)} %get-tuple-element.32) | copy-start | bytes 196612
  119.7 43.3 %copy-start.22 = (f32[64,4,128]{2,1,0:T(4,128)S(1)}, f32[64,4,128]{2,1,0:T(4,128)}, u32[]{:S(2)}) copy-start(f32[64,4,128]{2,1,0:T(4,128)} %bitcast_reduce_fusion.18) | copy-start | bytes 393220
  119.7 43.3 %copy-start.66 = (pred[384]{0:T(512)(128)(4,1)S(1)}, pred[384]{0:T(512)(128)(4,1)}, u32[]{:S(2)}) copy-start(pred[384]{0:T(512)(128)(4,1)} %fusion.117) | copy-start | bytes 1156
  128.2 18.3 %collective-permute-start.8 = (bf16[2,128,4,128]{3,1,2,0:T(8,128)(2,1)}, bf16[2,128,4,128]{3,1,2,0:T(8,128)(2,1)S(1)}, u32[]{:S(2)}, u32[]{:S(2)}) collective-permute-start(bf16[2,128,4,128]{3,1,2,0:T(8,128)(2,1)} %pad_maximum_fusion.9), channel_id=1, source_target_pairs={{0,8},{2,10},{4,12},{6,14},{8,16},{10,18},{12,20},{14,22},{16,24},... | collective-permute-start | bytes 786440 | tf_op jit(solution)/shard_map/ppermute | solution.py:31
  146.5 61.3 %collective-permute-start.14 = (bf16[2,128,4,128]{3,1,2,0:T(8,128)(2,1)}, bf16[2,128,4,128]{3,1,2,0:T(8,128)(2,1)}, u32[]{:S(2)}, u32[]{:S(2)}) collective-permute-start(bf16[2,128,4,128]{3,1,2,0:T(8,128)(2,1)} %pad_maximum_fusion.10), channel_id=1, source_target_pairs={{0,24},{2,26},{4,28},{6,30},{16,40},{18,42},{20,44},{22,46},{24,0}... | collective-permute-start | bytes 786440 | tf_op jit(solution)/shard_map/ppermute | solution.py:220
  148.6 51.5 %collective-permute-start.13 = (bf16[2,128,4,128]{3,1,2,0:T(8,128)(2,1)}, bf16[2,128,4,128]{3,1,2,0:T(8,128)(2,1)}, u32[]{:S(2)}, u32[]{:S(2)}) collective-permute-start(bf16[2,128,4,128]{3,1,2,0:T(8,128)(2,1)} %pad_maximum_fusion.10), channel_id=1, source_target_pairs={{16,0},{18,2},{20,4},{22,6},{24,8},{26,10},{28,12},{30,14},{32,16}... | collective-permute-start | bytes 786440 | tf_op jit(solution)/shard_map/ppermute | solution.py:31
  156.1 34.4 %collective-permute-start.12 = (bf16[2,128,4,128]{3,1,2,0:T(8,128)(2,1)}, bf16[2,128,4,128]{3,1,2,0:T(8,128)(2,1)}, u32[]{:S(2)}, u32[]{:S(2)}) collective-permute-start(bf16[2,128,4,128]{3,1,2,0:T(8,128)(2,1)} %pad_maximum_fusion.10), channel_id=1, source_target_pairs={{0,16},{2,18},{4,20},{6,22},{8,24},{10,26},{12,28},{14,30},{16,32}... | collective-permute-start | bytes 786440 | tf_op jit(solution)/shard_map/ppermute | solution.py:31
  163.0 5.7 %copy-start.11 = (bf16[1,256,4,128]{3,2,1,0:T(4,128)(2,1)S(1)}, bf16[1,256,4,128]{3,2,1,0:T(4,128)(2,1)}, u32[]{:S(2)}) copy-start(bf16[1,256,4,128]{3,2,1,0:T(4,128)(2,1)} %copy-done.10) | copy-start | bytes 786436
  165.7 18.9 %collective-permute-start.15 = (bf16[2,96,4,128]{3,1,2,0:T(8,128)(2,1)}, bf16[2,96,4,128]{3,1,2,0:T(8,128)(2,1)S(1)}, u32[]{:S(2)}, u32[]{:S(2)}) collective-permute-start(bf16[2,96,4,128]{3,1,2,0:T(8,128)(2,1)} %get-tuple-element.43), channel_id=1, source_target_pairs={{0,8},{2,10},{4,12},{6,14},{8,0},{10,2},{12,4},{14,6},{16,24},{18,... | collective-permute-start | bytes 589832 | tf_op jit(solution)/shard_map/ppermute | solution.py:12
  182.7 7.8 %copy-start.39 = (bf16[8,4,128]{2,0,1:T(8,128)(2,1)S(1)}, bf16[8,4,128]{2,0,1:T(8,128)(2,1)}, u32[]{:S(2)}) copy-start(bf16[8,4,128]{2,0,1:T(8,128)(2,1)} %copy-done.36) | copy-start | bytes 24580
  182.7 7.8 %copy-start.43 = (bf16[1,8,4,128]{3,1,2,0:T(8,128)(2,1)S(1)}, bf16[1,8,4,128]{3,1,2,0:T(8,128)(2,1)}, u32[]{:S(2)}) copy-start(bf16[1,8,4,128]{3,1,2,0:T(8,128)(2,1)} %copy-done.40) | copy-start | bytes 24580
  182.7 7.8 %copy-start.48 = (bf16[2,16,4,128]{3,1,2,0:T(8,128)(2,1)S(1)}, bf16[2,16,4,128]{3,1,2,0:T(8,128)(2,1)}, u32[]{:S(2)}) copy-start(bf16[2,16,4,128]{3,1,2,0:T(8,128)(2,1)} %get-tuple-element.42) | copy-start | bytes 98308
  182.7 7.8 %copy-start.50 = (bf16[2,8,4,128]{3,1,2,0:T(8,128)(2,1)S(1)}, bf16[2,8,4,128]{3,1,2,0:T(8,128)(2,1)}, u32[]{:S(2)}) copy-start(bf16[2,8,4,128]{3,1,2,0:T(8,128)(2,1)} %get-tuple-element.37) | copy-start | bytes 49156
  183.8 25.0 %copy-start.30 = (f32[32,4,128]{2,1,0:T(4,128)S(1)}, f32[32,4,128]{2,1,0:T(4,128)}, u32[]{:S(2)}) copy-start(f32[32,4,128]{2,1,0:T(4,128)} %bitcast_reduce_fusion.9) | copy-start | bytes 196612
  183.8 25.0 %copy-start.69 = (pred[384]{0:T(512)(128)(4,1)S(1)}, pred[384]{0:T(512)(128)(4,1)}, u32[]{:S(2)}) copy-start(pred[384]{0:T(512)(128)(4,1)} %fusion.116) | copy-start | bytes 1156
  185.2 41.7 %collective-permute-start.18 = (bf16[2,128,4,128]{3,1,2,0:T(8,128)(2,1)S(1)}, bf16[2,128,4,128]{3,1,2,0:T(8,128)(2,1)S(1)}, u32[]{:S(2)}, u32[]{:S(2)}) collective-permute-start(bf16[2,128,4,128]{3,1,2,0:T(8,128)(2,1)S(1)} %pad_maximum_fusion.11), channel_id=1, source_target_pairs={{0,48},{2,50},{4,52},{6,54},{8,56},{10,58},{12,60},{14,62},{32,80}... | collective-permute-start | bytes 786440 | tf_op jit(solution)/shard_map/ppermute | solution.py:220
  187.1 39.7 %collective-permute-start.17 = (bf16[2,128,4,128]{3,1,2,0:T(8,128)(2,1)S(1)}, bf16[2,128,4,128]{3,1,2,0:T(8,128)(2,1)S(1)}, u32[]{:S(2)}, u32[]{:S(2)}) collective-permute-start(bf16[2,128,4,128]{3,1,2,0:T(8,128)(2,1)S(1)} %pad_maximum_fusion.11), channel_id=1, source_target_pairs={{32,0},{34,2},{36,4},{38,6},{40,8},{42,10},{44,12},{46,14},{48,16}... | collective-permute-start | bytes 786440 | tf_op jit(solution)/shard_map/ppermute | solution.py:31
  190.6 25.4 %collective-permute-start.16 = (bf16[2,128,4,128]{3,1,2,0:T(8,128)(2,1)S(1)}, bf16[2,128,4,128]{3,1,2,0:T(8,128)(2,1)S(1)}, u32[]{:S(2)}, u32[]{:S(2)}) collective-permute-start(bf16[2,128,4,128]{3,1,2,0:T(8,128)(2,1)S(1)} %pad_maximum_fusion.11), channel_id=1, source_target_pairs={{0,32},{2,34},{4,36},{6,38},{8,40},{10,42},{12,44},{14,46},{16,48}... | collective-permute-start | bytes 786440 | tf_op jit(solution)/shard_map/ppermute | solution.py:31
  200.1 10.5 %collective-permute-start.19 = (bf16[2,64,4,128]{3,1,2,0:T(8,128)(2,1)S(1)}, bf16[2,64,4,128]{3,1,2,0:T(8,128)(2,1)}, u32[]{:S(2)}, u32[]{:S(2)}) collective-permute-start(bf16[2,64,4,128]{3,1,2,0:T(8,128)(2,1)S(1)} %pad_maximum_fusion.12), channel_id=1, source_target_pairs={{0,16},{2,18},{4,20},{6,22},{8,24},{10,26},{12,28},{14,30},{16,0},... | collective-permute-start | bytes 393224 | tf_op jit(solution)/shard_map/ppermute | solution.py:12
  209.1 17.8 %copy-start.45 = (f32[16,4,128]{2,1,0:T(4,128)S(1)}, f32[16,4,128]{2,1,0:T(4,128)}, u32[]{:S(2)}) copy-start(f32[16,4,128]{2,1,0:T(4,128)} %bitcast_reduce_fusion.8) | copy-start | bytes 98308
  209.1 17.9 %copy-start.65 = (pred[384]{0:T(512)(128)(4,1)S(1)}, pred[384]{0:T(512)(128)(4,1)}, u32[]{:S(2)}) copy-start(pred[384]{0:T(512)(128)(4,1)} %fusion.115) | copy-start | bytes 1156
  212.2 23.4 %collective-permute-start.22 = (bf16[2,128,4,128]{3,1,2,0:T(8,128)(2,1)}, bf16[2,128,4,128]{3,1,2,0:T(8,128)(2,1)}, u32[]{:S(2)}, u32[]{:S(2)}) collective-permute-start(bf16[2,128,4,128]{3,1,2,0:T(8,128)(2,1)} %constant_dynamic-update-slice_fusion.24), channel_id=1, source_target_pairs={{0,96},{2,98},{4,100},{6,102},{8,104},{10,106},{12,108},{14,110},{... | collective-permute-start | bytes 786440 | tf_op jit(solution)/shard_map/ppermute | solution.py:220
  214.1 20.5 %collective-permute-start.21 = (bf16[2,128,4,128]{3,1,2,0:T(8,128)(2,1)}, bf16[2,128,4,128]{3,1,2,0:T(8,128)(2,1)}, u32[]{:S(2)}, u32[]{:S(2)}) collective-permute-start(bf16[2,128,4,128]{3,1,2,0:T(8,128)(2,1)} %constant_dynamic-update-slice_fusion.24), channel_id=1, source_target_pairs={{64,0},{66,2},{68,4},{70,6},{72,8},{74,10},{76,12},{78,14},{80,16}... | collective-permute-start | bytes 786440 | tf_op jit(solution)/shard_map/ppermute | solution.py:31
  216.0 15.7 %collective-permute-start.20 = (bf16[2,128,4,128]{3,1,2,0:T(8,128)(2,1)}, bf16[2,128,4,128]{3,1,2,0:T(8,128)(2,1)}, u32[]{:S(2)}, u32[]{:S(2)}) collective-permute-start(bf16[2,128,4,128]{3,1,2,0:T(8,128)(2,1)} %constant_dynamic-update-slice_fusion.24), channel_id=1, source_target_pairs={{0,64},{2,66},{4,68},{6,70},{8,72},{10,74},{12,76},{14,78},{16,80}... | collective-permute-start | bytes 786440 | tf_op jit(solution)/shard_map/ppermute | solution.py:31
  227.0 9.6 %copy-start.49 = (f32[8,4,128]{2,1,0:T(4,128)S(1)}, f32[8,4,128]{2,1,0:T(4,128)}, u32[]{:S(2)}) copy-start(f32[8,4,128]{2,1,0:T(4,128)} %bitcast_reduce_fusion.7) | copy-start | bytes 49156
  227.0 9.6 %copy-start.68 = (pred[384]{0:T(512)(128)(4,1)S(1)}, pred[384]{0:T(512)(128)(4,1)}, u32[]{:S(2)}) copy-start(pred[384]{0:T(512)(128)(4,1)} %fusion.114) | copy-start | bytes 1156
  262.0 13.3 %copy-start.14 = (f32[128,4,128]{2,1,0:T(4,128)S(1)}, f32[128,4,128]{2,1,0:T(4,128)}, u32[]{:S(2)}) copy-start(f32[128,4,128]{2,1,0:T(4,128)} %copy.289) | copy-start | bytes 786436
  287.2 5.9 %collective-permute-start.23 = (bf16[512,1024]{1,0:T(8,128)(2,1)}, bf16[512,1024]{1,0:T(8,128)(2,1)}, u32[]{:S(2)}, u32[]{:S(2)}) collective-permute-start(bf16[512,1024]{1,0:T(8,128)(2,1)} %convolution_convert_fusion), channel_id=1, source_target_pairs={{0,1},{1,0},{2,3},{3,2},{4,5},{5,4},{6,7},{7,6},{8,9},{9,8},{10,11... | collective-permute-start | bytes 3145736 | tf_op jit(solution)/shard_map/ppermute | solution.py:292
  (41 other events, 69.3 us)
Sparse Core Ops, SparseCore 0:
  22.1 160.2 all-gather.2

commit v3 on v0

--- a/solution.py
+++ b/solution.py
@@ -134,11 +134,7 @@
             theirs = partner[:, offset : offset + width]
             offset = offset + width
             mine = current[level_index]
-            current[level_index] = jnp.where(
-                upper,
-                jnp.concatenate([theirs, mine], axis=1),
-                jnp.concatenate([mine, theirs], axis=1),
-            )
+            current[level_index] = jnp.concatenate([mine, theirs], axis=1)
     return current
 
 
@@ -204,7 +200,7 @@
         pieces[level_index] = jnp.stack(
             [coarsen(key_rows, level_index, True), coarsen(value_rows, level_index, False)]
         )
-    shift_levels = list(range(2, top_level - 1))
+    shift_levels = list(range(2, top_level - 2))
     assembled = assemble_joint(pieces, shift_levels, device_index)
     for level_index in shift_levels:
         group = 1 << level_index - 2
@@ -229,8 +225,8 @@
                 ),
             )
         )
-    coarse_list = [top_level - 1, top_level]
-    wholes = gather_packed((pieces[top_level - 1], pieces[top_level]), "seq", (1, 1))
+    coarse_list = [top_level - 2, top_level - 1, top_level]
+    wholes = gather_packed(tuple(pieces[level_index] for level_index in coarse_list), "seq", (1,) * len(coarse_list))
     for position, level_index in enumerate(coarse_list):
         group = 1 << level_index - 2
         block_total = seq_count // group

time: 290 us -> 296 us (1.021)
  the two profiles are of different devices: /device:TPU:193 before, /device:TPU:265 now
where the time goes in v3:
time: 296 us; the launch traced here: 293 us
  local copies, waits for them, and re-layouts  90.9 us (31%)
  starting transfers between devices  81.2 us (27%)
  other arithmetic  58.5 us (20%)
  blocking collectives  16.4 us (6%)
  matrix products  16.1 us (5%)
  waiting for transfers between devices  15.5 us (5%)
  between operations  14.8 us (5%)
    ppermute x8, starting transfers between devices, shifted(): lax.ppermute(value, axis, [(source, source + steps) for source in range(i...  42.7 us
    slice x6, local copies, waits for them, and re-layouts, gather_packed(): parts = lines[:, at:at + a.size].reshape(-1, *a.shape)  22.8 us
    ppermute x7, starting transfers between devices, partner_2(): return lax.ppermute(value, axis, pairs)  22.7 us
    all_to_all x1, blocking collectives, summed_on_arrival(): lax.all_to_all(cut_along(value, dim, length), axis, 0, 0, tiled=True)  16.4 us
    transpose x3, local copies, waits for them, and re-layouts, joined_along(): parts = jnp.moveaxis(parts, 0, dim)  15.4 us
    ppermute x7, waiting for transfers between devices, partner_2(): return lax.ppermute(value, axis, pairs)  14.7 us
    ppermute x2, starting transfers between devices, with_halo(): after = lax.ppermute(initial, axis, down)  12 us
    reduce_sum x24, other arithmetic, coarsen(): summed = jnp.sum(grouped, axis=1)  11.1 us
  transfers between devices with their start and end apart: 20, of which 3 were waited for; matrix products, arithmetic and copies ran while one was open for 29% of the time, Pallas kernels for 0%

profile of v3, /device:TPU:265, one launch (start us, length us, event | category | flops | bytes accessed | tf_op | source)
XLA Modules:
  0.0 293.4 jit_solution(15929069014872100116)
XLA Ops:
  6.5 1.6 bitcast_reduce_fusion.20
  8.2 1.4 bitcast_reduce_fusion.19
  10.4 4.2 %collective-permute-start.4 = (bf16[2,128,4,128]{3,1,2,0:T(8,128)(2,1)}, bf16[2,128,4,128]{3,1,2,0:T(8,128)(2,1)}, u32[]{:S(2)}, u32[]{:S(2)}) collective-permute-start(bf16[2,128,4,128]{3,1,2,0:T(8,128)(2,1)} %pad_maximum_fusion.9), channel_id=1, source_target_pairs={{0,4},{2,6},{4,8},{6,10},{8,12},{10,14},{12,16},{14,18},{16,20},{1... | collective-permute-start | bytes 786440 | tf_op jit(solution)/shard_map/ppermute | solution.py:31
  14.6 7.4 %collective-permute-start.5 = (bf16[2,128,4,128]{3,1,2,0:T(8,128)(2,1)}, bf16[2,128,4,128]{3,1,2,0:T(8,128)(2,1)}, u32[]{:S(2)}, u32[]{:S(2)}) collective-permute-start(bf16[2,128,4,128]{3,1,2,0:T(8,128)(2,1)} %pad_maximum_fusion.9), channel_id=1, source_target_pairs={{4,0},{6,2},{8,4},{10,6},{12,8},{14,10},{16,12},{18,14},{20,16},{2... | collective-permute-start | bytes 786440 | tf_op jit(solution)/shard_map/ppermute | solution.py:31
  26.4 2.1 collective-permute-start.7
  30.3 1.9 collective-permute-start
  32.2 3.4 %collective-permute-start.1 = (bf16[2,128,4,128]{3,1,2,0:T(8,128)(2,1)}, bf16[2,128,4,128]{3,1,2,0:T(8,128)(2,1)}, u32[]{:S(2)}, u32[]{:S(2)}) collective-permute-start(bf16[2,128,4,128]{3,1,2,0:T(8,128)(2,1)} %get-tuple-element.34), channel_id=1, source_target_pairs={{2,0},{4,2},{6,4},{8,6},{10,8},{12,10},{14,12},{16,14},{18,16},{20... | collective-permute-start | bytes 786440 | tf_op jit(solution)/shard_map/ppermute | solution.py:23
  37.4 1.2 pad_maximum_fusion.6
  41.8 1.0 bitcast_reduce_fusion.21
  56.6 1.2 fusion.111
  57.8 1.3 fusion.110
  59.1 1.2 fusion.109
  60.3 1.2 fusion.108
  61.5 1.2 fusion.107
  62.7 1.2 fusion.112
  63.9 1.9 collective-permute-start.2
  69.3 8.6 %collective-permute-start.3 = (bf16[2,256,4,128]{3,2,1,0:T(4,128)(2,1)}, bf16[2,256,4,128]{3,2,1,0:T(4,128)(2,1)S(1)}, u32[]{:S(2)}, u32[]{:S(2)}) collective-permute-start(bf16[2,256,4,128]{3,2,1,0:T(4,128)(2,1)} %pad_maximum_fusion.6), channel_id=1, source_target_pairs={{2,0},{4,2},{6,4},{8,6},{10,8},{12,10},{14,12},{16,14},{18,16},{20... | collective-permute-start | bytes 1572872 | tf_op jit(solution)/shard_map/ppermute | solution.py:23
  78.9 1.9 collective-permute-start.8
  80.8 11.7 %collective-permute-start.9 = (bf16[2,128,4,128]{3,1,2,0:T(8,128)(2,1)S(1)}, bf16[2,128,4,128]{3,1,2,0:T(8,128)(2,1)S(1)}, u32[]{:S(2)}, u32[]{:S(2)}) collective-permute-start(bf16[2,128,4,128]{3,1,2,0:T(8,128)(2,1)S(1)} %pad_maximum_fusion.10), channel_id=1, source_target_pairs={{8,0},{10,2},{12,4},{14,6},{16,8},{18,10},{20,12},{22,14},{24,16},... | collective-permute-start | bytes 786440 | tf_op jit(solution)/shard_map/ppermute | solution.py:31
  92.5 1.1 pad_maximum_fusion.1
  96.3 1.6 fusion.12
  97.9 1.4 fusion.1
  99.3 2.0 collective-permute-start.11
  101.4 1.1 broadcast_select_fusion.3
  102.5 1.1 copy.400
  103.5 14.5 %collective-permute-done.11 = bf16[2,96,4,128]{3,1,2,0:T(8,128)(2,1)S(1)} collective-permute-done((bf16[2,96,4,128]{3,1,2,0:T(8,128)(2,1)S(1)}, bf16[2,96,4,128]{3,1,2,0:T(8,128)(2,1)S(1)}, u32[]{:S(2)}, u32[]{:S(2)}) %collective-permute-start.11) | collective-permute-done | bytes 196640 | tf_op jit(solution)/shard_map/ppermute | solution.py:12
  118.0 5.3 %collective-permute-start.6 = (bf16[2,128,4,128]{3,1,2,0:T(8,128)(2,1)S(1)}, bf16[2,128,4,128]{3,1,2,0:T(8,128)(2,1)S(1)}, u32[]{:S(2)}, u32[]{:S(2)}) collective-permute-start(bf16[2,128,4,128]{3,1,2,0:T(8,128)(2,1)S(1)} %get-tuple-element.41), channel_id=1, source_target_pairs={{0,2},{2,0},{4,6},{6,4},{8,10},{10,8},{12,14},{14,12},{16,18},{18,... | collective-permute-start | bytes 786440 | tf_op jit(solution)/shard_map/ppermute | solution.py:12
  124.9 2.7 collective-permute-start.12
  127.6 5.9 %collective-permute-start.13 = (bf16[2,128,4,128]{3,1,2,0:T(8,128)(2,1)}, bf16[2,128,4,128]{3,1,2,0:T(8,128)(2,1)}, u32[]{:S(2)}, u32[]{:S(2)}) collective-permute-start(bf16[2,128,4,128]{3,1,2,0:T(8,128)(2,1)} %pad_maximum_fusion.11), channel_id=1, source_target_pairs={{16,0},{18,2},{20,4},{22,6},{24,8},{26,10},{28,12},{30,14},{32,16}... | collective-permute-start | bytes 786440 | tf_op jit(solution)/shard_map/ppermute | solution.py:31
  134.3 6.4 %collective-permute-start.15 = (bf16[2,64,4,128]{3,1,2,0:T(8,128)(2,1)}, bf16[2,64,4,128]{3,1,2,0:T(8,128)(2,1)}, u32[]{:S(2)}, u32[]{:S(2)}) collective-permute-start(bf16[2,64,4,128]{3,1,2,0:T(8,128)(2,1)} %pad_maximum_fusion.14), channel_id=1, source_target_pairs={{0,8},{2,10},{4,12},{6,14},{8,0},{10,2},{12,4},{14,6},{16,24},{18,... | collective-permute-start | bytes 393224 | tf_op jit(solution)/shard_map/ppermute | solution.py:12
  140.8 1.9 collective-permute-start.10
  142.7 6.8 %pad_maximum_fusion.2 = bf16[2,768,4,128]{3,2,1,0:T(4,128)(2,1)S(1)} fusion(bf16[2,256,4,128]{3,2,1,0:T(4,128)(2,1)S(1)} %collective-permute-done.3, bf16[1,256,4,128]{3,2,1,0:T(4,128)(2,1)S(1)} %bitcast.542, bf16[1,256,4,128]{3,2,1,0:T(4,128)(2,1)S(1)} %copy-done.10, bf16[2,256,4,128]{3,2,1,0:T(4,128)(2,1)S(1)} %collective-permute-done.2), kind=kLoop, calls=%fused_computation.11 | loop fusion | flops 2359296 | bytes 3145728 | tf_op jit(solution)/shard_map/concatenate | solution.py:24
  158.2 1.7 pad_maximum_fusion.12
  159.9 1.9 collective-permute-start.16
  161.8 7.0 %collective-permute-start.17 = (bf16[2,128,4,128]{3,1,2,0:T(8,128)(2,1)}, bf16[2,128,4,128]{3,1,2,0:T(8,128)(2,1)}, u32[]{:S(2)}, u32[]{:S(2)}) collective-permute-start(bf16[2,128,4,128]{3,1,2,0:T(8,128)(2,1)} %pad_maximum_fusion.12), channel_id=1, source_target_pairs={{32,0},{34,2},{36,4},{38,6},{40,8},{42,10},{44,12},{46,14},{48,16}... | collective-permute-start | bytes 786440 | tf_op jit(solution)/shard_map/ppermute | solution.py:31
  168.8 1.0 constant_dynamic-update-slice_fusion.8
  169.8 1.9 broadcast_select_fusion.1
  171.7 2.9 collective-permute-start.14
  174.6 1.0 constant_dynamic-update-slice_fusion.3
  178.7 1.3 convolution_bitcast_fusion.2
  181.8 1.9 broadcast_select_fusion
  183.7 2.0 collective-permute-start.18
  185.7 1.0 constant_dynamic-update-slice_fusion.6
  189.8 1.9 convolution_bitcast_fusion.3
  191.8 1.7 constant_dynamic-update-slice_fusion.9
  193.5 1.3 fusion.135
  196.5 1.9 convolution_bitcast_fusion.4
  198.4 10.9 %reshape.1312 = bf16[256,14336]{1,0:T(8,128)(2,1)} reshape(bf16[3670016]{0:T(1024)(128)(2,1)} %all-gather.3.cloned.1.call-done) | data formatting | bytes 14680064 | tf_op jit(solution)/shard_map/all_gather | solution.py:42
  209.3 4.5 %slice.172 = bf16[256,8192]{1,0:T(8,128)(2,1)} slice(bf16[256,14336]{1,0:T(8,128)(2,1)} %reshape.1312), slice={[0:256], [0:8192]} | slice | bytes 8388608 | tf_op jit(solution)/shard_map/slice | solution.py:44
  213.8 3.1 %slice.174 = bf16[256,4096]{1,0:T(8,128)(2,1)} slice(bf16[256,14336]{1,0:T(8,128)(2,1)} %reshape.1312), slice={[0:256], [8192:12288]} | slice | bytes 4194304 | tf_op jit(solution)/shard_map/slice | solution.py:44
  217.0 2.3 slice.176
  219.3 6.4 %copy.386 = bf16[256,8192]{0,1:T(8,128)(2,1)} copy(bf16[256,8192]{1,0:T(8,128)(2,1)} %slice.172) | data formatting | bytes 8388608 | tf_op jit(solution)/shard_map/slice | solution.py:44
  225.7 7.5 %copy.387 = bf16[2,256,8,4,128]{4,2,1,3,0:T(8,128)(2,1)} copy(bf16[2,256,8,4,128]{1,4,3,2,0:T(8,128)(2,1)} %bitcast.529) | data formatting | bytes 8388608 | tf_op jit(solution)/shard_map/transpose | solution.py:35
  233.2 1.2 dynamic-slice_bitcast_fusion.8
  236.4 2.3 copy.394
  238.7 3.7 %copy.395 = bf16[2,256,2,4,128]{4,2,1,3,0:T(2,128)(2,1)} copy(bf16[2,256,2,4,128]{1,4,3,2,0:T(8,128)(2,1)} %bitcast.538) | data formatting | bytes 2097152 | tf_op jit(solution)/shard_map/transpose | solution.py:35
  242.4 1.2 dynamic-slice_bitcast_fusion.2
  245.6 4.1 %copy.389 = bf16[256,4096]{0,1:T(8,128)(2,1)} copy(bf16[256,4096]{1,0:T(8,128)(2,1)} %slice.174) | data formatting | bytes 4194304 | tf_op jit(solution)/shard_map/slice | solution.py:44
  249.7 4.2 %copy.390 = bf16[2,256,4,4,128]{4,2,1,3,0:T(4,128)(2,1)} copy(bf16[2,256,4,4,128]{1,4,3,2,0:T(8,128)(2,1)} %bitcast.531) | data formatting | bytes 4194304 | tf_op jit(solution)/shard_map/transpose | solution.py:35
  253.9 1.2 dynamic-slice_bitcast_fusion.5
  261.8 3.6 %fusion.24 = bf16[512,4,128]{2,0,1:T(8,128)(2,1)S(1)} fusion(f32[4,128,4,128]{3,1,0,2:T(8,128)S(1)} %copy-done.8, f32[512,4,128]{2,0,1:T(8,128)S(1)} %bitcast.536, f32[512,4,128]{2,0,1:T(8,128)S(1)} %bitcast.537, f32[512,4]{0,1:T(4,128)S(1)} %get-tuple-element.5, f32[2,4,128]{2,0,1:T(2,128)S(1)} %copy-done.42, f32[512,4]{0,1:T(4,128)S(1)} %get-tuple-element.12, ...), kind=kLoop, calls=%fused_computation.50 | loop fusion | flops 4980736 | bytes 4009984 | tf_op jit(solution)/shard_map/convert_element_type | solution.py:276
  265.3 1.3 bitcast_convert_fusion
  266.8 16.4 %all_to_all.5 = bf16[2,512,1024]{2,1,0:T(8,128)(2,1)} all-to-all(bf16[2,512,1024]{2,1,0:T(8,128)(2,1)S(1)} %bitcast.532), channel_id=1, replica_groups=mesh['seq'=256,'head'=2] {'head'}, dimensions={0} | all-to-all | bytes 4194304 | tf_op jit(solution)/shard_map/all_to_all | solution.py:58
  283.2 3.3 %reduce_sum.342 = bf16[512,1024]{1,0:T(8,128)(2,1)} reduce(bf16[2,512,1024]{2,1,0:T(8,128)(2,1)} %all_to_all.5, bf16[]{:T(256)} %constant.335.clone.1), dimensions={0}, to_apply=%region_42.43 | reduce | flops 524288 | bytes 3145730 | tf_op jit(solution)/shard_map/reduce_sum | solution.py:59
  (319 shorter events, 63.6 us)
Async XLA Ops:
  6.5 258.8 %copy-start = (bf16[4,128,2048]{2,1,0:T(8,128)(2,1)S(1)}, bf16[4,128,2048]{2,1,0:T(8,128)(2,1)}, u32[]{:S(2)}) copy-start(bf16[4,128,2048]{2,1,0:T(8,128)(2,1)} %param.7) | copy-start | bytes 6291460
  6.5 15.4 %copy-start.1 = (bf16[512,4,128]{2,1,0:T(4,128)(2,1)S(1)}, bf16[512,4,128]{2,1,0:T(4,128)(2,1)}, u32[]{:S(2)}) copy-start(bf16[512,4,128]{2,1,0:T(4,128)(2,1)} %param.5) | copy-start | bytes 1572868
  6.5 15.7 %copy-start.2 = (bf16[512,4,128]{2,1,0:T(4,128)(2,1)S(1)}, bf16[512,4,128]{2,1,0:T(4,128)(2,1)}, u32[]{:S(2)}) copy-start(bf16[512,4,128]{2,1,0:T(4,128)(2,1)} %param.6) | copy-start | bytes 1572868
  6.5 191.9 %all-gather.3.cloned.1.call-start = ((), (), s32[]{:S(2)}) async-start(), calls=%async_computation.1 | async-start | bytes 7368704 | tf_op jit(solution)/shard_map/all_gather | solution.py:42
  10.4 58.9 %collective-permute-start.4 = (bf16[2,128,4,128]{3,1,2,0:T(8,128)(2,1)}, bf16[2,128,4,128]{3,1,2,0:T(8,128)(2,1)}, u32[]{:S(2)}, u32[]{:S(2)}) collective-permute-start(bf16[2,128,4,128]{3,1,2,0:T(8,128)(2,1)} %pad_maximum_fusion.9), channel_id=1, source_target_pairs={{0,4},{2,6},{4,8},{6,10},{8,12},{10,14},{12,16},{14,18},{16,20},{1... | collective-permute-start | bytes 786440 | tf_op jit(solution)/shard_map/ppermute | solution.py:31
  14.6 84.8 %collective-permute-start.5 = (bf16[2,128,4,128]{3,1,2,0:T(8,128)(2,1)}, bf16[2,128,4,128]{3,1,2,0:T(8,128)(2,1)}, u32[]{:S(2)}, u32[]{:S(2)}) collective-permute-start(bf16[2,128,4,128]{3,1,2,0:T(8,128)(2,1)} %pad_maximum_fusion.9), channel_id=1, source_target_pairs={{4,0},{6,2},{8,4},{10,6},{12,8},{14,10},{16,12},{18,14},{20,16},{2... | collective-permute-start | bytes 786440 | tf_op jit(solution)/shard_map/ppermute | solution.py:31
  25.6 4.7 %copy-start.26 = (bf16[16,4,128]{2,0,1:T(8,128)(2,1)}, bf16[16,4,128]{2,0,1:T(8,128)(2,1)S(1)}, u32[]{:S(2)}) copy-start(bf16[16,4,128]{2,0,1:T(8,128)(2,1)S(1)} %copy.532) | copy-start | bytes 49156
  25.6 4.7 %copy-start.21 = (bf16[32,4,128]{2,0,1:T(8,128)(2,1)}, bf16[32,4,128]{2,0,1:T(8,128)(2,1)S(1)}, u32[]{:S(2)}) copy-start(bf16[32,4,128]{2,0,1:T(8,128)(2,1)S(1)} %copy.531) | copy-start | bytes 98308
  25.6 4.6 %copy-start.19 = (bf16[1,32,4,128]{3,1,2,0:T(8,128)(2,1)}, bf16[1,32,4,128]{3,1,2,0:T(8,128)(2,1)S(1)}, u32[]{:S(2)}) copy-start(bf16[1,32,4,128]{3,1,2,0:T(8,128)(2,1)S(1)} %fusion.69) | copy-start | bytes 98308
  26.4 37.6 %collective-permute-start.7 = (bf16[2,112,4,128]{3,1,2,0:T(8,128)(2,1)}, bf16[2,112,4,128]{3,1,2,0:T(8,128)(2,1)}, u32[]{:S(2)}, u32[]{:S(2)}) collective-permute-start(bf16[2,112,4,128]{3,1,2,0:T(8,128)(2,1)} %maximum_maximum_fusion.1), channel_id=1, source_target_pairs={{0,2},{2,0},{4,6},{6,4},{8,10},{10,8},{12,14},{14,12},{16,18},{18,... | collective-permute-start | bytes 688136 | tf_op jit(solution)/shard_map/ppermute | solution.py:12
  28.6 1.7 copy-start.6
  30.3 48.6 %collective-permute-start = (bf16[2,128,4,128]{3,1,2,0:T(8,128)(2,1)}, bf16[2,128,4,128]{3,1,2,0:T(8,128)(2,1)}, u32[]{:S(2)}, u32[]{:S(2)}) collective-permute-start(bf16[2,128,4,128]{3,1,2,0:T(8,128)(2,1)} %get-tuple-element.33), channel_id=1, source_target_pairs={{0,2},{2,4},{4,6},{6,8},{8,10},{10,12},{12,14},{14,16},{16,18},{18... | collective-permute-start | bytes 786440 | tf_op jit(solution)/shard_map/ppermute | solution.py:22
  32.2 48.6 %collective-permute-start.1 = (bf16[2,128,4,128]{3,1,2,0:T(8,128)(2,1)}, bf16[2,128,4,128]{3,1,2,0:T(8,128)(2,1)}, u32[]{:S(2)}, u32[]{:S(2)}) collective-permute-start(bf16[2,128,4,128]{3,1,2,0:T(8,128)(2,1)} %get-tuple-element.34), channel_id=1, source_target_pairs={{2,0},{4,2},{6,4},{8,6},{10,8},{12,10},{14,12},{16,14},{18,16},{20... | collective-permute-start | bytes 786440 | tf_op jit(solution)/shard_map/ppermute | solution.py:23
  36.8 1.8 copy-start.3
  37.4 3.3 %copy-start.9 = (bf16[1,256,4,128]{3,2,1,0:T(4,128)(2,1)}, bf16[1,256,4,128]{3,2,1,0:T(4,128)(2,1)S(1)}, u32[]{:S(2)}) copy-start(bf16[1,256,4,128]{3,2,1,0:T(4,128)(2,1)S(1)} %fusion.41) | copy-start | bytes 786436
  45.8 46.7 %copy-start.5 = (bf16[1,512,4,128]{3,1,2,0:T(8,128)(2,1)S(1)}, bf16[1,512,4,128]{3,1,2,0:T(8,128)(2,1)}, u32[]{:S(2)}) copy-start(bf16[1,512,4,128]{3,1,2,0:T(8,128)(2,1)} %copy-done.4) | copy-start | bytes 1572868
  56.5 36.0 %copy-start.7 = (bf16[1,512,4,128]{3,1,2,0:T(8,128)(2,1)S(1)}, bf16[1,512,4,128]{3,1,2,0:T(8,128)(2,1)}, u32[]{:S(2)}) copy-start(bf16[1,512,4,128]{3,1,2,0:T(8,128)(2,1)} %copy-done.6) | copy-start | bytes 1572868
  63.9 70.4 %collective-permute-start.2 = (bf16[2,256,4,128]{3,2,1,0:T(4,128)(2,1)}, bf16[2,256,4,128]{3,2,1,0:T(4,128)(2,1)S(1)}, u32[]{:S(2)}, u32[]{:S(2)}) collective-permute-start(bf16[2,256,4,128]{3,2,1,0:T(4,128)(2,1)} %pad_maximum_fusion.6), channel_id=1, source_target_pairs={{0,2},{2,4},{4,6},{6,8},{8,10},{10,12},{12,14},{14,16},{16,18},{18... | collective-permute-start | bytes 1572872 | tf_op jit(solution)/shard_map/ppermute | solution.py:22
  66.6 56.8 %copy-start.24 = (bf16[2,16,4,128]{3,1,2,0:T(8,128)(2,1)}, bf16[2,16,4,128]{3,1,2,0:T(8,128)(2,1)S(1)}, u32[]{:S(2)}) copy-start(bf16[2,16,4,128]{3,1,2,0:T(8,128)(2,1)S(1)} %slice.167) | copy-start | bytes 98308
  69.3 71.5 %collective-permute-start.3 = (bf16[2,256,4,128]{3,2,1,0:T(4,128)(2,1)}, bf16[2,256,4,128]{3,2,1,0:T(4,128)(2,1)S(1)}, u32[]{:S(2)}, u32[]{:S(2)}) collective-permute-start(bf16[2,256,4,128]{3,2,1,0:T(4,128)(2,1)} %pad_maximum_fusion.6), channel_id=1, source_target_pairs={{2,0},{4,2},{6,4},{8,6},{10,8},{12,10},{14,12},{16,14},{18,16},{20... | collective-permute-start | bytes 1572872 | tf_op jit(solution)/shard_map/ppermute | solution.py:23
  78.9 46.0 %collective-permute-start.8 = (bf16[2,128,4,128]{3,1,2,0:T(8,128)(2,1)S(1)}, bf16[2,128,4,128]{3,1,2,0:T(8,128)(2,1)S(1)}, u32[]{:S(2)}, u32[]{:S(2)}) collective-permute-start(bf16[2,128,4,128]{3,1,2,0:T(8,128)(2,1)S(1)} %pad_maximum_fusion.10), channel_id=1, source_target_pairs={{0,8},{2,10},{4,12},{6,14},{8,16},{10,18},{12,20},{14,22},{16,24},... | collective-permute-start | bytes 786440 | tf_op jit(solution)/shard_map/ppermute | solution.py:31
  80.8 46.7 %collective-permute-start.9 = (bf16[2,128,4,128]{3,1,2,0:T(8,128)(2,1)S(1)}, bf16[2,128,4,128]{3,1,2,0:T(8,128)(2,1)S(1)}, u32[]{:S(2)}, u32[]{:S(2)}) collective-permute-start(bf16[2,128,4,128]{3,1,2,0:T(8,128)(2,1)S(1)} %pad_maximum_fusion.10), channel_id=1, source_target_pairs={{8,0},{10,2},{12,4},{14,6},{16,8},{18,10},{20,12},{22,14},{24,16},... | collective-permute-start | bytes 786440 | tf_op jit(solution)/shard_map/ppermute | solution.py:31
  96.3 1.6 copy-start.34
  99.3 24.1 %copy-start.27 = (bf16[16,4,128]{2,0,1:T(8,128)(2,1)S(1)}, bf16[16,4,128]{2,0,1:T(8,128)(2,1)}, u32[]{:S(2)}) copy-start(bf16[16,4,128]{2,0,1:T(8,128)(2,1)} %copy-done.26) | copy-start | bytes 49156
  99.3 18.7 %collective-permute-start.11 = (bf16[2,96,4,128]{3,1,2,0:T(8,128)(2,1)S(1)}, bf16[2,96,4,128]{3,1,2,0:T(8,128)(2,1)S(1)}, u32[]{:S(2)}, u32[]{:S(2)}) collective-permute-start(bf16[2,96,4,128]{3,1,2,0:T(8,128)(2,1)S(1)} %pad_maximum_fusion.13), channel_id=1, source_target_pairs={{0,4},{2,6},{4,0},{6,2},{8,12},{10,14},{12,8},{14,10},{16,20},{18,... | collective-permute-start | bytes 589832 | tf_op jit(solution)/shard_map/ppermute | solution.py:12
  102.5 21.6 %copy-start.20 = (bf16[1,32,4,128]{3,1,2,0:T(8,128)(2,1)S(1)}, bf16[1,32,4,128]{3,1,2,0:T(8,128)(2,1)}, u32[]{:S(2)}) copy-start(bf16[1,32,4,128]{3,1,2,0:T(8,128)(2,1)} %copy-done.19) | copy-start | bytes 98308
  102.5 21.6 %copy-start.22 = (bf16[32,4,128]{2,0,1:T(8,128)(2,1)S(1)}, bf16[32,4,128]{2,0,1:T(8,128)(2,1)}, u32[]{:S(2)}) copy-start(bf16[32,4,128]{2,0,1:T(8,128)(2,1)} %copy-done.21) | copy-start | bytes 98308
  103.5 39.2 %copy-start.10 = (bf16[1,256,4,128]{3,2,1,0:T(4,128)(2,1)S(1)}, bf16[1,256,4,128]{3,2,1,0:T(4,128)(2,1)}, u32[]{:S(2)}) copy-start(bf16[1,256,4,128]{3,2,1,0:T(4,128)(2,1)} %copy-done.9) | copy-start | bytes 786436
  118.0 31.7 %collective-permute-start.6 = (bf16[2,128,4,128]{3,1,2,0:T(8,128)(2,1)S(1)}, bf16[2,128,4,128]{3,1,2,0:T(8,128)(2,1)S(1)}, u32[]{:S(2)}, u32[]{:S(2)}) collective-permute-start(bf16[2,128,4,128]{3,1,2,0:T(8,128)(2,1)S(1)} %get-tuple-element.41), channel_id=1, source_target_pairs={{0,2},{2,0},{4,6},{6,4},{8,10},{10,8},{12,14},{14,12},{16,18},{18,... | collective-permute-start | bytes 786440 | tf_op jit(solution)/shard_map/ppermute | solution.py:12
  124.9 43.9 %collective-permute-start.12 = (bf16[2,128,4,128]{3,1,2,0:T(8,128)(2,1)}, bf16[2,128,4,128]{3,1,2,0:T(8,128)(2,1)}, u32[]{:S(2)}, u32[]{:S(2)}) collective-permute-start(bf16[2,128,4,128]{3,1,2,0:T(8,128)(2,1)} %pad_maximum_fusion.11), channel_id=1, source_target_pairs={{0,16},{2,18},{4,20},{6,22},{8,24},{10,26},{12,28},{14,30},{16,32}... | collective-permute-start | bytes 786440 | tf_op jit(solution)/shard_map/ppermute | solution.py:31
  127.6 42.2 %collective-permute-start.13 = (bf16[2,128,4,128]{3,1,2,0:T(8,128)(2,1)}, bf16[2,128,4,128]{3,1,2,0:T(8,128)(2,1)}, u32[]{:S(2)}, u32[]{:S(2)}) collective-permute-start(bf16[2,128,4,128]{3,1,2,0:T(8,128)(2,1)} %pad_maximum_fusion.11), channel_id=1, source_target_pairs={{16,0},{18,2},{20,4},{22,6},{24,8},{26,10},{28,12},{30,14},{32,16}... | collective-permute-start | bytes 786440 | tf_op jit(solution)/shard_map/ppermute | solution.py:31
  134.3 6.4 %copy-start.11 = (bf16[2,384,4,128]{3,1,2,0:T(8,128)(2,1)}, bf16[2,384,4,128]{3,1,2,0:T(8,128)(2,1)S(1)}, u32[]{:S(2)}) copy-start(bf16[2,384,4,128]{3,1,2,0:T(8,128)(2,1)S(1)} %get-tuple-element.36) | copy-start | bytes 2359300
  134.3 23.8 %collective-permute-start.15 = (bf16[2,64,4,128]{3,1,2,0:T(8,128)(2,1)}, bf16[2,64,4,128]{3,1,2,0:T(8,128)(2,1)}, u32[]{:S(2)}, u32[]{:S(2)}) collective-permute-start(bf16[2,64,4,128]{3,1,2,0:T(8,128)(2,1)} %pad_maximum_fusion.14), channel_id=1, source_target_pairs={{0,8},{2,10},{4,12},{6,14},{8,0},{10,2},{12,4},{14,6},{16,24},{18,... | collective-permute-start | bytes 393224 | tf_op jit(solution)/shard_map/ppermute | solution.py:12
  140.8 33.8 %collective-permute-start.10 = (bf16[2,128,4,128]{3,1,2,0:T(8,128)(2,1)}, bf16[2,128,4,128]{3,1,2,0:T(8,128)(2,1)}, u32[]{:S(2)}, u32[]{:S(2)}) collective-permute-start(bf16[2,128,4,128]{3,1,2,0:T(8,128)(2,1)} %get-tuple-element.35), channel_id=1, source_target_pairs={{0,4},{2,6},{4,0},{6,2},{8,12},{10,14},{12,8},{14,10},{16,20},{18,... | collective-permute-start | bytes 786440 | tf_op jit(solution)/shard_map/ppermute | solution.py:12
  156.0 2.1 copy-start.25
  158.1 16.5 %copy-start.12 = (bf16[2,384,4,128]{3,1,2,0:T(8,128)(2,1)S(1)}, bf16[2,384,4,128]{3,1,2,0:T(8,128)(2,1)}, u32[]{:S(2)}) copy-start(bf16[2,384,4,128]{3,1,2,0:T(8,128)(2,1)} %copy-done.11) | copy-start | bytes 2359300
  158.1 18.3 %copy-start.23 = (f32[64,4,128]{2,1,0:T(4,128)S(1)}, f32[64,4,128]{2,1,0:T(4,128)}, u32[]{:S(2)}) copy-start(f32[64,4,128]{2,1,0:T(4,128)} %bitcast_reduce_fusion.18) | copy-start | bytes 393220
  158.2 18.3 %copy-start.45 = (pred[384]{0:T(512)(128)(4,1)S(1)}, pred[384]{0:T(512)(128)(4,1)}, u32[]{:S(2)}) copy-start(pred[384]{0:T(512)(128)(4,1)} %fusion.112) | copy-start | bytes 1156
  159.9 20.2 %collective-permute-start.16 = (bf16[2,128,4,128]{3,1,2,0:T(8,128)(2,1)}, bf16[2,128,4,128]{3,1,2,0:T(8,128)(2,1)}, u32[]{:S(2)}, u32[]{:S(2)}) collective-permute-start(bf16[2,128,4,128]{3,1,2,0:T(8,128)(2,1)} %pad_maximum_fusion.12), channel_id=1, source_target_pairs={{0,32},{2,34},{4,36},{6,38},{8,40},{10,42},{12,44},{14,46},{16,48}... | collective-permute-start | bytes 786440 | tf_op jit(solution)/shard_map/ppermute | solution.py:31
  161.8 20.0 %collective-permute-start.17 = (bf16[2,128,4,128]{3,1,2,0:T(8,128)(2,1)}, bf16[2,128,4,128]{3,1,2,0:T(8,128)(2,1)}, u32[]{:S(2)}, u32[]{:S(2)}) collective-permute-start(bf16[2,128,4,128]{3,1,2,0:T(8,128)(2,1)} %pad_maximum_fusion.12), channel_id=1, source_target_pairs={{32,0},{34,2},{36,4},{38,6},{40,8},{42,10},{44,12},{46,14},{48,16}... | collective-permute-start | bytes 786440 | tf_op jit(solution)/shard_map/ppermute | solution.py:31
  171.7 5.2 %copy-start.14 = (bf16[2,384,4,128]{3,1,2,0:T(8,128)(2,1)}, bf16[2,384,4,128]{3,1,2,0:T(8,128)(2,1)S(1)}, u32[]{:S(2)}) copy-start(bf16[2,384,4,128]{3,1,2,0:T(8,128)(2,1)S(1)} %get-tuple-element.38) | copy-start | bytes 2359300
  171.7 14.0 %collective-permute-start.14 = (bf16[2,128,4,128]{3,1,2,0:T(8,128)(2,1)}, bf16[2,128,4,128]{3,1,2,0:T(8,128)(2,1)}, u32[]{:S(2)}, u32[]{:S(2)}) collective-permute-start(bf16[2,128,4,128]{3,1,2,0:T(8,128)(2,1)} %get-tuple-element.37), channel_id=1, source_target_pairs={{0,8},{2,10},{4,12},{6,14},{8,0},{10,2},{12,4},{14,6},{16,24},{18,... | collective-permute-start | bytes 786440 | tf_op jit(solution)/shard_map/ppermute | solution.py:12
  178.0 9.7 %copy-start.48 = (pred[384]{0:T(512)(128)(4,1)S(1)}, pred[384]{0:T(512)(128)(4,1)}, u32[]{:S(2)}) copy-start(pred[384]{0:T(512)(128)(4,1)} %fusion.111) | copy-start | bytes 1156
  178.7 7.0 %copy-start.15 = (bf16[2,384,4,128]{3,1,2,0:T(8,128)(2,1)S(1)}, bf16[2,384,4,128]{3,1,2,0:T(8,128)(2,1)}, u32[]{:S(2)}) copy-start(bf16[2,384,4,128]{3,1,2,0:T(8,128)(2,1)} %copy-done.14) | copy-start | bytes 2359300
  178.7 9.0 %copy-start.30 = (f32[32,4,128]{2,1,0:T(4,128)S(1)}, f32[32,4,128]{2,1,0:T(4,128)}, u32[]{:S(2)}) copy-start(f32[32,4,128]{2,1,0:T(4,128)} %bitcast_reduce_fusion.11) | copy-start | bytes 196612
  183.7 4.4 %copy-start.17 = (bf16[2,384,4,128]{3,1,2,0:T(8,128)(2,1)}, bf16[2,384,4,128]{3,1,2,0:T(8,128)(2,1)S(1)}, u32[]{:S(2)}) copy-start(bf16[2,384,4,128]{3,1,2,0:T(8,128)(2,1)S(1)} %get-tuple-element.40) | copy-start | bytes 2359300
  183.7 9.9 %copy-start.32 = (f32[16,4,128]{2,1,0:T(4,128)S(1)}, f32[16,4,128]{2,1,0:T(4,128)}, u32[]{:S(2)}) copy-start(f32[16,4,128]{2,1,0:T(4,128)} %bitcast_reduce_fusion.10) | copy-start | bytes 98308
  183.7 9.9 %copy-start.44 = (pred[384]{0:T(512)(128)(4,1)S(1)}, pred[384]{0:T(512)(128)(4,1)}, u32[]{:S(2)}) copy-start(pred[384]{0:T(512)(128)(4,1)} %fusion.110) | copy-start | bytes 1156
  183.7 8.2 %collective-permute-start.18 = (bf16[2,128,4,128]{3,1,2,0:T(8,128)(2,1)}, bf16[2,128,4,128]{3,1,2,0:T(8,128)(2,1)}, u32[]{:S(2)}, u32[]{:S(2)}) collective-permute-start(bf16[2,128,4,128]{3,1,2,0:T(8,128)(2,1)} %get-tuple-element.39), channel_id=1, source_target_pairs={{0,16},{2,18},{4,20},{6,22},{8,24},{10,26},{12,28},{14,30},{16,0},... | collective-permute-start | bytes 786440 | tf_op jit(solution)/shard_map/ppermute | solution.py:12
  233.2 1.3 copy-start.33
  233.2 1.3 copy-start.47
  242.4 1.3 copy-start.46
  242.4 1.3 copy-start.51
  244.0 5.7 %copy-start.40 = (f32[4,2]{1,0:T(4,128)}, f32[4,2]{1,0:T(4,128)S(1)}, u32[]{:S(2)}) copy-start(f32[4,2]{1,0:T(4,128)S(1)} %get-tuple-element.51) | copy-start | bytes 100
  253.9 1.3 copy-start.43
  253.9 1.3 copy-start.50
  255.1 5.1 %copy-start.35 = (f32[4,4,128]{2,1,0:T(4,128)S(1)}, f32[4,4,128]{2,1,0:T(4,128)}, u32[]{:S(2)}) copy-start(f32[4,4,128]{2,1,0:T(4,128)} %copy-done.34) | copy-start | bytes 24580
  255.1 5.1 %copy-start.36 = (f32[4,4,128]{2,1,0:T(4,128)S(1)}, f32[4,4,128]{2,1,0:T(4,128)}, u32[]{:S(2)}) copy-start(f32[4,4,128]{2,1,0:T(4,128)} %fusion.1) | copy-start | bytes 24580
  260.2 1.5 copy-start.8
  260.2 1.5 copy-start.28
  260.2 1.5 copy-start.31
  260.2 1.5 copy-start.38
  260.2 1.5 copy-start.39
  260.2 1.5 copy-start.42
  (8 other events, 7.0 us)
Sparse Core Ops, SparseCore 0:
  24.3 170.2 all-gather.2

commit v4 on v3

--- a/solution.py
+++ b/solution.py
@@ -226,19 +226,25 @@
             )
         )
     coarse_list = [top_level - 2, top_level - 1, top_level]
-    wholes = gather_packed(tuple(pieces[level_index] for level_index in coarse_list), "seq", (1,) * len(coarse_list))
-    for position, level_index in enumerate(coarse_list):
+    lines = lax.all_gather(
+        jnp.concatenate([pieces[level_index].reshape(-1) for level_index in coarse_list]), "seq"
+    )
+    at = 0
+    for level_index in coarse_list:
         group = 1 << level_index - 2
         block_total = seq_count // group
-        whole_level = wholes[position].reshape(2, block_total, BLOCK, head_local, head_size)
+        rows = pieces[level_index].shape[1]
+        size = pieces[level_index].size
         block_index = device_index // group
         targets = slot_targets(block_index, level_index)
-        chosen = [
-            lax.dynamic_index_in_dim(
-                whole_level, jnp.clip(target, 0, block_total - 1), axis=1, keepdims=False
+        chosen = []
+        for target in targets:
+            part = lax.dynamic_slice_in_dim(
+                lines, jnp.clip(target, 0, block_total - 1) * group, group, axis=0
             )
-            for target in targets
-        ]
+            part = part[:, at : at + size].reshape(group, 2, rows, head_local, head_size)
+            chosen.append(jnp.moveaxis(part, 1, 0).reshape(2, group * rows, head_local, head_size))
+        at += size
         level_keys = jnp.concatenate(chosen, axis=1)[:, None]
         valid = slot_masks(jnp.reshape(block_index, (1,)), block_total, level_index, BLOCK)
         results.append(

time: 296 us -> 282 us (0.953)
  the two profiles are of different devices: /device:TPU:265 before, /device:TPU:207 now
where the time goes in v4:
time: 282 us; the launch traced here: 279 us
  starting transfers between devices  95.3 us (34%)
  local copies, waits for them, and re-layouts  72.2 us (26%)
  other arithmetic  62.6 us (22%)
  matrix products  17 us (6%)
  between operations  14.8 us (5%)
  waiting for transfers between devices  10.5 us (4%)
  blocking collectives  6.79 us (2%)
    ppermute x8, starting transfers between devices, shifted(): lax.ppermute(value, axis, [(source, source + steps) for source in range(i...  46.4 us
    ppermute x7, starting transfers between devices, partner_2(): return lax.ppermute(value, axis, pairs)  36.5 us
    reduce_sum x24, other arithmetic, coarsen(): summed = jnp.sum(grouped, axis=1)  12.2 us
    concatenate x21, local copies, waits for them, and re-layouts, slot_masks(): jnp.concatenate([jnp.repeat(((target >= 0) & (target < block_total))[:, N...  11.9 us
    all_gather x1, local copies, waits for them, and re-layouts, per_device(): lax.all_gather(jnp.concatenate([pieces[level_index].reshape(-1) for level...  10.9 us
    ppermute x7, waiting for transfers between devices, partner_2(): return lax.ppermute(value, axis, pairs)  10.4 us
    dot_general x9, matrix products, level_attend(): jnp.einsum('nhqk,nkhd->nqhd', weights.astype(jnp.bfloat16), value_blocks,...  10.1 us
    concatenate x9, other arithmetic, slot_masks(): jnp.concatenate([jnp.repeat(((target >= 0) & (target < block_total))[:, N...  9.56 us
  transfers between devices with their start and end apart: 20, of which 2 were waited for; matrix products, arithmetic and copies ran while one was open for 33% of the time, Pallas kernels for 0%

profile of v4, /device:TPU:207, one launch (start us, length us, event | category | flops | bytes accessed | tf_op | source)
XLA Modules:
  0.0 279.1 jit_solution(13980980734136998416)
XLA Ops:
  6.5 1.6 bitcast_reduce_fusion.19
  8.2 1.4 bitcast_reduce_fusion.20
  10.4 5.2 %collective-permute-start.5 = (bf16[2,128,4,128]{3,1,2,0:T(8,128)(2,1)}, bf16[2,128,4,128]{3,1,2,0:T(8,128)(2,1)}, u32[]{:S(2)}, u32[]{:S(2)}) collective-permute-start(bf16[2,128,4,128]{3,1,2,0:T(8,128)(2,1)} %pad_maximum_fusion.9), channel_id=1, source_target_pairs={{4,0},{6,2},{8,4},{10,6},{12,8},{14,10},{16,12},{18,14},{20,16},{2... | collective-permute-start | bytes 786440 | tf_op jit(solution)/shard_map/ppermute | solution.py:31
  15.6 1.9 collective-permute-start.4
  21.9 3.0 %collective-permute-start.7 = (bf16[2,112,4,128]{3,1,2,0:T(8,128)(2,1)}, bf16[2,112,4,128]{3,1,2,0:T(8,128)(2,1)}, u32[]{:S(2)}, u32[]{:S(2)}) collective-permute-start(bf16[2,112,4,128]{3,1,2,0:T(8,128)(2,1)} %maximum_maximum_fusion.1), channel_id=1, source_target_pairs={{0,2},{2,0},{4,6},{6,4},{8,10},{10,8},{12,14},{14,12},{16,18},{18,... | collective-permute-start | bytes 688136 | tf_op jit(solution)/shard_map/ppermute | solution.py:12
  25.8 1.2 pad_maximum_fusion.6
  27.0 2.3 collective-permute-start.3
  31.1 3.3 %collective-permute-start = (bf16[2,128,4,128]{3,1,2,0:T(8,128)(2,1)}, bf16[2,128,4,128]{3,1,2,0:T(8,128)(2,1)}, u32[]{:S(2)}, u32[]{:S(2)}) collective-permute-start(bf16[2,128,4,128]{3,1,2,0:T(8,128)(2,1)} %get-tuple-element.33), channel_id=1, source_target_pairs={{0,2},{2,4},{4,6},{6,8},{8,10},{10,12},{12,14},{14,16},{16,18},{18... | collective-permute-start | bytes 786440 | tf_op jit(solution)/shard_map/ppermute | solution.py:22
  35.3 1.3 bitcast_reduce_fusion.1
  57.2 1.3 fusion.112
  58.5 1.3 fusion.111
  59.7 1.3 fusion.110
  61.0 1.3 fusion.109
  62.3 1.2 fusion.108
  63.6 1.2 fusion.107
  64.8 4.9 %collective-permute-start.1 = (bf16[2,128,4,128]{3,1,2,0:T(8,128)(2,1)}, bf16[2,128,4,128]{3,1,2,0:T(8,128)(2,1)S(1)}, u32[]{:S(2)}, u32[]{:S(2)}) collective-permute-start(bf16[2,128,4,128]{3,1,2,0:T(8,128)(2,1)} %get-tuple-element.34), channel_id=1, source_target_pairs={{2,0},{4,2},{6,4},{8,6},{10,8},{12,10},{14,12},{16,14},{18,16},{20... | collective-permute-start | bytes 786440 | tf_op jit(solution)/shard_map/ppermute | solution.py:23
  73.1 1.9 collective-permute-start.2
  76.0 4.4 %collective-permute-start.9 = (bf16[2,128,4,128]{3,1,2,0:T(8,128)(2,1)S(1)}, bf16[2,128,4,128]{3,1,2,0:T(8,128)(2,1)S(1)}, u32[]{:S(2)}, u32[]{:S(2)}) collective-permute-start(bf16[2,128,4,128]{3,1,2,0:T(8,128)(2,1)S(1)} %pad_maximum_fusion.10), channel_id=1, source_target_pairs={{8,0},{10,2},{12,4},{14,6},{16,8},{18,10},{20,12},{22,14},{24,16},... | collective-permute-start | bytes 786440 | tf_op jit(solution)/shard_map/ppermute | solution.py:31
  80.4 5.2 %collective-permute-start.8 = (bf16[2,128,4,128]{3,1,2,0:T(8,128)(2,1)S(1)}, bf16[2,128,4,128]{3,1,2,0:T(8,128)(2,1)S(1)}, u32[]{:S(2)}, u32[]{:S(2)}) collective-permute-start(bf16[2,128,4,128]{3,1,2,0:T(8,128)(2,1)S(1)} %pad_maximum_fusion.10), channel_id=1, source_target_pairs={{0,8},{2,10},{4,12},{6,14},{8,16},{10,18},{12,20},{14,22},{16,24},... | collective-permute-start | bytes 786440 | tf_op jit(solution)/shard_map/ppermute | solution.py:31
  85.6 1.1 pad_maximum_fusion.1
  89.3 1.6 fusion.12
  90.9 1.4 fusion.1
  92.3 15.1 %collective-permute-start.11 = (bf16[2,96,4,128]{3,1,2,0:T(8,128)(2,1)S(1)}, bf16[2,96,4,128]{3,1,2,0:T(8,128)(2,1)S(1)}, u32[]{:S(2)}, u32[]{:S(2)}) collective-permute-start(bf16[2,96,4,128]{3,1,2,0:T(8,128)(2,1)S(1)} %pad_maximum_fusion.13), channel_id=1, source_target_pairs={{0,4},{2,6},{4,0},{6,2},{8,12},{10,14},{12,8},{14,10},{16,20},{18,... | collective-permute-start | bytes 589832 | tf_op jit(solution)/shard_map/ppermute | solution.py:12
  107.5 1.1 broadcast_select_fusion.3
  108.6 1.1 copy.374
  109.6 4.0 %collective-permute-done.11 = bf16[2,96,4,128]{3,1,2,0:T(8,128)(2,1)S(1)} collective-permute-done((bf16[2,96,4,128]{3,1,2,0:T(8,128)(2,1)S(1)}, bf16[2,96,4,128]{3,1,2,0:T(8,128)(2,1)S(1)}, u32[]{:S(2)}, u32[]{:S(2)}) %collective-permute-start.11) | collective-permute-done | bytes 196640 | tf_op jit(solution)/shard_map/ppermute | solution.py:12
  113.6 1.9 collective-permute-start.6
  117.0 13.0 %collective-permute-start.13 = (bf16[2,128,4,128]{3,1,2,0:T(8,128)(2,1)}, bf16[2,128,4,128]{3,1,2,0:T(8,128)(2,1)}, u32[]{:S(2)}, u32[]{:S(2)}) collective-permute-start(bf16[2,128,4,128]{3,1,2,0:T(8,128)(2,1)} %pad_maximum_fusion.11), channel_id=1, source_target_pairs={{16,0},{18,2},{20,4},{22,6},{24,8},{26,10},{28,12},{30,14},{32,16}... | collective-permute-start | bytes 786440 | tf_op jit(solution)/shard_map/ppermute | solution.py:31
  130.0 7.8 %collective-permute-start.12 = (bf16[2,128,4,128]{3,1,2,0:T(8,128)(2,1)}, bf16[2,128,4,128]{3,1,2,0:T(8,128)(2,1)}, u32[]{:S(2)}, u32[]{:S(2)}) collective-permute-start(bf16[2,128,4,128]{3,1,2,0:T(8,128)(2,1)} %pad_maximum_fusion.11), channel_id=1, source_target_pairs={{0,16},{2,18},{4,20},{6,22},{8,24},{10,26},{12,28},{14,30},{16,32}... | collective-permute-start | bytes 786440 | tf_op jit(solution)/shard_map/ppermute | solution.py:31
  138.7 3.5 %collective-permute-start.15 = (bf16[2,64,4,128]{3,1,2,0:T(8,128)(2,1)}, bf16[2,64,4,128]{3,1,2,0:T(8,128)(2,1)}, u32[]{:S(2)}, u32[]{:S(2)}) collective-permute-start(bf16[2,64,4,128]{3,1,2,0:T(8,128)(2,1)} %pad_maximum_fusion.14), channel_id=1, source_target_pairs={{0,8},{2,10},{4,12},{6,14},{8,0},{10,2},{12,4},{14,6},{16,24},{18,... | collective-permute-start | bytes 393224 | tf_op jit(solution)/shard_map/ppermute | solution.py:12
  142.2 5.0 %collective-permute-start.10 = (bf16[2,128,4,128]{3,1,2,0:T(8,128)(2,1)}, bf16[2,128,4,128]{3,1,2,0:T(8,128)(2,1)}, u32[]{:S(2)}, u32[]{:S(2)}) collective-permute-start(bf16[2,128,4,128]{3,1,2,0:T(8,128)(2,1)} %get-tuple-element.35), channel_id=1, source_target_pairs={{0,4},{2,6},{4,0},{6,2},{8,12},{10,14},{12,8},{14,10},{16,20},{18,... | collective-permute-start | bytes 786440 | tf_op jit(solution)/shard_map/ppermute | solution.py:12
  147.2 7.7 %pad_maximum_fusion.2 = bf16[2,768,4,128]{3,2,1,0:T(4,128)(2,1)S(1)} fusion(bf16[2,256,4,128]{3,2,1,0:T(4,128)(2,1)} %collective-permute-done.3, bf16[1,256,4,128]{3,2,1,0:T(4,128)(2,1)S(1)} %bitcast.528, bf16[1,256,4,128]{3,2,1,0:T(4,128)(2,1)S(1)} %copy-done.10, bf16[2,256,4,128]{3,2,1,0:T(4,128)(2,1)S(1)} %collective-permute-done.2), kind=kLoop, calls=%fused_computation.11 | loop fusion | flops 2359296 | bytes 3145728 | tf_op jit(solution)/shard_map/concatenate | solution.py:24
  163.5 1.6 pad_maximum_fusion.12
  165.2 1.9 collective-permute-start.17
  167.1 7.0 %collective-permute-start.16 = (bf16[2,128,4,128]{3,1,2,0:T(8,128)(2,1)}, bf16[2,128,4,128]{3,1,2,0:T(8,128)(2,1)}, u32[]{:S(2)}, u32[]{:S(2)}) collective-permute-start(bf16[2,128,4,128]{3,1,2,0:T(8,128)(2,1)} %pad_maximum_fusion.12), channel_id=1, source_target_pairs={{0,32},{2,34},{4,36},{6,38},{8,40},{10,42},{12,44},{14,46},{16,48}... | collective-permute-start | bytes 786440 | tf_op jit(solution)/shard_map/ppermute | solution.py:31
  175.1 1.9 broadcast_select_fusion.1
  176.9 6.0 %collective-permute-start.14 = (bf16[2,128,4,128]{3,1,2,0:T(8,128)(2,1)}, bf16[2,128,4,128]{3,1,2,0:T(8,128)(2,1)}, u32[]{:S(2)}, u32[]{:S(2)}) collective-permute-start(bf16[2,128,4,128]{3,1,2,0:T(8,128)(2,1)} %get-tuple-element.37), channel_id=1, source_target_pairs={{0,8},{2,10},{4,12},{6,14},{8,0},{10,2},{12,4},{14,6},{16,24},{18,... | collective-permute-start | bytes 786440 | tf_op jit(solution)/shard_map/ppermute | solution.py:12
  182.9 1.7 constant_dynamic-update-slice_fusion.3
  184.6 1.4 fusion.139
  187.9 1.3 convolution_bitcast_fusion.2
  190.2 1.8 broadcast_select_fusion
  192.0 2.0 collective-permute-start.18
  194.1 6.4 %collective-permute-done.14 = bf16[2,128,4,128]{3,1,2,0:T(8,128)(2,1)} collective-permute-done((bf16[2,128,4,128]{3,1,2,0:T(8,128)(2,1)}, bf16[2,128,4,128]{3,1,2,0:T(8,128)(2,1)}, u32[]{:S(2)}, u32[]{:S(2)}) %collective-permute-start.14) | collective-permute-done | bytes 262176 | tf_op jit(solution)/shard_map/ppermute | solution.py:12
  204.5 1.9 convolution_bitcast_fusion.3
  206.4 1.7 constant_dynamic-update-slice_fusion.9
  208.1 1.3 fusion.137
  211.1 1.8 convolution_bitcast_fusion.4
  213.0 10.9 %reshape.1372 = bf16[256,14336]{1,0:T(8,128)(2,1)} reshape(bf16[3670016]{0:T(1024)(128)(2,1)} %all-gather.3.cloned.1.call-done) | data formatting | bytes 14680064 | tf_op jit(solution)/shard_map/all_gather | solution.py:229
  223.9 2.0 fusion.127
  225.8 1.1 reshape.1323
  227.9 1.1 reshape.1327
  230.3 1.1 pad_maximum_fusion.5
  233.9 1.9 fusion.128
  235.9 1.1 reshape.1312
  237.8 1.1 reshape.1316
  240.0 1.1 pad_maximum_fusion.4
  243.1 1.8 constant_dynamic-slice_fusion.2
  244.9 1.8 reshape.1301
  246.7 1.7 copy.506
  250.1 1.1 copy_bitcast_fusion.8
  257.1 3.6 %fusion.24 = bf16[512,4,128]{2,0,1:T(8,128)(2,1)S(1)} fusion(f32[4,128,4,128]{3,1,0,2:T(8,128)S(1)} %copy-done.8, f32[512,4,128]{2,0,1:T(8,128)S(1)} %bitcast.525, f32[512,4,128]{2,0,1:T(8,128)S(1)} %bitcast.526, f32[512,4]{0,1:T(4,128)S(1)} %get-tuple-element.5, f32[2,4,128]{2,0,1:T(2,128)S(1)} %copy-done.40, f32[512,4]{0,1:T(4,128)S(1)} %get-tuple-element.12, ...), kind=kLoop, calls=%fused_computation.50 | loop fusion | flops 4980736 | bytes 4009984 | tf_op jit(solution)/shard_map/convert_element_type | solution.py:282
  260.7 1.3 bitcast_convert_fusion
  262.2 6.8 %all_to_all.5 = bf16[2,512,1024]{2,1,0:T(8,128)(2,1)} all-to-all(bf16[2,512,1024]{2,1,0:T(8,128)(2,1)S(1)} %bitcast.522), channel_id=1, replica_groups=mesh['seq'=256,'head'=2] {'head'}, dimensions={0} | all-to-all | bytes 4194304 | tf_op jit(solution)/shard_map/all_to_all | solution.py:58
  269.0 3.3 %reduce_sum.342 = bf16[512,1024]{1,0:T(8,128)(2,1)} reduce(bf16[2,512,1024]{2,1,0:T(8,128)(2,1)} %all_to_all.5, bf16[]{:T(256)} %constant.307.clone.1), dimensions={0}, to_apply=%region_42.43 | reduce | flops 524288 | bytes 3145730 | tf_op jit(solution)/shard_map/reduce_sum | solution.py:59
  (323 shorter events, 72.4 us)
Async XLA Ops:
  6.5 254.1 %copy-start = (bf16[4,128,2048]{2,1,0:T(8,128)(2,1)S(1)}, bf16[4,128,2048]{2,1,0:T(8,128)(2,1)}, u32[]{:S(2)}) copy-start(bf16[4,128,2048]{2,1,0:T(8,128)(2,1)} %param.7) | copy-start | bytes 6291460
  6.5 11.0 %copy-start.1 = (bf16[512,4,128]{2,1,0:T(4,128)(2,1)S(1)}, bf16[512,4,128]{2,1,0:T(4,128)(2,1)}, u32[]{:S(2)}) copy-start(bf16[512,4,128]{2,1,0:T(4,128)(2,1)} %param.6) | copy-start | bytes 1572868
  6.5 11.3 %copy-start.2 = (bf16[512,4,128]{2,1,0:T(4,128)(2,1)S(1)}, bf16[512,4,128]{2,1,0:T(4,128)(2,1)}, u32[]{:S(2)}) copy-start(bf16[512,4,128]{2,1,0:T(4,128)(2,1)} %param.5) | copy-start | bytes 1572868
  6.5 206.4 %all-gather.3.cloned.1.call-start = ((), (), s32[]{:S(2)}) async-start(), calls=%async_computation.1 | async-start | bytes 7368704 | tf_op jit(solution)/shard_map/all_gather | solution.py:229
  10.4 82.0 %collective-permute-start.5 = (bf16[2,128,4,128]{3,1,2,0:T(8,128)(2,1)}, bf16[2,128,4,128]{3,1,2,0:T(8,128)(2,1)}, u32[]{:S(2)}, u32[]{:S(2)}) collective-permute-start(bf16[2,128,4,128]{3,1,2,0:T(8,128)(2,1)} %pad_maximum_fusion.9), channel_id=1, source_target_pairs={{4,0},{6,2},{8,4},{10,6},{12,8},{14,10},{16,12},{18,14},{20,16},{2... | collective-permute-start | bytes 786440 | tf_op jit(solution)/shard_map/ppermute | solution.py:31
  15.6 57.5 %collective-permute-start.4 = (bf16[2,128,4,128]{3,1,2,0:T(8,128)(2,1)}, bf16[2,128,4,128]{3,1,2,0:T(8,128)(2,1)}, u32[]{:S(2)}, u32[]{:S(2)}) collective-permute-start(bf16[2,128,4,128]{3,1,2,0:T(8,128)(2,1)} %pad_maximum_fusion.9), channel_id=1, source_target_pairs={{0,4},{2,6},{4,8},{6,10},{8,12},{10,14},{12,16},{14,18},{16,20},{1... | collective-permute-start | bytes 786440 | tf_op jit(solution)/shard_map/ppermute | solution.py:31
  21.9 42.9 %collective-permute-start.7 = (bf16[2,112,4,128]{3,1,2,0:T(8,128)(2,1)}, bf16[2,112,4,128]{3,1,2,0:T(8,128)(2,1)}, u32[]{:S(2)}, u32[]{:S(2)}) collective-permute-start(bf16[2,112,4,128]{3,1,2,0:T(8,128)(2,1)} %maximum_maximum_fusion.1), channel_id=1, source_target_pairs={{0,2},{2,0},{4,6},{6,4},{8,10},{10,8},{12,14},{14,12},{16,18},{18,... | collective-permute-start | bytes 688136 | tf_op jit(solution)/shard_map/ppermute | solution.py:12
  25.8 1.2 copy-start.9
  27.0 111.6 %collective-permute-start.3 = (bf16[2,256,4,128]{3,2,1,0:T(4,128)(2,1)}, bf16[2,256,4,128]{3,2,1,0:T(4,128)(2,1)}, u32[]{:S(2)}, u32[]{:S(2)}) collective-permute-start(bf16[2,256,4,128]{3,2,1,0:T(4,128)(2,1)} %pad_maximum_fusion.6), channel_id=1, source_target_pairs={{2,0},{4,2},{6,4},{8,6},{10,8},{12,10},{14,12},{16,14},{18,16},{20... | collective-permute-start | bytes 1572872 | tf_op jit(solution)/shard_map/ppermute | solution.py:23
  29.5 1.6 copy-start.6
  29.5 7.1 %copy-start.3 = (bf16[512,4,128]{2,1,0:T(4,128)(2,1)S(1)}, bf16[512,4,128]{2,1,0:T(4,128)(2,1)}, u32[]{:S(2)}) copy-start(bf16[512,4,128]{2,1,0:T(4,128)(2,1)} %param.4) | copy-start | bytes 1572868
  31.1 44.9 %collective-permute-start = (bf16[2,128,4,128]{3,1,2,0:T(8,128)(2,1)}, bf16[2,128,4,128]{3,1,2,0:T(8,128)(2,1)}, u32[]{:S(2)}, u32[]{:S(2)}) collective-permute-start(bf16[2,128,4,128]{3,1,2,0:T(8,128)(2,1)} %get-tuple-element.33), channel_id=1, source_target_pairs={{0,2},{2,4},{4,6},{6,8},{8,10},{10,12},{12,14},{14,16},{16,18},{18... | collective-permute-start | bytes 786440 | tf_op jit(solution)/shard_map/ppermute | solution.py:22
  43.5 42.0 %copy-start.5 = (bf16[1,512,4,128]{3,1,2,0:T(8,128)(2,1)S(1)}, bf16[1,512,4,128]{3,1,2,0:T(8,128)(2,1)}, u32[]{:S(2)}) copy-start(bf16[1,512,4,128]{3,1,2,0:T(8,128)(2,1)} %copy-done.4) | copy-start | bytes 1572868
  56.4 29.1 %copy-start.7 = (bf16[1,512,4,128]{3,1,2,0:T(8,128)(2,1)S(1)}, bf16[1,512,4,128]{3,1,2,0:T(8,128)(2,1)}, u32[]{:S(2)}) copy-start(bf16[1,512,4,128]{3,1,2,0:T(8,128)(2,1)} %copy-done.6) | copy-start | bytes 1572868
  64.8 15.6 %collective-permute-start.1 = (bf16[2,128,4,128]{3,1,2,0:T(8,128)(2,1)}, bf16[2,128,4,128]{3,1,2,0:T(8,128)(2,1)S(1)}, u32[]{:S(2)}, u32[]{:S(2)}) collective-permute-start(bf16[2,128,4,128]{3,1,2,0:T(8,128)(2,1)} %get-tuple-element.34), channel_id=1, source_target_pairs={{2,0},{4,2},{6,4},{8,6},{10,8},{12,10},{14,12},{16,14},{18,16},{20... | collective-permute-start | bytes 786440 | tf_op jit(solution)/shard_map/ppermute | solution.py:23
  70.5 45.1 %copy-start.23 = (bf16[2,16,4,128]{3,1,2,0:T(8,128)(2,1)}, bf16[2,16,4,128]{3,1,2,0:T(8,128)(2,1)S(1)}, u32[]{:S(2)}) copy-start(bf16[2,16,4,128]{3,1,2,0:T(8,128)(2,1)S(1)} %slice.191) | copy-start | bytes 98308
  73.1 69.1 %collective-permute-start.2 = (bf16[2,256,4,128]{3,2,1,0:T(4,128)(2,1)}, bf16[2,256,4,128]{3,2,1,0:T(4,128)(2,1)S(1)}, u32[]{:S(2)}, u32[]{:S(2)}) collective-permute-start(bf16[2,256,4,128]{3,2,1,0:T(4,128)(2,1)} %pad_maximum_fusion.6), channel_id=1, source_target_pairs={{0,2},{2,4},{4,6},{6,8},{8,10},{10,12},{12,14},{14,16},{16,18},{18... | collective-permute-start | bytes 1572872 | tf_op jit(solution)/shard_map/ppermute | solution.py:22
  76.0 54.0 %collective-permute-start.9 = (bf16[2,128,4,128]{3,1,2,0:T(8,128)(2,1)S(1)}, bf16[2,128,4,128]{3,1,2,0:T(8,128)(2,1)S(1)}, u32[]{:S(2)}, u32[]{:S(2)}) collective-permute-start(bf16[2,128,4,128]{3,1,2,0:T(8,128)(2,1)S(1)} %pad_maximum_fusion.10), channel_id=1, source_target_pairs={{8,0},{10,2},{12,4},{14,6},{16,8},{18,10},{20,12},{22,14},{24,16},... | collective-permute-start | bytes 786440 | tf_op jit(solution)/shard_map/ppermute | solution.py:31
  80.4 36.6 %collective-permute-start.8 = (bf16[2,128,4,128]{3,1,2,0:T(8,128)(2,1)S(1)}, bf16[2,128,4,128]{3,1,2,0:T(8,128)(2,1)S(1)}, u32[]{:S(2)}, u32[]{:S(2)}) collective-permute-start(bf16[2,128,4,128]{3,1,2,0:T(8,128)(2,1)S(1)} %pad_maximum_fusion.10), channel_id=1, source_target_pairs={{0,8},{2,10},{4,12},{6,14},{8,16},{10,18},{12,20},{14,22},{16,24},... | collective-permute-start | bytes 786440 | tf_op jit(solution)/shard_map/ppermute | solution.py:31
  89.3 1.6 copy-start.33
  92.3 23.2 %copy-start.26 = (bf16[16,4,128]{2,0,1:T(8,128)(2,1)S(1)}, bf16[16,4,128]{2,0,1:T(8,128)(2,1)}, u32[]{:S(2)}) copy-start(bf16[16,4,128]{2,0,1:T(8,128)(2,1)} %copy-done.25) | copy-start | bytes 49156
  92.3 21.2 %collective-permute-start.11 = (bf16[2,96,4,128]{3,1,2,0:T(8,128)(2,1)S(1)}, bf16[2,96,4,128]{3,1,2,0:T(8,128)(2,1)S(1)}, u32[]{:S(2)}, u32[]{:S(2)}) collective-permute-start(bf16[2,96,4,128]{3,1,2,0:T(8,128)(2,1)S(1)} %pad_maximum_fusion.13), channel_id=1, source_target_pairs={{0,4},{2,6},{4,0},{6,2},{8,12},{10,14},{12,8},{14,10},{16,20},{18,... | collective-permute-start | bytes 589832 | tf_op jit(solution)/shard_map/ppermute | solution.py:12
  108.6 7.7 %copy-start.19 = (bf16[1,32,4,128]{3,1,2,0:T(8,128)(2,1)S(1)}, bf16[1,32,4,128]{3,1,2,0:T(8,128)(2,1)}, u32[]{:S(2)}) copy-start(bf16[1,32,4,128]{3,1,2,0:T(8,128)(2,1)} %copy-done.18) | copy-start | bytes 98308
  108.6 7.7 %copy-start.21 = (bf16[32,4,128]{2,0,1:T(8,128)(2,1)S(1)}, bf16[32,4,128]{2,0,1:T(8,128)(2,1)}, u32[]{:S(2)}) copy-start(bf16[32,4,128]{2,0,1:T(8,128)(2,1)} %copy-done.20) | copy-start | bytes 98308
  109.6 37.6 %copy-start.10 = (bf16[1,256,4,128]{3,2,1,0:T(4,128)(2,1)S(1)}, bf16[1,256,4,128]{3,2,1,0:T(4,128)(2,1)}, u32[]{:S(2)}) copy-start(bf16[1,256,4,128]{3,2,1,0:T(4,128)(2,1)} %copy-done.9) | copy-start | bytes 786436
  113.6 41.6 %collective-permute-start.6 = (bf16[2,128,4,128]{3,1,2,0:T(8,128)(2,1)S(1)}, bf16[2,128,4,128]{3,1,2,0:T(8,128)(2,1)S(1)}, u32[]{:S(2)}, u32[]{:S(2)}) collective-permute-start(bf16[2,128,4,128]{3,1,2,0:T(8,128)(2,1)S(1)} %get-tuple-element.41), channel_id=1, source_target_pairs={{0,2},{2,0},{4,6},{6,4},{8,10},{10,8},{12,14},{14,12},{16,18},{18,... | collective-permute-start | bytes 786440 | tf_op jit(solution)/shard_map/ppermute | solution.py:12
  117.0 58.1 %collective-permute-start.13 = (bf16[2,128,4,128]{3,1,2,0:T(8,128)(2,1)}, bf16[2,128,4,128]{3,1,2,0:T(8,128)(2,1)}, u32[]{:S(2)}, u32[]{:S(2)}) collective-permute-start(bf16[2,128,4,128]{3,1,2,0:T(8,128)(2,1)} %pad_maximum_fusion.11), channel_id=1, source_target_pairs={{16,0},{18,2},{20,4},{22,6},{24,8},{26,10},{28,12},{30,14},{32,16}... | collective-permute-start | bytes 786440 | tf_op jit(solution)/shard_map/ppermute | solution.py:31
  130.0 44.1 %collective-permute-start.12 = (bf16[2,128,4,128]{3,1,2,0:T(8,128)(2,1)}, bf16[2,128,4,128]{3,1,2,0:T(8,128)(2,1)}, u32[]{:S(2)}, u32[]{:S(2)}) collective-permute-start(bf16[2,128,4,128]{3,1,2,0:T(8,128)(2,1)} %pad_maximum_fusion.11), channel_id=1, source_target_pairs={{0,16},{2,18},{4,20},{6,22},{8,24},{10,26},{12,28},{14,30},{16,32}... | collective-permute-start | bytes 786440 | tf_op jit(solution)/shard_map/ppermute | solution.py:31
  138.7 3.5 %copy-start.11 = (bf16[2,384,4,128]{3,1,2,0:T(8,128)(2,1)}, bf16[2,384,4,128]{3,1,2,0:T(8,128)(2,1)S(1)}, u32[]{:S(2)}) copy-start(bf16[2,384,4,128]{3,1,2,0:T(8,128)(2,1)S(1)} %get-tuple-element.36) | copy-start | bytes 2359300
  138.7 24.9 %collective-permute-start.15 = (bf16[2,64,4,128]{3,1,2,0:T(8,128)(2,1)}, bf16[2,64,4,128]{3,1,2,0:T(8,128)(2,1)}, u32[]{:S(2)}, u32[]{:S(2)}) collective-permute-start(bf16[2,64,4,128]{3,1,2,0:T(8,128)(2,1)} %pad_maximum_fusion.14), channel_id=1, source_target_pairs={{0,8},{2,10},{4,12},{6,14},{8,0},{10,2},{12,4},{14,6},{16,24},{18,... | collective-permute-start | bytes 393224 | tf_op jit(solution)/shard_map/ppermute | solution.py:12
  142.2 40.7 %collective-permute-start.10 = (bf16[2,128,4,128]{3,1,2,0:T(8,128)(2,1)}, bf16[2,128,4,128]{3,1,2,0:T(8,128)(2,1)}, u32[]{:S(2)}, u32[]{:S(2)}) collective-permute-start(bf16[2,128,4,128]{3,1,2,0:T(8,128)(2,1)} %get-tuple-element.35), channel_id=1, source_target_pairs={{0,4},{2,6},{4,0},{6,2},{8,12},{10,14},{12,8},{14,10},{16,20},{18,... | collective-permute-start | bytes 786440 | tf_op jit(solution)/shard_map/ppermute | solution.py:12
  154.9 1.0 copy-start.16
  156.7 1.0 copy-start.28
  156.7 1.0 copy-start.47
  160.7 2.8 %copy-start.24 = (bf16[2,16,4,128]{3,1,2,0:T(8,128)(2,1)S(1)}, bf16[2,16,4,128]{3,1,2,0:T(8,128)(2,1)}, u32[]{:S(2)}) copy-start(bf16[2,16,4,128]{3,1,2,0:T(8,128)(2,1)} %copy-done.23) | copy-start | bytes 98308
  162.7 21.9 %copy-start.22 = (f32[64,4,128]{2,1,0:T(4,128)S(1)}, f32[64,4,128]{2,1,0:T(4,128)}, u32[]{:S(2)}) copy-start(f32[64,4,128]{2,1,0:T(4,128)} %bitcast_reduce_fusion.18) | copy-start | bytes 393220
  162.7 21.9 %copy-start.43 = (pred[384]{0:T(512)(128)(4,1)S(1)}, pred[384]{0:T(512)(128)(4,1)}, u32[]{:S(2)}) copy-start(pred[384]{0:T(512)(128)(4,1)} %fusion.112) | copy-start | bytes 1156
  165.2 25.0 %collective-permute-start.17 = (bf16[2,128,4,128]{3,1,2,0:T(8,128)(2,1)}, bf16[2,128,4,128]{3,1,2,0:T(8,128)(2,1)}, u32[]{:S(2)}, u32[]{:S(2)}) collective-permute-start(bf16[2,128,4,128]{3,1,2,0:T(8,128)(2,1)} %pad_maximum_fusion.12), channel_id=1, source_target_pairs={{32,0},{34,2},{36,4},{38,6},{40,8},{42,10},{44,12},{46,14},{48,16}... | collective-permute-start | bytes 786440 | tf_op jit(solution)/shard_map/ppermute | solution.py:31
  167.1 22.1 %collective-permute-start.16 = (bf16[2,128,4,128]{3,1,2,0:T(8,128)(2,1)}, bf16[2,128,4,128]{3,1,2,0:T(8,128)(2,1)}, u32[]{:S(2)}, u32[]{:S(2)}) collective-permute-start(bf16[2,128,4,128]{3,1,2,0:T(8,128)(2,1)} %pad_maximum_fusion.12), channel_id=1, source_target_pairs={{0,32},{2,34},{4,36},{6,38},{8,40},{10,42},{12,44},{14,46},{16,48}... | collective-permute-start | bytes 786440 | tf_op jit(solution)/shard_map/ppermute | solution.py:31
  176.9 6.0 %copy-start.12 = (bf16[2,384,4,128]{3,1,2,0:T(8,128)(2,1)}, bf16[2,384,4,128]{3,1,2,0:T(8,128)(2,1)S(1)}, u32[]{:S(2)}) copy-start(bf16[2,384,4,128]{3,1,2,0:T(8,128)(2,1)S(1)} %get-tuple-element.38) | copy-start | bytes 2359300
  176.9 23.5 %collective-permute-start.14 = (bf16[2,128,4,128]{3,1,2,0:T(8,128)(2,1)}, bf16[2,128,4,128]{3,1,2,0:T(8,128)(2,1)}, u32[]{:S(2)}, u32[]{:S(2)}) collective-permute-start(bf16[2,128,4,128]{3,1,2,0:T(8,128)(2,1)} %get-tuple-element.37), channel_id=1, source_target_pairs={{0,8},{2,10},{4,12},{6,14},{8,0},{10,2},{12,4},{14,6},{16,24},{18,... | collective-permute-start | bytes 786440 | tf_op jit(solution)/shard_map/ppermute | solution.py:12
  187.1 15.3 %copy-start.46 = (pred[384]{0:T(512)(128)(4,1)S(1)}, pred[384]{0:T(512)(128)(4,1)}, u32[]{:S(2)}) copy-start(pred[384]{0:T(512)(128)(4,1)} %fusion.111) | copy-start | bytes 1156
  187.9 12.6 %copy-start.13 = (bf16[2,384,4,128]{3,1,2,0:T(8,128)(2,1)S(1)}, bf16[2,384,4,128]{3,1,2,0:T(8,128)(2,1)}, u32[]{:S(2)}) copy-start(bf16[2,384,4,128]{3,1,2,0:T(8,128)(2,1)} %copy-done.12) | copy-start | bytes 2359300
  187.9 14.6 %copy-start.29 = (f32[32,4,128]{2,1,0:T(4,128)S(1)}, f32[32,4,128]{2,1,0:T(4,128)}, u32[]{:S(2)}) copy-start(f32[32,4,128]{2,1,0:T(4,128)} %bitcast_reduce_fusion.11) | copy-start | bytes 196612
  192.0 10.8 %copy-start.15 = (bf16[2,384,4,128]{3,1,2,0:T(8,128)(2,1)}, bf16[2,384,4,128]{3,1,2,0:T(8,128)(2,1)S(1)}, u32[]{:S(2)}) copy-start(bf16[2,384,4,128]{3,1,2,0:T(8,128)(2,1)S(1)} %get-tuple-element.40) | copy-start | bytes 2359300
  192.0 16.1 %copy-start.31 = (f32[16,4,128]{2,1,0:T(4,128)S(1)}, f32[16,4,128]{2,1,0:T(4,128)}, u32[]{:S(2)}) copy-start(f32[16,4,128]{2,1,0:T(4,128)} %bitcast_reduce_fusion.10) | copy-start | bytes 98308
  192.0 16.1 %copy-start.42 = (pred[384]{0:T(512)(128)(4,1)S(1)}, pred[384]{0:T(512)(128)(4,1)}, u32[]{:S(2)}) copy-start(pred[384]{0:T(512)(128)(4,1)} %fusion.110) | copy-start | bytes 1156
  192.0 14.4 %collective-permute-start.18 = (bf16[2,128,4,128]{3,1,2,0:T(8,128)(2,1)}, bf16[2,128,4,128]{3,1,2,0:T(8,128)(2,1)}, u32[]{:S(2)}, u32[]{:S(2)}) collective-permute-start(bf16[2,128,4,128]{3,1,2,0:T(8,128)(2,1)} %get-tuple-element.39), channel_id=1, source_target_pairs={{0,16},{2,18},{4,20},{6,22},{8,24},{10,26},{12,28},{14,30},{16,0},... | collective-permute-start | bytes 786440 | tf_op jit(solution)/shard_map/ppermute | solution.py:12
  201.5 1.0 copy-start.14
  229.0 2.4 copy-start.44
  229.0 2.4 copy-start.49
  238.9 2.2 copy-start.41
  238.9 2.2 copy-start.48
  249.3 2.0 copy-start.17
  249.3 2.1 copy-start.32
  250.1 1.2 copy-start.45
  251.3 1.5 copy-start.38
  251.3 4.3 %copy-start.34 = (f32[4,4,128]{2,1,0:T(4,128)S(1)}, f32[4,4,128]{2,1,0:T(4,128)}, u32[]{:S(2)}) copy-start(f32[4,4,128]{2,1,0:T(4,128)} %copy-done.33) | copy-start | bytes 24580
  255.5 1.5 copy-start.8
  255.5 1.5 copy-start.27
  255.5 1.5 copy-start.30
  255.6 1.5 copy-start.35
  255.6 1.5 copy-start.36
  255.6 1.5 copy-start.40
  (6 other events, 4.7 us)
Sparse Core Ops, SparseCore 0:
  19.8 177.0 all-gather.2

commit v5 on v4

--- a/solution.py
+++ b/solution.py
@@ -227,14 +227,17 @@
         )
     coarse_list = [top_level - 2, top_level - 1, top_level]
     lines = lax.all_gather(
-        jnp.concatenate([pieces[level_index].reshape(-1) for level_index in coarse_list]), "seq"
+        jnp.concatenate(
+            [pieces[level_index].reshape(-1, head_size) for level_index in coarse_list]
+        ),
+        "seq",
     )
     at = 0
     for level_index in coarse_list:
         group = 1 << level_index - 2
         block_total = seq_count // group
         rows = pieces[level_index].shape[1]
-        size = pieces[level_index].size
+        size = pieces[level_index].size // head_size
         block_index = device_index // group
         targets = slot_targets(block_index, level_index)
         chosen = []

time: 282 us -> 251 us (0.89)
  the two profiles are of different devices: /device:TPU:207 before, /device:TPU:273 now
where the time goes in v5:
time: 251 us; the launch traced here: 249 us
  starting transfers between devices  87.6 us (35%)
  other arithmetic  59.3 us (24%)
  local copies, waits for them, and re-layouts  47.4 us (19%)
  matrix products  16.2 us (6%)
  between operations  14.9 us (6%)
  waiting for transfers between devices  13.6 us (5%)
  blocking collectives  10.1 us (4%)
    ppermute x8, starting transfers between devices, shifted(): lax.ppermute(value, axis, [(source, source + steps) for source in range(i...  38.4 us
    ppermute x7, starting transfers between devices, partner_2(): return lax.ppermute(value, axis, pairs)  35.9 us
    ppermute x7, waiting for transfers between devices, partner_2(): return lax.ppermute(value, axis, pairs)  13.5 us
    concatenate x21, local copies, waits for them, and re-layouts, slot_masks(): jnp.concatenate([jnp.repeat(((target >= 0) & (target < block_total))[:, N...  11.8 us
    reduce_sum x24, other arithmetic, coarsen(): summed = jnp.sum(grouped, axis=1)  11.1 us
    dot_general x9, matrix products, level_attend(): jnp.einsum('nhqk,nkhd->nqhd', weights.astype(jnp.bfloat16), value_blocks,...  10.2 us
    all_to_all x1, blocking collectives, summed_on_arrival(): lax.all_to_all(cut_along(value, dim, length), axis, 0, 0, tiled=True)  10.1 us
    unnamed x123, local copies, waits for them, and re-layouts  9.6 us
  transfers between devices with their start and end apart: 20, of which 2 were waited for; matrix products, arithmetic and copies ran while one was open for 36% of the time, Pallas kernels for 0%

profile of v5, /device:TPU:273, one launch (start us, length us, event | category | flops | bytes accessed | tf_op | source)
XLA Modules:
  0.0 249.0 jit_solution(2432363182477382706)
XLA Ops:
  6.5 1.6 bitcast_reduce_fusion.20
  8.2 1.4 bitcast_reduce_fusion.19
  10.4 5.4 %collective-permute-start.4 = (bf16[2,128,4,128]{3,1,2,0:T(8,128)(2,1)}, bf16[2,128,4,128]{3,1,2,0:T(8,128)(2,1)}, u32[]{:S(2)}, u32[]{:S(2)}) collective-permute-start(bf16[2,128,4,128]{3,1,2,0:T(8,128)(2,1)} %pad_maximum_fusion.9), channel_id=1, source_target_pairs={{0,4},{2,6},{4,8},{6,10},{8,12},{10,14},{12,16},{14,18},{16,20},{1... | collective-permute-start | bytes 786440 | tf_op jit(solution)/shard_map/ppermute | solution.py:31
  15.8 1.9 collective-permute-start.5
  22.1 2.3 collective-permute-start.7
  25.3 0.9 pad_maximum_fusion.8
  26.2 3.0 %collective-permute-start = (bf16[2,128,4,128]{3,1,2,0:T(8,128)(2,1)}, bf16[2,128,4,128]{3,1,2,0:T(8,128)(2,1)}, u32[]{:S(2)}, u32[]{:S(2)}) collective-permute-start(bf16[2,128,4,128]{3,1,2,0:T(8,128)(2,1)} %get-tuple-element.33), channel_id=1, source_target_pairs={{0,2},{2,4},{4,6},{6,8},{8,10},{10,12},{12,14},{14,16},{16,18},{18... | collective-permute-start | bytes 786440 | tf_op jit(solution)/shard_map/ppermute | solution.py:22
  29.2 5.1 %collective-permute-start.1 = (bf16[2,128,4,128]{3,1,2,0:T(8,128)(2,1)}, bf16[2,128,4,128]{3,1,2,0:T(8,128)(2,1)}, u32[]{:S(2)}, u32[]{:S(2)}) collective-permute-start(bf16[2,128,4,128]{3,1,2,0:T(8,128)(2,1)} %get-tuple-element.34), channel_id=1, source_target_pairs={{2,0},{4,2},{6,4},{8,6},{10,8},{12,10},{14,12},{16,14},{18,16},{20... | collective-permute-start | bytes 786440 | tf_op jit(solution)/shard_map/ppermute | solution.py:23
  36.1 1.2 pad_maximum_fusion.6
  37.3 0.9 bitcast_reduce_fusion.18
  40.5 1.0 bitcast_reduce_fusion.21
  57.1 1.3 fusion.112
  58.5 1.2 fusion.111
  59.6 1.2 fusion.110
  60.9 1.2 fusion.109
  62.1 1.2 fusion.108
  63.3 1.3 fusion.107
  65.3 1.9 collective-permute-start.2
  69.7 0.9 slice.188
  70.6 3.4 %collective-permute-start.3 = (bf16[2,256,4,128]{3,2,1,0:T(4,128)(2,1)}, bf16[2,256,4,128]{3,2,1,0:T(4,128)(2,1)S(1)}, u32[]{:S(2)}, u32[]{:S(2)}) collective-permute-start(bf16[2,256,4,128]{3,2,1,0:T(4,128)(2,1)} %pad_maximum_fusion.6), channel_id=1, source_target_pairs={{2,0},{4,2},{6,4},{8,6},{10,8},{12,10},{14,12},{16,14},{18,16},{20... | collective-permute-start | bytes 1572872 | tf_op jit(solution)/shard_map/ppermute | solution.py:23
  74.0 1.0 constant_dynamic-update-slice_fusion.2
  75.0 3.2 %collective-permute-start.8 = (bf16[2,128,4,128]{3,1,2,0:T(8,128)(2,1)S(1)}, bf16[2,128,4,128]{3,1,2,0:T(8,128)(2,1)S(1)}, u32[]{:S(2)}, u32[]{:S(2)}) collective-permute-start(bf16[2,128,4,128]{3,1,2,0:T(8,128)(2,1)S(1)} %pad_maximum_fusion.10), channel_id=1, source_target_pairs={{0,8},{2,10},{4,12},{6,14},{8,16},{10,18},{12,20},{14,22},{16,24},... | collective-permute-start | bytes 786440 | tf_op jit(solution)/shard_map/ppermute | solution.py:31
  78.3 10.4 %collective-permute-start.9 = (bf16[2,128,4,128]{3,1,2,0:T(8,128)(2,1)S(1)}, bf16[2,128,4,128]{3,1,2,0:T(8,128)(2,1)S(1)}, u32[]{:S(2)}, u32[]{:S(2)}) collective-permute-start(bf16[2,128,4,128]{3,1,2,0:T(8,128)(2,1)S(1)} %pad_maximum_fusion.10), channel_id=1, source_target_pairs={{8,0},{10,2},{12,4},{14,6},{16,8},{18,10},{20,12},{22,14},{24,16},... | collective-permute-start | bytes 786440 | tf_op jit(solution)/shard_map/ppermute | solution.py:31
  88.6 1.1 pad_maximum_fusion.1
  92.4 1.6 fusion.12
  94.0 1.4 fusion.1
  95.4 15.4 %collective-permute-start.11 = (bf16[2,96,4,128]{3,1,2,0:T(8,128)(2,1)S(1)}, bf16[2,96,4,128]{3,1,2,0:T(8,128)(2,1)S(1)}, u32[]{:S(2)}, u32[]{:S(2)}) collective-permute-start(bf16[2,96,4,128]{3,1,2,0:T(8,128)(2,1)S(1)} %pad_maximum_fusion.13), channel_id=1, source_target_pairs={{0,4},{2,6},{4,0},{6,2},{8,12},{10,14},{12,8},{14,10},{16,20},{18,... | collective-permute-start | bytes 589832 | tf_op jit(solution)/shard_map/ppermute | solution.py:12
  110.8 1.1 broadcast_select_fusion.3
  111.9 1.1 copy.428
  113.0 7.9 %collective-permute-done.11 = bf16[2,96,4,128]{3,1,2,0:T(8,128)(2,1)S(1)} collective-permute-done((bf16[2,96,4,128]{3,1,2,0:T(8,128)(2,1)S(1)}, bf16[2,96,4,128]{3,1,2,0:T(8,128)(2,1)S(1)}, u32[]{:S(2)}, u32[]{:S(2)}) %collective-permute-start.11) | collective-permute-done | bytes 196640 | tf_op jit(solution)/shard_map/ppermute | solution.py:12
  120.9 3.7 %collective-permute-start.6 = (bf16[2,128,4,128]{3,1,2,0:T(8,128)(2,1)S(1)}, bf16[2,128,4,128]{3,1,2,0:T(8,128)(2,1)S(1)}, u32[]{:S(2)}, u32[]{:S(2)}) collective-permute-start(bf16[2,128,4,128]{3,1,2,0:T(8,128)(2,1)S(1)} %get-tuple-element.41), channel_id=1, source_target_pairs={{0,2},{2,0},{4,6},{6,4},{8,10},{10,8},{12,14},{14,12},{16,18},{18,... | collective-permute-start | bytes 786440 | tf_op jit(solution)/shard_map/ppermute | solution.py:12
  126.1 1.9 collective-permute-start.12
  128.1 6.7 %collective-permute-start.13 = (bf16[2,128,4,128]{3,1,2,0:T(8,128)(2,1)}, bf16[2,128,4,128]{3,1,2,0:T(8,128)(2,1)}, u32[]{:S(2)}, u32[]{:S(2)}) collective-permute-start(bf16[2,128,4,128]{3,1,2,0:T(8,128)(2,1)} %pad_maximum_fusion.11), channel_id=1, source_target_pairs={{16,0},{18,2},{20,4},{22,6},{24,8},{26,10},{28,12},{30,14},{32,16}... | collective-permute-start | bytes 786440 | tf_op jit(solution)/shard_map/ppermute | solution.py:31
  135.6 3.7 %collective-permute-start.15 = (bf16[2,64,4,128]{3,1,2,0:T(8,128)(2,1)}, bf16[2,64,4,128]{3,1,2,0:T(8,128)(2,1)}, u32[]{:S(2)}, u32[]{:S(2)}) collective-permute-start(bf16[2,64,4,128]{3,1,2,0:T(8,128)(2,1)} %pad_maximum_fusion.14), channel_id=1, source_target_pairs={{0,8},{2,10},{4,12},{6,14},{8,0},{10,2},{12,4},{14,6},{16,24},{18,... | collective-permute-start | bytes 393224 | tf_op jit(solution)/shard_map/ppermute | solution.py:12
  139.3 5.3 %collective-permute-start.10 = (bf16[2,128,4,128]{3,1,2,0:T(8,128)(2,1)}, bf16[2,128,4,128]{3,1,2,0:T(8,128)(2,1)}, u32[]{:S(2)}, u32[]{:S(2)}) collective-permute-start(bf16[2,128,4,128]{3,1,2,0:T(8,128)(2,1)} %get-tuple-element.35), channel_id=1, source_target_pairs={{0,4},{2,6},{4,0},{6,2},{8,12},{10,14},{12,8},{14,10},{16,20},{18,... | collective-permute-start | bytes 786440 | tf_op jit(solution)/shard_map/ppermute | solution.py:12
  144.7 6.8 %pad_maximum_fusion.2 = bf16[2,768,4,128]{3,2,1,0:T(4,128)(2,1)S(1)} fusion(bf16[2,256,4,128]{3,2,1,0:T(4,128)(2,1)S(1)} %collective-permute-done.3, bf16[1,256,4,128]{3,2,1,0:T(4,128)(2,1)S(1)} %bitcast.547, bf16[1,256,4,128]{3,2,1,0:T(4,128)(2,1)S(1)} %copy-done.10, bf16[2,256,4,128]{3,2,1,0:T(4,128)(2,1)S(1)} %collective-permute-done.2), kind=kLoop, calls=%fused_computation.11 | loop fusion | flops 2359296 | bytes 3145728 | tf_op jit(solution)/shard_map/concatenate | solution.py:24
  155.3 1.2 convolution_bitcast_fusion.1
  161.5 1.7 pad_maximum_fusion.12
  163.3 1.9 collective-permute-start.16
  165.2 7.0 %collective-permute-start.17 = (bf16[2,128,4,128]{3,1,2,0:T(8,128)(2,1)}, bf16[2,128,4,128]{3,1,2,0:T(8,128)(2,1)}, u32[]{:S(2)}, u32[]{:S(2)}) collective-permute-start(bf16[2,128,4,128]{3,1,2,0:T(8,128)(2,1)} %pad_maximum_fusion.12), channel_id=1, source_target_pairs={{32,0},{34,2},{36,4},{38,6},{40,8},{42,10},{44,12},{46,14},{48,16}... | collective-permute-start | bytes 786440 | tf_op jit(solution)/shard_map/ppermute | solution.py:31
  172.2 1.0 constant_dynamic-update-slice_fusion.8
  173.1 1.9 broadcast_select_fusion.1
  175.0 3.4 %collective-permute-start.14 = (bf16[2,128,4,128]{3,1,2,0:T(8,128)(2,1)}, bf16[2,128,4,128]{3,1,2,0:T(8,128)(2,1)}, u32[]{:S(2)}, u32[]{:S(2)}) collective-permute-start(bf16[2,128,4,128]{3,1,2,0:T(8,128)(2,1)} %get-tuple-element.37), channel_id=1, source_target_pairs={{0,8},{2,10},{4,12},{6,14},{8,0},{10,2},{12,4},{14,6},{16,24},{18,... | collective-permute-start | bytes 786440 | tf_op jit(solution)/shard_map/ppermute | solution.py:12
  178.5 1.0 constant_dynamic-update-slice_fusion.3
  179.5 0.9 copy-done.13
  182.6 1.3 convolution_bitcast_fusion.2
  184.0 1.7 constant_dynamic-update-slice_fusion.11
  185.7 2.0 broadcast_select_fusion
  187.6 2.0 collective-permute-start.18
  189.7 5.6 %collective-permute-done.14 = bf16[2,128,4,128]{3,1,2,0:T(8,128)(2,1)} collective-permute-done((bf16[2,128,4,128]{3,1,2,0:T(8,128)(2,1)}, bf16[2,128,4,128]{3,1,2,0:T(8,128)(2,1)}, u32[]{:S(2)}, u32[]{:S(2)}) %collective-permute-start.14) | collective-permute-done | bytes 262176 | tf_op jit(solution)/shard_map/ppermute | solution.py:12
  195.3 1.0 constant_dynamic-update-slice_fusion.6
  196.3 0.9 copy-done.16
  199.3 1.9 convolution_bitcast_fusion.3
  202.0 1.3 fusion.135
  205.0 1.8 convolution_bitcast_fusion.4
  206.8 1.2 constant_dynamic-slice_fusion.8
  209.6 0.9 convolution_bitcast_fusion.5
  211.2 1.3 constant_dynamic-slice_fusion.2
  215.5 1.2 constant_dynamic-slice_fusion.5
  222.2 0.9 fusion.87
  223.7 3.6 %fusion.24 = bf16[512,4,128]{2,0,1:T(8,128)(2,1)S(1)} fusion(f32[4,128,4,128]{3,1,0,2:T(8,128)S(1)} %copy-done.8, f32[512,4,128]{2,0,1:T(8,128)S(1)} %bitcast.544, f32[512,4,128]{2,0,1:T(8,128)S(1)} %bitcast.545, f32[512,4]{0,1:T(4,128)S(1)} %get-tuple-element.5, f32[2,4,128]{2,0,1:T(2,128)S(1)} %copy-done.42, f32[512,4]{0,1:T(4,128)S(1)} %get-tuple-element.12, ...), kind=kLoop, calls=%fused_computation.50 | loop fusion | flops 4980736 | bytes 4009984 | tf_op jit(solution)/shard_map/convert_element_type | solution.py:285
  227.3 1.3 bitcast_convert_fusion
  228.7 10.1 %all_to_all.5 = bf16[2,512,1024]{2,1,0:T(8,128)(2,1)} all-to-all(bf16[2,512,1024]{2,1,0:T(8,128)(2,1)S(1)} %bitcast.541), channel_id=1, replica_groups=mesh['seq'=256,'head'=2] {'head'}, dimensions={0} | all-to-all | bytes 4194304 | tf_op jit(solution)/shard_map/all_to_all | solution.py:58
  238.8 3.3 %reduce_sum.342 = bf16[512,1024]{1,0:T(8,128)(2,1)} reduce(bf16[2,512,1024]{2,1,0:T(8,128)(2,1)} %all_to_all.5, bf16[]{:T(256)} %constant.307.clone.1), dimensions={0}, to_apply=%region_42.43 | reduce | flops 524288 | bytes 3145730 | tf_op jit(solution)/shard_map/reduce_sum | solution.py:59
  (326 shorter events, 60.4 us)
Async XLA Ops:
  6.5 220.7 %copy-start = (bf16[4,128,2048]{2,1,0:T(8,128)(2,1)S(1)}, bf16[4,128,2048]{2,1,0:T(8,128)(2,1)}, u32[]{:S(2)}) copy-start(bf16[4,128,2048]{2,1,0:T(8,128)(2,1)} %param.7) | copy-start | bytes 6291460
  6.5 11.2 %copy-start.1 = (bf16[512,4,128]{2,1,0:T(4,128)(2,1)S(1)}, bf16[512,4,128]{2,1,0:T(4,128)(2,1)}, u32[]{:S(2)}) copy-start(bf16[512,4,128]{2,1,0:T(4,128)(2,1)} %param.5) | copy-start | bytes 1572868
  6.5 11.4 %copy-start.2 = (bf16[512,4,128]{2,1,0:T(4,128)(2,1)S(1)}, bf16[512,4,128]{2,1,0:T(4,128)(2,1)}, u32[]{:S(2)}) copy-start(bf16[512,4,128]{2,1,0:T(4,128)(2,1)} %param.6) | copy-start | bytes 1572868
  6.5 200.3 %all-gather.3.cloned.1.call-start = ((), (), s32[]{:S(2)}) async-start(), calls=%async_computation.1 | async-start | bytes 7368704 | tf_op jit(solution)/shard_map/all_gather | solution.py:229
  10.4 60.3 %collective-permute-start.4 = (bf16[2,128,4,128]{3,1,2,0:T(8,128)(2,1)}, bf16[2,128,4,128]{3,1,2,0:T(8,128)(2,1)}, u32[]{:S(2)}, u32[]{:S(2)}) collective-permute-start(bf16[2,128,4,128]{3,1,2,0:T(8,128)(2,1)} %pad_maximum_fusion.9), channel_id=1, source_target_pairs={{0,4},{2,6},{4,8},{6,10},{8,12},{10,14},{12,16},{14,18},{16,20},{1... | collective-permute-start | bytes 786440 | tf_op jit(solution)/shard_map/ppermute | solution.py:31
  15.8 79.6 %collective-permute-start.5 = (bf16[2,128,4,128]{3,1,2,0:T(8,128)(2,1)}, bf16[2,128,4,128]{3,1,2,0:T(8,128)(2,1)}, u32[]{:S(2)}, u32[]{:S(2)}) collective-permute-start(bf16[2,128,4,128]{3,1,2,0:T(8,128)(2,1)} %pad_maximum_fusion.9), channel_id=1, source_target_pairs={{4,0},{6,2},{8,4},{10,6},{12,8},{14,10},{16,12},{18,14},{20,16},{2... | collective-permute-start | bytes 786440 | tf_op jit(solution)/shard_map/ppermute | solution.py:31
  21.3 4.9 %copy-start.27 = (bf16[16,4,128]{2,0,1:T(8,128)(2,1)}, bf16[16,4,128]{2,0,1:T(8,128)(2,1)S(1)}, u32[]{:S(2)}) copy-start(bf16[16,4,128]{2,0,1:T(8,128)(2,1)S(1)} %copy.582) | copy-start | bytes 49156
  21.3 4.9 %copy-start.22 = (bf16[32,4,128]{2,0,1:T(8,128)(2,1)}, bf16[32,4,128]{2,0,1:T(8,128)(2,1)S(1)}, u32[]{:S(2)}) copy-start(bf16[32,4,128]{2,0,1:T(8,128)(2,1)S(1)} %copy.581) | copy-start | bytes 98308
  21.4 4.9 %copy-start.20 = (bf16[1,32,4,128]{3,1,2,0:T(8,128)(2,1)}, bf16[1,32,4,128]{3,1,2,0:T(8,128)(2,1)S(1)}, u32[]{:S(2)}) copy-start(bf16[1,32,4,128]{3,1,2,0:T(8,128)(2,1)S(1)} %fusion.69) | copy-start | bytes 98308
  22.1 43.2 %collective-permute-start.7 = (bf16[2,112,4,128]{3,1,2,0:T(8,128)(2,1)}, bf16[2,112,4,128]{3,1,2,0:T(8,128)(2,1)}, u32[]{:S(2)}, u32[]{:S(2)}) collective-permute-start(bf16[2,112,4,128]{3,1,2,0:T(8,128)(2,1)} %maximum_maximum_fusion.1), channel_id=1, source_target_pairs={{0,2},{2,0},{4,6},{6,4},{8,10},{10,8},{12,14},{14,12},{16,18},{18,... | collective-permute-start | bytes 688136 | tf_op jit(solution)/shard_map/ppermute | solution.py:12
  24.6 1.7 copy-start.6
  26.2 48.8 %collective-permute-start = (bf16[2,128,4,128]{3,1,2,0:T(8,128)(2,1)}, bf16[2,128,4,128]{3,1,2,0:T(8,128)(2,1)}, u32[]{:S(2)}, u32[]{:S(2)}) collective-permute-start(bf16[2,128,4,128]{3,1,2,0:T(8,128)(2,1)} %get-tuple-element.33), channel_id=1, source_target_pairs={{0,2},{2,4},{4,6},{6,8},{8,10},{10,12},{12,14},{14,16},{16,18},{18... | collective-permute-start | bytes 786440 | tf_op jit(solution)/shard_map/ppermute | solution.py:22
  29.2 49.0 %collective-permute-start.1 = (bf16[2,128,4,128]{3,1,2,0:T(8,128)(2,1)}, bf16[2,128,4,128]{3,1,2,0:T(8,128)(2,1)}, u32[]{:S(2)}, u32[]{:S(2)}) collective-permute-start(bf16[2,128,4,128]{3,1,2,0:T(8,128)(2,1)} %get-tuple-element.34), channel_id=1, source_target_pairs={{2,0},{4,2},{6,4},{8,6},{10,8},{12,10},{14,12},{16,14},{18,16},{20... | collective-permute-start | bytes 786440 | tf_op jit(solution)/shard_map/ppermute | solution.py:23
  35.5 1.8 copy-start.3
  36.0 4.0 %copy-start.9 = (bf16[1,256,4,128]{3,2,1,0:T(4,128)(2,1)}, bf16[1,256,4,128]{3,2,1,0:T(4,128)(2,1)S(1)}, u32[]{:S(2)}) copy-start(bf16[1,256,4,128]{3,2,1,0:T(4,128)(2,1)S(1)} %fusion.41) | copy-start | bytes 786436
  44.4 44.2 %copy-start.5 = (bf16[1,512,4,128]{3,1,2,0:T(8,128)(2,1)S(1)}, bf16[1,512,4,128]{3,1,2,0:T(8,128)(2,1)}, u32[]{:S(2)}) copy-start(bf16[1,512,4,128]{3,1,2,0:T(8,128)(2,1)} %copy-done.4) | copy-start | bytes 1572868
  57.1 31.5 %copy-start.7 = (bf16[1,512,4,128]{3,1,2,0:T(8,128)(2,1)S(1)}, bf16[1,512,4,128]{3,1,2,0:T(8,128)(2,1)}, u32[]{:S(2)}) copy-start(bf16[1,512,4,128]{3,1,2,0:T(8,128)(2,1)} %copy-done.6) | copy-start | bytes 1572868
  65.3 70.3 %collective-permute-start.2 = (bf16[2,256,4,128]{3,2,1,0:T(4,128)(2,1)}, bf16[2,256,4,128]{3,2,1,0:T(4,128)(2,1)S(1)}, u32[]{:S(2)}, u32[]{:S(2)}) collective-permute-start(bf16[2,256,4,128]{3,2,1,0:T(4,128)(2,1)} %pad_maximum_fusion.6), channel_id=1, source_target_pairs={{0,2},{2,4},{4,6},{6,8},{8,10},{10,12},{12,14},{14,16},{16,18},{18... | collective-permute-start | bytes 1572872 | tf_op jit(solution)/shard_map/ppermute | solution.py:22
  68.0 56.7 %copy-start.25 = (bf16[2,16,4,128]{3,1,2,0:T(8,128)(2,1)}, bf16[2,16,4,128]{3,1,2,0:T(8,128)(2,1)S(1)}, u32[]{:S(2)}) copy-start(bf16[2,16,4,128]{3,1,2,0:T(8,128)(2,1)S(1)} %slice.191) | copy-start | bytes 98308
  70.6 68.7 %collective-permute-start.3 = (bf16[2,256,4,128]{3,2,1,0:T(4,128)(2,1)}, bf16[2,256,4,128]{3,2,1,0:T(4,128)(2,1)S(1)}, u32[]{:S(2)}, u32[]{:S(2)}) collective-permute-start(bf16[2,256,4,128]{3,2,1,0:T(4,128)(2,1)} %pad_maximum_fusion.6), channel_id=1, source_target_pairs={{2,0},{4,2},{6,4},{8,6},{10,8},{12,10},{14,12},{16,14},{18,16},{20... | collective-permute-start | bytes 1572872 | tf_op jit(solution)/shard_map/ppermute | solution.py:23
  75.0 51.1 %collective-permute-start.8 = (bf16[2,128,4,128]{3,1,2,0:T(8,128)(2,1)S(1)}, bf16[2,128,4,128]{3,1,2,0:T(8,128)(2,1)S(1)}, u32[]{:S(2)}, u32[]{:S(2)}) collective-permute-start(bf16[2,128,4,128]{3,1,2,0:T(8,128)(2,1)S(1)} %pad_maximum_fusion.10), channel_id=1, source_target_pairs={{0,8},{2,10},{4,12},{6,14},{8,16},{10,18},{12,20},{14,22},{16,24},... | collective-permute-start | bytes 786440 | tf_op jit(solution)/shard_map/ppermute | solution.py:31
  78.3 49.8 %collective-permute-start.9 = (bf16[2,128,4,128]{3,1,2,0:T(8,128)(2,1)S(1)}, bf16[2,128,4,128]{3,1,2,0:T(8,128)(2,1)S(1)}, u32[]{:S(2)}, u32[]{:S(2)}) collective-permute-start(bf16[2,128,4,128]{3,1,2,0:T(8,128)(2,1)S(1)} %pad_maximum_fusion.10), channel_id=1, source_target_pairs={{8,0},{10,2},{12,4},{14,6},{16,8},{18,10},{20,12},{22,14},{24,16},... | collective-permute-start | bytes 786440 | tf_op jit(solution)/shard_map/ppermute | solution.py:31
  92.4 1.6 copy-start.35
  95.4 29.3 %copy-start.28 = (bf16[16,4,128]{2,0,1:T(8,128)(2,1)S(1)}, bf16[16,4,128]{2,0,1:T(8,128)(2,1)}, u32[]{:S(2)}) copy-start(bf16[16,4,128]{2,0,1:T(8,128)(2,1)} %copy-done.27) | copy-start | bytes 49156
  95.4 25.5 %collective-permute-start.11 = (bf16[2,96,4,128]{3,1,2,0:T(8,128)(2,1)S(1)}, bf16[2,96,4,128]{3,1,2,0:T(8,128)(2,1)S(1)}, u32[]{:S(2)}, u32[]{:S(2)}) collective-permute-start(bf16[2,96,4,128]{3,1,2,0:T(8,128)(2,1)S(1)} %pad_maximum_fusion.13), channel_id=1, source_target_pairs={{0,4},{2,6},{4,0},{6,2},{8,12},{10,14},{12,8},{14,10},{16,20},{18,... | collective-permute-start | bytes 589832 | tf_op jit(solution)/shard_map/ppermute | solution.py:12
  111.9 13.4 %copy-start.21 = (bf16[1,32,4,128]{3,1,2,0:T(8,128)(2,1)S(1)}, bf16[1,32,4,128]{3,1,2,0:T(8,128)(2,1)}, u32[]{:S(2)}) copy-start(bf16[1,32,4,128]{3,1,2,0:T(8,128)(2,1)} %copy-done.20) | copy-start | bytes 98308
  111.9 13.4 %copy-start.23 = (bf16[32,4,128]{2,0,1:T(8,128)(2,1)S(1)}, bf16[32,4,128]{2,0,1:T(8,128)(2,1)}, u32[]{:S(2)}) copy-start(bf16[32,4,128]{2,0,1:T(8,128)(2,1)} %copy-done.22) | copy-start | bytes 98308
  113.0 31.7 %copy-start.10 = (bf16[1,256,4,128]{3,2,1,0:T(4,128)(2,1)S(1)}, bf16[1,256,4,128]{3,2,1,0:T(4,128)(2,1)}, u32[]{:S(2)}) copy-start(bf16[1,256,4,128]{3,2,1,0:T(4,128)(2,1)} %copy-done.9) | copy-start | bytes 786436
  120.9 30.8 %collective-permute-start.6 = (bf16[2,128,4,128]{3,1,2,0:T(8,128)(2,1)S(1)}, bf16[2,128,4,128]{3,1,2,0:T(8,128)(2,1)S(1)}, u32[]{:S(2)}, u32[]{:S(2)}) collective-permute-start(bf16[2,128,4,128]{3,1,2,0:T(8,128)(2,1)S(1)} %get-tuple-element.41), channel_id=1, source_target_pairs={{0,2},{2,0},{4,6},{6,4},{8,10},{10,8},{12,14},{14,12},{16,18},{18,... | collective-permute-start | bytes 786440 | tf_op jit(solution)/shard_map/ppermute | solution.py:12
  126.1 46.0 %collective-permute-start.12 = (bf16[2,128,4,128]{3,1,2,0:T(8,128)(2,1)}, bf16[2,128,4,128]{3,1,2,0:T(8,128)(2,1)}, u32[]{:S(2)}, u32[]{:S(2)}) collective-permute-start(bf16[2,128,4,128]{3,1,2,0:T(8,128)(2,1)} %pad_maximum_fusion.11), channel_id=1, source_target_pairs={{0,16},{2,18},{4,20},{6,22},{8,24},{10,26},{12,28},{14,30},{16,32}... | collective-permute-start | bytes 786440 | tf_op jit(solution)/shard_map/ppermute | solution.py:31
  128.1 45.1 %collective-permute-start.13 = (bf16[2,128,4,128]{3,1,2,0:T(8,128)(2,1)}, bf16[2,128,4,128]{3,1,2,0:T(8,128)(2,1)}, u32[]{:S(2)}, u32[]{:S(2)}) collective-permute-start(bf16[2,128,4,128]{3,1,2,0:T(8,128)(2,1)} %pad_maximum_fusion.11), channel_id=1, source_target_pairs={{16,0},{18,2},{20,4},{22,6},{24,8},{26,10},{28,12},{30,14},{32,16}... | collective-permute-start | bytes 786440 | tf_op jit(solution)/shard_map/ppermute | solution.py:31
  135.6 16.1 %copy-start.11 = (bf16[2,384,4,128]{3,1,2,0:T(8,128)(2,1)}, bf16[2,384,4,128]{3,1,2,0:T(8,128)(2,1)S(1)}, u32[]{:S(2)}) copy-start(bf16[2,384,4,128]{3,1,2,0:T(8,128)(2,1)S(1)} %get-tuple-element.36) | copy-start | bytes 2359300
  135.6 25.9 %collective-permute-start.15 = (bf16[2,64,4,128]{3,1,2,0:T(8,128)(2,1)}, bf16[2,64,4,128]{3,1,2,0:T(8,128)(2,1)}, u32[]{:S(2)}, u32[]{:S(2)}) collective-permute-start(bf16[2,64,4,128]{3,1,2,0:T(8,128)(2,1)} %pad_maximum_fusion.14), channel_id=1, source_target_pairs={{0,8},{2,10},{4,12},{6,14},{8,0},{10,2},{12,4},{14,6},{16,24},{18,... | collective-permute-start | bytes 393224 | tf_op jit(solution)/shard_map/ppermute | solution.py:12
  139.3 39.1 %collective-permute-start.10 = (bf16[2,128,4,128]{3,1,2,0:T(8,128)(2,1)}, bf16[2,128,4,128]{3,1,2,0:T(8,128)(2,1)}, u32[]{:S(2)}, u32[]{:S(2)}) collective-permute-start(bf16[2,128,4,128]{3,1,2,0:T(8,128)(2,1)} %get-tuple-element.35), channel_id=1, source_target_pairs={{0,4},{2,6},{4,0},{6,2},{8,12},{10,14},{12,8},{14,10},{16,20},{18,... | collective-permute-start | bytes 786440 | tf_op jit(solution)/shard_map/ppermute | solution.py:12
  151.4 1.0 copy-start.18
  153.2 1.0 copy-start.30
  153.2 1.0 copy-start.49
  156.9 3.7 %copy-start.19 = (f32[128,4,128]{0,2,1:T(8,128)S(1)}, f32[128,4,128]{0,2,1:T(8,128)}, u32[]{:S(2)}) copy-start(f32[128,4,128]{0,2,1:T(8,128)} %convolution_bitcast_fusion.1) | copy-start | bytes 786436
  158.7 2.8 %copy-start.26 = (bf16[2,16,4,128]{3,1,2,0:T(8,128)(2,1)S(1)}, bf16[2,16,4,128]{3,1,2,0:T(8,128)(2,1)}, u32[]{:S(2)}) copy-start(bf16[2,16,4,128]{3,1,2,0:T(8,128)(2,1)} %copy-done.25) | copy-start | bytes 98308
  161.5 17.0 %copy-start.12 = (bf16[2,384,4,128]{3,1,2,0:T(8,128)(2,1)S(1)}, bf16[2,384,4,128]{3,1,2,0:T(8,128)(2,1)}, u32[]{:S(2)}) copy-start(bf16[2,384,4,128]{3,1,2,0:T(8,128)(2,1)} %copy-done.11) | copy-start | bytes 2359300
  161.5 18.9 %copy-start.24 = (f32[64,4,128]{2,1,0:T(4,128)S(1)}, f32[64,4,128]{2,1,0:T(4,128)}, u32[]{:S(2)}) copy-start(f32[64,4,128]{2,1,0:T(4,128)} %bitcast_reduce_fusion.18) | copy-start | bytes 393220
  161.5 18.9 %copy-start.45 = (pred[384]{0:T(512)(128)(4,1)S(1)}, pred[384]{0:T(512)(128)(4,1)}, u32[]{:S(2)}) copy-start(pred[384]{0:T(512)(128)(4,1)} %fusion.112) | copy-start | bytes 1156
  163.3 20.7 %collective-permute-start.16 = (bf16[2,128,4,128]{3,1,2,0:T(8,128)(2,1)}, bf16[2,128,4,128]{3,1,2,0:T(8,128)(2,1)}, u32[]{:S(2)}, u32[]{:S(2)}) collective-permute-start(bf16[2,128,4,128]{3,1,2,0:T(8,128)(2,1)} %pad_maximum_fusion.12), channel_id=1, source_target_pairs={{0,32},{2,34},{4,36},{6,38},{8,40},{10,42},{12,44},{14,46},{16,48}... | collective-permute-start | bytes 786440 | tf_op jit(solution)/shard_map/ppermute | solution.py:31
  165.2 20.5 %collective-permute-start.17 = (bf16[2,128,4,128]{3,1,2,0:T(8,128)(2,1)}, bf16[2,128,4,128]{3,1,2,0:T(8,128)(2,1)}, u32[]{:S(2)}, u32[]{:S(2)}) collective-permute-start(bf16[2,128,4,128]{3,1,2,0:T(8,128)(2,1)} %pad_maximum_fusion.12), channel_id=1, source_target_pairs={{32,0},{34,2},{36,4},{38,6},{40,8},{42,10},{44,12},{46,14},{48,16}... | collective-permute-start | bytes 786440 | tf_op jit(solution)/shard_map/ppermute | solution.py:31
  175.0 3.5 %copy-start.14 = (bf16[2,384,4,128]{3,1,2,0:T(8,128)(2,1)}, bf16[2,384,4,128]{3,1,2,0:T(8,128)(2,1)S(1)}, u32[]{:S(2)}) copy-start(bf16[2,384,4,128]{3,1,2,0:T(8,128)(2,1)S(1)} %get-tuple-element.38) | copy-start | bytes 2359300
  175.0 20.3 %collective-permute-start.14 = (bf16[2,128,4,128]{3,1,2,0:T(8,128)(2,1)}, bf16[2,128,4,128]{3,1,2,0:T(8,128)(2,1)}, u32[]{:S(2)}, u32[]{:S(2)}) collective-permute-start(bf16[2,128,4,128]{3,1,2,0:T(8,128)(2,1)} %get-tuple-element.37), channel_id=1, source_target_pairs={{0,8},{2,10},{4,12},{6,14},{8,0},{10,2},{12,4},{14,6},{16,24},{18,... | collective-permute-start | bytes 786440 | tf_op jit(solution)/shard_map/ppermute | solution.py:12
  179.5 0.9 copy-start.13
  181.9 15.4 %copy-start.31 = (f32[32,4,128]{2,1,0:T(4,128)S(1)}, f32[32,4,128]{2,1,0:T(4,128)}, u32[]{:S(2)}) copy-start(f32[32,4,128]{2,1,0:T(4,128)} %bitcast_reduce_fusion.11) | copy-start | bytes 196612
  181.9 15.4 %copy-start.48 = (pred[384]{0:T(512)(128)(4,1)S(1)}, pred[384]{0:T(512)(128)(4,1)}, u32[]{:S(2)}) copy-start(pred[384]{0:T(512)(128)(4,1)} %fusion.111) | copy-start | bytes 1156
  182.6 12.7 %copy-start.15 = (bf16[2,384,4,128]{3,1,2,0:T(8,128)(2,1)S(1)}, bf16[2,384,4,128]{3,1,2,0:T(8,128)(2,1)}, u32[]{:S(2)}) copy-start(bf16[2,384,4,128]{3,1,2,0:T(8,128)(2,1)} %copy-done.14) | copy-start | bytes 2359300
  187.6 14.3 %copy-start.33 = (f32[16,4,128]{2,1,0:T(4,128)S(1)}, f32[16,4,128]{2,1,0:T(4,128)}, u32[]{:S(2)}) copy-start(f32[16,4,128]{2,1,0:T(4,128)} %bitcast_reduce_fusion.10) | copy-start | bytes 98308
  187.6 14.3 %copy-start.44 = (pred[384]{0:T(512)(128)(4,1)S(1)}, pred[384]{0:T(512)(128)(4,1)}, u32[]{:S(2)}) copy-start(pred[384]{0:T(512)(128)(4,1)} %fusion.110) | copy-start | bytes 1156
  187.6 13.6 %collective-permute-start.18 = (bf16[2,128,4,128]{3,1,2,0:T(8,128)(2,1)}, bf16[2,128,4,128]{3,1,2,0:T(8,128)(2,1)S(1)}, u32[]{:S(2)}, u32[]{:S(2)}) collective-permute-start(bf16[2,128,4,128]{3,1,2,0:T(8,128)(2,1)} %get-tuple-element.39), channel_id=1, source_target_pairs={{0,16},{2,18},{4,20},{6,22},{8,24},{10,26},{12,28},{14,30},{16,0},... | collective-permute-start | bytes 786440 | tf_op jit(solution)/shard_map/ppermute | solution.py:12
  196.3 1.0 copy-start.16
  209.6 0.9 copy-start.38
  213.9 2.7 %copy-start.40 = (f32[4,2]{1,0:T(4,128)}, f32[4,2]{1,0:T(4,128)S(1)}, u32[]{:S(2)}) copy-start(f32[4,2]{1,0:T(4,128)S(1)} %get-tuple-element.51) | copy-start | bytes 100
  217.5 4.7 %copy-start.36 = (f32[4,4,128]{2,1,0:T(4,128)S(1)}, f32[4,4,128]{2,1,0:T(4,128)}, u32[]{:S(2)}) copy-start(f32[4,4,128]{2,1,0:T(4,128)} %copy-done.35) | copy-start | bytes 24580
  217.5 4.7 %copy-start.37 = (f32[4,4,128]{2,1,0:T(4,128)S(1)}, f32[4,4,128]{2,1,0:T(4,128)}, u32[]{:S(2)}) copy-start(f32[4,4,128]{2,1,0:T(4,128)} %fusion.1) | copy-start | bytes 24580
  217.7 5.4 %copy-start.17 = (f32[128,4,128]{2,0,1:T(8,128)S(1)}, f32[128,4,128]{2,0,1:T(8,128)}, u32[]{:S(2)}) copy-start(f32[128,4,128]{2,0,1:T(8,128)} %copy.432) | copy-start | bytes 786436
  222.1 1.5 copy-start.8
  222.1 1.5 copy-start.29
  222.1 1.5 copy-start.32
  222.1 1.5 copy-start.39
  222.1 1.5 copy-start.42
  (8 other events, 5.6 us)
Sparse Core Ops, SparseCore 0:
  20.0 174.8 all-gather.2

commit v6 on v5

--- a/solution.py
+++ b/solution.py
@@ -200,7 +200,7 @@
         pieces[level_index] = jnp.stack(
             [coarsen(key_rows, level_index, True), coarsen(value_rows, level_index, False)]
         )
-    shift_levels = list(range(2, top_level - 2))
+    shift_levels = list(range(2, top_level - 3))
     assembled = assemble_joint(pieces, shift_levels, device_index)
     for level_index in shift_levels:
         group = 1 << level_index - 2
@@ -225,7 +225,7 @@
                 ),
             )
         )
-    coarse_list = [top_level - 2, top_level - 1, top_level]
+    coarse_list = [top_level - 3, top_level - 2, top_level - 1, top_level]
     lines = lax.all_gather(
         jnp.concatenate(
             [pieces[level_index].reshape(-1, head_size) for level_index in coarse_list]

time: 251 us -> 256 us (1.020)
  the two profiles are of different devices: /device:TPU:273 before, /device:TPU:1 now
where the time goes in v6:
time: 256 us; the launch traced here: 253 us
  starting transfers between devices  60.6 us (24%)
  other arithmetic  57.3 us (22%)
  local copies, waits for them, and re-layouts  54.8 us (21%)
  waiting for transfers between devices  41.9 us (16%)
  matrix products  16.1 us (6%)
  between operations  14.8 us (6%)
  blocking collectives  7.32 us (3%)
    ppermute x6, starting transfers between devices, shifted(): lax.ppermute(value, axis, [(source, source + steps) for source in range(i...  35.9 us
    ppermute x5, waiting for transfers between devices, partner_2(): return lax.ppermute(value, axis, pairs)  28.2 us
    ppermute x5, starting transfers between devices, partner_2(): return lax.ppermute(value, axis, pairs)  14.4 us
    all_gather x1, waiting for transfers between devices, per_device(): lax.all_gather(jnp.concatenate([pieces[level_index].reshape(-1, head_size...  13.7 us
    concatenate x21, local copies, waits for them, and re-layouts, slot_masks(): jnp.concatenate([jnp.repeat(((target >= 0) & (target < block_total))[:, N...  11.7 us
    reduce_sum x24, other arithmetic, coarsen(): summed = jnp.sum(grouped, axis=1)  11.5 us
    dot_general x9, matrix products, level_attend(): jnp.einsum('nhqk,nkhd->nqhd', weights.astype(jnp.bfloat16), value_blocks,...  10.1 us
    concatenate x9, other arithmetic, slot_masks(): jnp.concatenate([jnp.repeat(((target >= 0) & (target < block_total))[:, N...  9.34 us
  transfers between devices with their start and end apart: 16, of which 3 were waited for; matrix products, arithmetic and copies ran while one was open for 35% of the time, Pallas kernels for 0%

profile of v6, /device:TPU:1, one launch (start us, length us, event | category | flops | bytes accessed | tf_op | source)
XLA Modules:
  0.0 252.8 jit_solution(4564970132780011806)
XLA Ops:
  6.5 1.4 bitcast_reduce_fusion.11
  8.0 1.3 bitcast_reduce_fusion.9
  9.2 1.3 bitcast_reduce_fusion.10
  14.0 5.7 %collective-permute-start.4 = (bf16[2,128,4,128]{3,1,2,0:T(8,128)(2,1)}, bf16[2,128,4,128]{3,1,2,0:T(8,128)(2,1)}, u32[]{:S(2)}, u32[]{:S(2)}) collective-permute-start(bf16[2,128,4,128]{3,1,2,0:T(8,128)(2,1)} %pad_maximum_fusion.10), channel_id=1, source_target_pairs={{0,4},{2,6},{4,8},{6,10},{8,12},{10,14},{12,16},{14,18},{16,20},{1... | collective-permute-start | bytes 786440 | tf_op jit(solution)/shard_map/ppermute | solution.py:31
  19.7 1.3 collective-permute-start.5
  22.7 3.2 %collective-permute-start.7 = (bf16[2,96,4,128]{3,1,2,0:T(8,128)(2,1)}, bf16[2,96,4,128]{3,1,2,0:T(8,128)(2,1)}, u32[]{:S(2)}, u32[]{:S(2)}) collective-permute-start(bf16[2,96,4,128]{3,1,2,0:T(8,128)(2,1)} %maximum_maximum_fusion.1), channel_id=1, source_target_pairs={{0,2},{2,0},{4,6},{6,4},{8,10},{10,8},{12,14},{14,12},{16,18},{18,... | collective-permute-start | bytes 589832 | tf_op jit(solution)/shard_map/ppermute | solution.py:12
  27.7 2.8 %collective-permute-start = (bf16[2,128,4,128]{3,1,2,0:T(8,128)(2,1)}, bf16[2,128,4,128]{3,1,2,0:T(8,128)(2,1)}, u32[]{:S(2)}, u32[]{:S(2)}) collective-permute-start(bf16[2,128,4,128]{3,1,2,0:T(8,128)(2,1)} %get-tuple-element.36), channel_id=1, source_target_pairs={{0,2},{2,4},{4,6},{6,8},{8,10},{10,12},{12,14},{14,16},{16,18},{18... | collective-permute-start | bytes 786440 | tf_op jit(solution)/shard_map/ppermute | solution.py:22
  30.5 1.3 collective-permute-start.1
  33.6 1.2 pad_maximum_fusion.7
  34.8 0.9 bitcast_reduce_fusion.18
  37.4 1.0 bitcast_reduce_fusion.21
  54.1 1.3 fusion.108
  55.4 1.2 fusion.107
  56.6 1.2 fusion.106
  57.8 1.3 fusion.105
  59.1 1.2 fusion.104
  60.3 1.3 fusion.103
  62.3 5.0 %collective-permute-start.2 = (bf16[2,256,4,128]{3,2,1,0:T(4,128)(2,1)}, bf16[2,256,4,128]{3,2,1,0:T(4,128)(2,1)S(1)}, u32[]{:S(2)}, u32[]{:S(2)}) collective-permute-start(bf16[2,256,4,128]{3,2,1,0:T(4,128)(2,1)} %pad_maximum_fusion.7), channel_id=1, source_target_pairs={{0,2},{2,4},{4,6},{6,8},{8,10},{10,12},{12,14},{14,16},{16,18},{18... | collective-permute-start | bytes 1572872 | tf_op jit(solution)/shard_map/ppermute | solution.py:22
  67.3 0.9 slice.190
  68.9 0.9 slice.188
  69.9 1.3 collective-permute-start.3
  71.2 1.0 constant_dynamic-update-slice_fusion.2
  72.1 10.4 %collective-permute-start.8 = (bf16[2,128,4,128]{3,1,2,0:T(8,128)(2,1)S(1)}, bf16[2,128,4,128]{3,1,2,0:T(8,128)(2,1)S(1)}, u32[]{:S(2)}, u32[]{:S(2)}) collective-permute-start(bf16[2,128,4,128]{3,1,2,0:T(8,128)(2,1)S(1)} %pad_maximum_fusion.11), channel_id=1, source_target_pairs={{0,8},{2,10},{4,12},{6,14},{8,16},{10,18},{12,20},{14,22},{16,24},... | collective-permute-start | bytes 786440 | tf_op jit(solution)/shard_map/ppermute | solution.py:31
  82.6 1.5 collective-permute-start.9
  84.1 1.1 pad_maximum_fusion.1
  87.9 1.6 fusion.12
  89.5 1.4 fusion.1
  90.9 2.0 collective-permute-start.11
  93.0 1.1 broadcast_select_fusion.2
  94.1 1.1 copy.458
  95.2 16.3 %collective-permute-done.11 = bf16[2,64,4,128]{3,1,2,0:T(8,128)(2,1)S(1)} collective-permute-done((bf16[2,64,4,128]{3,1,2,0:T(8,128)(2,1)S(1)}, bf16[2,64,4,128]{3,1,2,0:T(8,128)(2,1)S(1)}, u32[]{:S(2)}, u32[]{:S(2)}) %collective-permute-start.11) | collective-permute-done | bytes 131104 | tf_op jit(solution)/shard_map/ppermute | solution.py:12
  111.5 1.9 collective-permute-start.6
  114.1 15.7 %collective-permute-start.12 = (bf16[2,128,4,128]{3,1,2,0:T(8,128)(2,1)}, bf16[2,128,4,128]{3,1,2,0:T(8,128)(2,1)}, u32[]{:S(2)}, u32[]{:S(2)}) collective-permute-start(bf16[2,128,4,128]{3,1,2,0:T(8,128)(2,1)} %pad_maximum_fusion.12), channel_id=1, source_target_pairs={{0,16},{2,18},{4,20},{6,22},{8,24},{10,26},{12,28},{14,30},{16,32}... | collective-permute-start | bytes 786440 | tf_op jit(solution)/shard_map/ppermute | solution.py:31
  129.9 1.3 collective-permute-start.13
  132.0 1.9 collective-permute-start.10
  134.0 6.8 %pad_maximum_fusion.2 = bf16[2,768,4,128]{3,2,1,0:T(4,128)(2,1)S(1)} fusion(bf16[2,256,4,128]{3,2,1,0:T(4,128)(2,1)S(1)} %collective-permute-done.3, bf16[1,256,4,128]{3,2,1,0:T(4,128)(2,1)S(1)} %bitcast.560, bf16[1,256,4,128]{3,2,1,0:T(4,128)(2,1)S(1)} %copy-done.10, bf16[2,256,4,128]{3,2,1,0:T(4,128)(2,1)S(1)} %collective-permute-done.2), kind=kLoop, calls=%fused_computation.11 | loop fusion | flops 2359296 | bytes 3145728 | tf_op jit(solution)/shard_map/concatenate | solution.py:24
  146.6 1.7 reshape.1386
  149.2 1.7 reshape.1289
  152.5 1.7 copy.464
  155.8 1.7 copy.415
  157.5 2.1 convolution_bitcast_fusion.1
  159.6 1.8 copy.462
  161.5 1.0 constant_dynamic-update-slice_fusion.8
  162.5 1.9 broadcast_select_fusion
  164.4 5.3 %collective-permute-start.14 = (bf16[2,128,4,128]{3,1,2,0:T(8,128)(2,1)}, bf16[2,128,4,128]{3,1,2,0:T(8,128)(2,1)}, u32[]{:S(2)}, u32[]{:S(2)}) collective-permute-start(bf16[2,128,4,128]{3,1,2,0:T(8,128)(2,1)} %get-tuple-element.40), channel_id=1, source_target_pairs={{0,8},{2,10},{4,12},{6,14},{8,0},{10,2},{12,4},{14,6},{16,24},{18,... | collective-permute-start | bytes 786440 | tf_op jit(solution)/shard_map/ppermute | solution.py:12
  169.7 1.0 constant_dynamic-update-slice_fusion.3
  170.7 0.9 copy-done.13
  173.9 1.3 convolution_bitcast_fusion.2
  175.2 11.9 %collective-permute-done.14 = bf16[2,128,4,128]{3,1,2,0:T(8,128)(2,1)} collective-permute-done((bf16[2,128,4,128]{3,1,2,0:T(8,128)(2,1)}, bf16[2,128,4,128]{3,1,2,0:T(8,128)(2,1)}, u32[]{:S(2)}, u32[]{:S(2)}) %collective-permute-start.14) | collective-permute-done | bytes 262176 | tf_op jit(solution)/shard_map/ppermute | solution.py:12
  187.1 1.7 constant_dynamic-update-slice_fusion.6
  188.8 1.3 fusion.131
  191.9 1.9 convolution_bitcast_fusion.3
  193.8 13.7 %all-gather.3.cloned.1.call-done = bf16[61440,128]{1,0:T(8,128)(2,1)} async-done(((bf16[240,128]{1,0:T(8,128)(2,1)}), bf16[61440,128]{1,0:T(8,128)(2,1)}) %all-gather.3.cloned.1.call-update) | async-done | bytes 15728656 | tf_op jit(solution)/shard_map/all_gather | solution.py:229
  207.5 1.2 constant_dynamic-slice_fusion.11
  210.1 0.9 convolution_bitcast_fusion.4
  211.8 1.2 constant_dynamic-slice_fusion.8
  214.5 0.9 convolution_bitcast_fusion.5
  216.1 1.3 constant_dynamic-slice_fusion.2
  220.4 1.2 constant_dynamic-slice_fusion.5
  228.8 0.9 fusion.83
  230.3 3.6 %fusion.24 = bf16[512,4,128]{2,0,1:T(8,128)(2,1)S(1)} fusion(f32[4,128,4,128]{3,1,0,2:T(8,128)S(1)} %copy-done.8, f32[512,4,128]{2,0,1:T(8,128)S(1)} %bitcast.557, f32[512,4,128]{2,0,1:T(8,128)S(1)} %bitcast.558, f32[512,4]{0,1:T(4,128)S(1)} %get-tuple-element.5, f32[2,4,128]{2,0,1:T(2,128)S(1)} %copy-done.38, f32[512,4]{0,1:T(4,128)S(1)} %get-tuple-element.12, ...), kind=kLoop, calls=%fused_computation.50 | loop fusion | flops 4980736 | bytes 4009984 | tf_op jit(solution)/shard_map/convert_element_type | solution.py:285
  233.9 1.3 bitcast_convert_fusion
  235.3 7.3 %all_to_all.5 = bf16[2,512,1024]{2,1,0:T(8,128)(2,1)} all-to-all(bf16[2,512,1024]{2,1,0:T(8,128)(2,1)S(1)} %bitcast.554), channel_id=1, replica_groups=mesh['seq'=256,'head'=2] {'head'}, dimensions={0} | all-to-all | bytes 4194304 | tf_op jit(solution)/shard_map/all_to_all | solution.py:58
  242.7 3.3 %reduce_sum.342 = bf16[512,1024]{1,0:T(8,128)(2,1)} reduce(bf16[2,512,1024]{2,1,0:T(8,128)(2,1)} %all_to_all.5, bf16[]{:T(256)} %constant.311.clone.1), dimensions={0}, to_apply=%region_42.43 | reduce | flops 524288 | bytes 3145730 | tf_op jit(solution)/shard_map/reduce_sum | solution.py:59
  (311 shorter events, 60.6 us)
Async XLA Ops:
  6.5 227.3 %copy-start = (bf16[4,128,2048]{2,1,0:T(8,128)(2,1)S(1)}, bf16[4,128,2048]{2,1,0:T(8,128)(2,1)}, u32[]{:S(2)}) copy-start(bf16[4,128,2048]{2,1,0:T(8,128)(2,1)} %param.7) | copy-start | bytes 6291460
  6.5 4.2 %copy-start.1 = (bf16[512,4,128]{2,1,0:T(4,128)(2,1)S(1)}, bf16[512,4,128]{2,1,0:T(4,128)(2,1)}, u32[]{:S(2)}) copy-start(bf16[512,4,128]{2,1,0:T(4,128)(2,1)} %param.5) | copy-start | bytes 1572868
  6.5 4.0 %copy-start.2 = (bf16[512,4,128]{2,1,0:T(4,128)(2,1)S(1)}, bf16[512,4,128]{2,1,0:T(4,128)(2,1)}, u32[]{:S(2)}) copy-start(bf16[512,4,128]{2,1,0:T(4,128)(2,1)} %param.6) | copy-start | bytes 1572868
  6.5 200.9 %all-gather.3.cloned.1.call-start = ((), (), s32[]{:S(2)}) async-start(), calls=%async_computation.1 | async-start | bytes 15790080 | tf_op jit(solution)/shard_map/all_gather | solution.py:229
  14.0 55.8 %collective-permute-start.4 = (bf16[2,128,4,128]{3,1,2,0:T(8,128)(2,1)}, bf16[2,128,4,128]{3,1,2,0:T(8,128)(2,1)}, u32[]{:S(2)}, u32[]{:S(2)}) collective-permute-start(bf16[2,128,4,128]{3,1,2,0:T(8,128)(2,1)} %pad_maximum_fusion.10), channel_id=1, source_target_pairs={{0,4},{2,6},{4,8},{6,10},{8,12},{10,14},{12,16},{14,18},{16,20},{1... | collective-permute-start | bytes 786440 | tf_op jit(solution)/shard_map/ppermute | solution.py:31
  19.7 71.2 %collective-permute-start.5 = (bf16[2,128,4,128]{3,1,2,0:T(8,128)(2,1)}, bf16[2,128,4,128]{3,1,2,0:T(8,128)(2,1)}, u32[]{:S(2)}, u32[]{:S(2)}) collective-permute-start(bf16[2,128,4,128]{3,1,2,0:T(8,128)(2,1)} %pad_maximum_fusion.10), channel_id=1, source_target_pairs={{4,0},{6,2},{8,4},{10,6},{12,8},{14,10},{16,12},{18,14},{20,16},{2... | collective-permute-start | bytes 786440 | tf_op jit(solution)/shard_map/ppermute | solution.py:31
  21.3 4.8 %copy-start.19 = (bf16[32,4,128]{2,0,1:T(8,128)(2,1)}, bf16[32,4,128]{2,0,1:T(8,128)(2,1)S(1)}, u32[]{:S(2)}) copy-start(bf16[32,4,128]{2,0,1:T(8,128)(2,1)S(1)} %copy.607) | copy-start | bytes 98308
  22.0 5.7 %copy-start.21 = (bf16[1,32,4,128]{3,1,2,0:T(8,128)(2,1)}, bf16[1,32,4,128]{3,1,2,0:T(8,128)(2,1)S(1)}, u32[]{:S(2)}) copy-start(bf16[1,32,4,128]{3,1,2,0:T(8,128)(2,1)S(1)} %fusion.69) | copy-start | bytes 98308
  22.7 39.6 %collective-permute-start.7 = (bf16[2,96,4,128]{3,1,2,0:T(8,128)(2,1)}, bf16[2,96,4,128]{3,1,2,0:T(8,128)(2,1)}, u32[]{:S(2)}, u32[]{:S(2)}) collective-permute-start(bf16[2,96,4,128]{3,1,2,0:T(8,128)(2,1)} %maximum_maximum_fusion.1), channel_id=1, source_target_pairs={{0,2},{2,0},{4,6},{6,4},{8,10},{10,8},{12,14},{14,12},{16,18},{18,... | collective-permute-start | bytes 589832 | tf_op jit(solution)/shard_map/ppermute | solution.py:12
  26.1 0.8 copy-start.4
  26.1 1.6 copy-start.6
  27.7 44.4 %collective-permute-start = (bf16[2,128,4,128]{3,1,2,0:T(8,128)(2,1)}, bf16[2,128,4,128]{3,1,2,0:T(8,128)(2,1)}, u32[]{:S(2)}, u32[]{:S(2)}) collective-permute-start(bf16[2,128,4,128]{3,1,2,0:T(8,128)(2,1)} %get-tuple-element.36), channel_id=1, source_target_pairs={{0,2},{2,4},{4,6},{6,8},{8,10},{10,12},{12,14},{14,16},{16,18},{18... | collective-permute-start | bytes 786440 | tf_op jit(solution)/shard_map/ppermute | solution.py:22
  30.5 52.1 %collective-permute-start.1 = (bf16[2,128,4,128]{3,1,2,0:T(8,128)(2,1)}, bf16[2,128,4,128]{3,1,2,0:T(8,128)(2,1)}, u32[]{:S(2)}, u32[]{:S(2)}) collective-permute-start(bf16[2,128,4,128]{3,1,2,0:T(8,128)(2,1)} %get-tuple-element.37), channel_id=1, source_target_pairs={{2,0},{4,2},{6,4},{8,6},{10,8},{12,10},{14,12},{16,14},{18,16},{20... | collective-permute-start | bytes 786440 | tf_op jit(solution)/shard_map/ppermute | solution.py:23
  33.0 1.8 copy-start.3
  33.6 3.4 %copy-start.9 = (bf16[1,256,4,128]{3,2,1,0:T(4,128)(2,1)}, bf16[1,256,4,128]{3,2,1,0:T(4,128)(2,1)S(1)}, u32[]{:S(2)}) copy-start(bf16[1,256,4,128]{3,2,1,0:T(4,128)(2,1)S(1)} %fusion.41) | copy-start | bytes 786436
  40.6 43.5 %copy-start.5 = (bf16[1,512,4,128]{3,1,2,0:T(8,128)(2,1)S(1)}, bf16[1,512,4,128]{3,1,2,0:T(8,128)(2,1)}, u32[]{:S(2)}) copy-start(bf16[1,512,4,128]{3,1,2,0:T(8,128)(2,1)} %copy-done.4) | copy-start | bytes 1572868
  54.1 30.0 %copy-start.7 = (bf16[1,512,4,128]{3,1,2,0:T(8,128)(2,1)S(1)}, bf16[1,512,4,128]{3,1,2,0:T(8,128)(2,1)}, u32[]{:S(2)}) copy-start(bf16[1,512,4,128]{3,1,2,0:T(8,128)(2,1)} %copy-done.6) | copy-start | bytes 1572868
  62.3 69.7 %collective-permute-start.2 = (bf16[2,256,4,128]{3,2,1,0:T(4,128)(2,1)}, bf16[2,256,4,128]{3,2,1,0:T(4,128)(2,1)S(1)}, u32[]{:S(2)}, u32[]{:S(2)}) collective-permute-start(bf16[2,256,4,128]{3,2,1,0:T(4,128)(2,1)} %pad_maximum_fusion.7), channel_id=1, source_target_pairs={{0,2},{2,4},{4,6},{6,8},{8,10},{10,12},{12,14},{14,16},{16,18},{18... | collective-permute-start | bytes 1572872 | tf_op jit(solution)/shard_map/ppermute | solution.py:22
  69.9 64.1 %collective-permute-start.3 = (bf16[2,256,4,128]{3,2,1,0:T(4,128)(2,1)}, bf16[2,256,4,128]{3,2,1,0:T(4,128)(2,1)S(1)}, u32[]{:S(2)}, u32[]{:S(2)}) collective-permute-start(bf16[2,256,4,128]{3,2,1,0:T(4,128)(2,1)} %pad_maximum_fusion.7), channel_id=1, source_target_pairs={{2,0},{4,2},{6,4},{8,6},{10,8},{12,10},{14,12},{16,14},{18,16},{20... | collective-permute-start | bytes 1572872 | tf_op jit(solution)/shard_map/ppermute | solution.py:23
  72.1 42.0 %collective-permute-start.8 = (bf16[2,128,4,128]{3,1,2,0:T(8,128)(2,1)S(1)}, bf16[2,128,4,128]{3,1,2,0:T(8,128)(2,1)S(1)}, u32[]{:S(2)}, u32[]{:S(2)}) collective-permute-start(bf16[2,128,4,128]{3,1,2,0:T(8,128)(2,1)S(1)} %pad_maximum_fusion.11), channel_id=1, source_target_pairs={{0,8},{2,10},{4,12},{6,14},{8,16},{10,18},{12,20},{14,22},{16,24},... | collective-permute-start | bytes 786440 | tf_op jit(solution)/shard_map/ppermute | solution.py:31
  82.6 47.3 %collective-permute-start.9 = (bf16[2,128,4,128]{3,1,2,0:T(8,128)(2,1)S(1)}, bf16[2,128,4,128]{3,1,2,0:T(8,128)(2,1)S(1)}, u32[]{:S(2)}, u32[]{:S(2)}) collective-permute-start(bf16[2,128,4,128]{3,1,2,0:T(8,128)(2,1)S(1)} %pad_maximum_fusion.11), channel_id=1, source_target_pairs={{8,0},{10,2},{12,4},{14,6},{16,8},{18,10},{20,12},{22,14},{24,16},... | collective-permute-start | bytes 786440 | tf_op jit(solution)/shard_map/ppermute | solution.py:31
  86.4 0.7 copy-start.37
  87.9 1.6 copy-start.30
  90.9 22.5 %copy-start.20 = (bf16[32,4,128]{2,0,1:T(8,128)(2,1)S(1)}, bf16[32,4,128]{2,0,1:T(8,128)(2,1)}, u32[]{:S(2)}) copy-start(bf16[32,4,128]{2,0,1:T(8,128)(2,1)} %copy-done.19) | copy-start | bytes 98308
  90.9 22.5 %copy-start.22 = (bf16[1,32,4,128]{3,1,2,0:T(8,128)(2,1)S(1)}, bf16[1,32,4,128]{3,1,2,0:T(8,128)(2,1)}, u32[]{:S(2)}) copy-start(bf16[1,32,4,128]{3,1,2,0:T(8,128)(2,1)} %copy-done.21) | copy-start | bytes 98308
  90.9 20.5 %collective-permute-start.11 = (bf16[2,64,4,128]{3,1,2,0:T(8,128)(2,1)S(1)}, bf16[2,64,4,128]{3,1,2,0:T(8,128)(2,1)S(1)}, u32[]{:S(2)}, u32[]{:S(2)}) collective-permute-start(bf16[2,64,4,128]{3,1,2,0:T(8,128)(2,1)S(1)} %pad_maximum_fusion.13), channel_id=1, source_target_pairs={{0,4},{2,6},{4,0},{6,2},{8,12},{10,14},{12,8},{14,10},{16,20},{18,... | collective-permute-start | bytes 393224 | tf_op jit(solution)/shard_map/ppermute | solution.py:12
  95.2 38.8 %copy-start.10 = (bf16[1,256,4,128]{3,2,1,0:T(4,128)(2,1)S(1)}, bf16[1,256,4,128]{3,2,1,0:T(4,128)(2,1)}, u32[]{:S(2)}) copy-start(bf16[1,256,4,128]{3,2,1,0:T(4,128)(2,1)} %copy-done.9) | copy-start | bytes 786436
  111.5 29.5 %collective-permute-start.6 = (bf16[2,128,4,128]{3,1,2,0:T(8,128)(2,1)S(1)}, bf16[2,128,4,128]{3,1,2,0:T(8,128)(2,1)S(1)}, u32[]{:S(2)}, u32[]{:S(2)}) collective-permute-start(bf16[2,128,4,128]{3,1,2,0:T(8,128)(2,1)S(1)} %get-tuple-element.42), channel_id=1, source_target_pairs={{0,2},{2,0},{4,6},{6,4},{8,10},{10,8},{12,14},{14,12},{16,18},{18,... | collective-permute-start | bytes 786440 | tf_op jit(solution)/shard_map/ppermute | solution.py:12
  114.1 47.3 %collective-permute-start.12 = (bf16[2,128,4,128]{3,1,2,0:T(8,128)(2,1)}, bf16[2,128,4,128]{3,1,2,0:T(8,128)(2,1)}, u32[]{:S(2)}, u32[]{:S(2)}) collective-permute-start(bf16[2,128,4,128]{3,1,2,0:T(8,128)(2,1)} %pad_maximum_fusion.12), channel_id=1, source_target_pairs={{0,16},{2,18},{4,20},{6,22},{8,24},{10,26},{12,28},{14,30},{16,32}... | collective-permute-start | bytes 786440 | tf_op jit(solution)/shard_map/ppermute | solution.py:31
  129.9 32.6 %collective-permute-start.13 = (bf16[2,128,4,128]{3,1,2,0:T(8,128)(2,1)}, bf16[2,128,4,128]{3,1,2,0:T(8,128)(2,1)}, u32[]{:S(2)}, u32[]{:S(2)}) collective-permute-start(bf16[2,128,4,128]{3,1,2,0:T(8,128)(2,1)} %pad_maximum_fusion.12), channel_id=1, source_target_pairs={{16,0},{18,2},{20,4},{22,6},{24,8},{26,10},{28,12},{30,14},{32,16}... | collective-permute-start | bytes 786440 | tf_op jit(solution)/shard_map/ppermute | solution.py:31
  132.0 8.9 %copy-start.11 = (bf16[2,384,4,128]{3,1,2,0:T(8,128)(2,1)}, bf16[2,384,4,128]{3,1,2,0:T(8,128)(2,1)S(1)}, u32[]{:S(2)}) copy-start(bf16[2,384,4,128]{3,1,2,0:T(8,128)(2,1)S(1)} %get-tuple-element.39) | copy-start | bytes 2359300
  132.0 37.7 %collective-permute-start.10 = (bf16[2,128,4,128]{3,1,2,0:T(8,128)(2,1)}, bf16[2,128,4,128]{3,1,2,0:T(8,128)(2,1)}, u32[]{:S(2)}, u32[]{:S(2)}) collective-permute-start(bf16[2,128,4,128]{3,1,2,0:T(8,128)(2,1)} %get-tuple-element.38), channel_id=1, source_target_pairs={{0,4},{2,6},{4,0},{6,2},{8,12},{10,14},{12,8},{14,10},{16,20},{18,... | collective-permute-start | bytes 786440 | tf_op jit(solution)/shard_map/ppermute | solution.py:12
  140.7 1.0 copy-start.17
  141.7 0.9 copy-start.15
  142.1 6.3 %copy-start.28 = (f32[4,128]{1,0:T(4,128)}, f32[4,128]{1,0:T(4,128)S(1)}, u32[]{:S(2)}) copy-start(f32[4,128]{1,0:T(4,128)S(1)} %get-tuple-element.46) | copy-start | bytes 6148
  142.7 1.0 copy-start.24
  142.7 1.0 copy-start.45
  144.2 1.6 copy-start.27
  161.4 8.3 %copy-start.12 = (bf16[2,384,4,128]{3,1,2,0:T(8,128)(2,1)S(1)}, bf16[2,384,4,128]{3,1,2,0:T(8,128)(2,1)}, u32[]{:S(2)}) copy-start(bf16[2,384,4,128]{3,1,2,0:T(8,128)(2,1)} %copy-done.11) | copy-start | bytes 2359300
  161.4 10.2 %copy-start.18 = (f32[64,4,128]{2,1,0:T(4,128)S(1)}, f32[64,4,128]{2,1,0:T(4,128)}, u32[]{:S(2)}) copy-start(f32[64,4,128]{2,1,0:T(4,128)} %bitcast_reduce_fusion.18) | copy-start | bytes 393220
  161.4 10.2 %copy-start.41 = (pred[384]{0:T(512)(128)(4,1)S(1)}, pred[384]{0:T(512)(128)(4,1)}, u32[]{:S(2)}) copy-start(pred[384]{0:T(512)(128)(4,1)} %fusion.108) | copy-start | bytes 1156
  164.4 5.3 %copy-start.14 = (bf16[2,384,4,128]{3,1,2,0:T(8,128)(2,1)}, bf16[2,384,4,128]{3,1,2,0:T(8,128)(2,1)S(1)}, u32[]{:S(2)}) copy-start(bf16[2,384,4,128]{3,1,2,0:T(8,128)(2,1)S(1)} %get-tuple-element.41) | copy-start | bytes 2359300
  164.4 22.7 %collective-permute-start.14 = (bf16[2,128,4,128]{3,1,2,0:T(8,128)(2,1)}, bf16[2,128,4,128]{3,1,2,0:T(8,128)(2,1)}, u32[]{:S(2)}, u32[]{:S(2)}) collective-permute-start(bf16[2,128,4,128]{3,1,2,0:T(8,128)(2,1)} %get-tuple-element.40), channel_id=1, source_target_pairs={{0,8},{2,10},{4,12},{6,14},{8,0},{10,2},{12,4},{14,6},{16,24},{18,... | collective-permute-start | bytes 786440 | tf_op jit(solution)/shard_map/ppermute | solution.py:12
  170.7 0.9 copy-start.13
  171.6 17.2 %copy-start.25 = (f32[32,4,128]{2,1,0:T(4,128)S(1)}, f32[32,4,128]{2,1,0:T(4,128)}, u32[]{:S(2)}) copy-start(f32[32,4,128]{2,1,0:T(4,128)} %bitcast_reduce_fusion.13) | copy-start | bytes 196612
  171.6 17.2 %copy-start.44 = (pred[384]{0:T(512)(128)(4,1)S(1)}, pred[384]{0:T(512)(128)(4,1)}, u32[]{:S(2)}) copy-start(pred[384]{0:T(512)(128)(4,1)} %fusion.107) | copy-start | bytes 1156
  209.1 0.7 copy-start.40
  210.1 0.9 copy-start.33
  213.5 0.7 copy-start.29
  213.5 0.7 copy-start.43
  214.5 0.9 copy-start.34
  217.8 0.7 copy-start.42
  217.8 0.7 copy-start.47
  218.8 2.8 %copy-start.36 = (f32[4,2]{1,0:T(4,128)}, f32[4,2]{1,0:T(4,128)S(1)}, u32[]{:S(2)}) copy-start(f32[4,2]{1,0:T(4,128)S(1)} %get-tuple-element.52) | copy-start | bytes 100
  222.0 0.7 copy-start.39
  222.0 0.7 copy-start.46
  222.6 6.1 %copy-start.31 = (f32[4,4,128]{2,1,0:T(4,128)S(1)}, f32[4,4,128]{2,1,0:T(4,128)}, u32[]{:S(2)}) copy-start(f32[4,4,128]{2,1,0:T(4,128)} %copy-done.30) | copy-start | bytes 24580
  222.6 6.1 %copy-start.32 = (f32[4,4,128]{2,1,0:T(4,128)S(1)}, f32[4,4,128]{2,1,0:T(4,128)}, u32[]{:S(2)}) copy-start(f32[4,4,128]{2,1,0:T(4,128)} %fusion.1) | copy-start | bytes 24580
  222.6 7.0 %copy-start.16 = (f32[128,4,128]{2,0,1:T(8,128)S(1)}, f32[128,4,128]{2,0,1:T(8,128)}, u32[]{:S(2)}) copy-start(f32[128,4,128]{2,0,1:T(8,128)} %copy.462) | copy-start | bytes 786436
  228.7 1.5 copy-start.8
  228.7 1.5 copy-start.23
  228.7 1.5 copy-start.26
  228.7 1.5 copy-start.35
  228.7 1.5 copy-start.38
Sparse Core Ops, SparseCore 0:
  12.7 194.7 all-gather.2
